TPU v7x, 1024 devices: a whole 4x4x32 slice. The times are simulated.
1024 devices in a mesh: pair: 64 (over z, core), narrow: 16 (over y, x).
Axes of the slice: x: 4, y: 4, z: 32, core: 2. Of those that a mesh axis runs over, the one named last changes fastest.
Arguments:
- trial_slab: bfloat16 [8, 2048, 10240], P(None, 'pair', 'narrow'), may hold values from -6 to 6
- ladder: bfloat16 [65536, 10240], P('pair', 'narrow'), may hold values from -0.0625 to 0.0625
- range_irreps: int32 [64], replicated, may hold values from 0 to 7, as said below
Outputs:
- sigma: bfloat16 [2048, 65536], P(('pair', 'narrow'))
Inputs may be any that keep to these rules, and one draw needn't show every extreme that they name: `range_irreps`: non-decreasing along the pair index; the first entry is 0 and the last is 7.
All inputs are finite; a program needn't handle non-finite values.
Results may differ from a plain program's by a relative error of at most 0.019.
Values may be sent and summed in bfloat16 or wider, within the bound.
No kernel may reach another device: no remote copies, remote signals or barrier semaphores. Data moves between devices by JAX's collectives and lax.ppermute only.
A program may use at most 32 MiB of HBM per device.

v0:
```python
import jax
import jax.numpy as jnp
from jax import lax
from jax.sharding import PartitionSpec as P


def body(trial_slab, ladder, range_irreps):
    pair_count = lax.axis_size("pair")
    narrow_count = lax.axis_size("narrow")
    rows_out = trial_slab.shape[1] // narrow_count
    local_pairs = ladder.shape[0]
    chosen = jnp.take(trial_slab, range_irreps, axis=0)
    arrived = lax.all_to_all(chosen, "pair", split_axis=0, concat_axis=0, tiled=True)
    products = jnp.einsum("pmc,ac->mpa", arrived, ladder, preferred_element_type=jnp.float32)
    summed = lax.psum_scatter(
        products.reshape(-1, local_pairs).astype(jnp.bfloat16),
        "narrow",
        scatter_dimension=0,
        tiled=True,
    )
    rounded = summed.reshape(rows_out, pair_count, local_pairs)
    owned = lax.all_to_all(rounded, "pair", split_axis=1, concat_axis=1, tiled=True)
    return owned.reshape(rows_out, pair_count * local_pairs)


def solution(mesh):
    placed = (P(None, "pair", "narrow"), P("pair", "narrow"), P())
    return jax.shard_map(
        body, mesh=mesh, in_specs=placed, out_specs=P(("pair", "narrow"), None), check_vma=False
    )
```

profile of v0, /device:TPU:1, one launch (start us, length us, event | category | flops | bytes accessed | tf_op | source)
XLA Modules:
  0.0 466.2 jit_solution(17039020693372295729)
XLA Ops:
  6.5 0.0 copy-start
  6.5 0.0 reduce-scatter.2.cloned.1.call-start
  6.5 0.8 compare_and_fusion
  7.3 0.7 compare_select_fusion
  8.0 3.3 gather_fusion
  11.3 2.1 broadcast_select_fusion
  13.4 274.0 %all_to_all.10 = bf16[64,32,640]{2,1,0:T(8,128)(2,1)S(1)} all-to-all(bf16[64,32,640]{2,1,0:T(8,128)(2,1)S(1)} %broadcast_select_fusion), channel_id=1, replica_groups=mesh['pair'=64,'narrow'=16] {'pair'}, dimensions={0} | all-to-all | bytes 5242880 | tf_op jit(solution)/shard_map/all_to_all | solution.py:13
  287.4 0.0 copy-done
  287.4 3.7 convert_bitcast_fusion
  291.2 4.3 copy.5
  295.4 0.0 reduce-scatter.2.cloned.1.call-update
  295.5 95.2 %reduce-scatter.2.cloned.1.call-done = bf16[128,1024]{1,0:T(8,128)(2,1)} async-done(((bf16[2048,1024]{1,0:T(8,128)(2,1)}), bf16[128,1024]{1,0:T(8,128)(2,1)}) %reduce-scatter.2.cloned.1.call-update) | async-done | bytes 262160 | tf_op jit(solution)/shard_map/reduce_scatter | solution.py:15
  390.7 1.2 copy.6
  391.9 66.7 %all_to_all.11 = bf16[2,64,1024]{2,0,1:T(2,128)(2,1)S(1)} all-to-all(bf16[2,64,1024]{2,0,1:T(2,128)(2,1)S(1)} %copy.6), channel_id=1, replica_groups=mesh['pair'=64,'narrow'=16] {'pair'}, dimensions={1} | all-to-all | bytes 524288 | tf_op jit(solution)/shard_map/all_to_all | solution.py:22
  458.6 0.7 copy.8
  (1 shorter events, 0.0 us)
Async XLA Ops:
  6.5 280.9 %copy-start = (bf16[1024,640]{1,0:T(8,128)(2,1)S(1)}, bf16[1024,640]{1,0:T(8,128)(2,1)}, u32[]{:S(2)}) copy-start(bf16[1024,640]{1,0:T(8,128)(2,1)} %param.4) | copy-start | bytes 3932164
  6.5 384.1 %reduce-scatter.2.cloned.1.call-start = ((), (), s32[]{:S(2)}) async-start(), calls=%async_computation.3 | async-start | bytes 4456448 | tf_op jit(solution)/shard_map/reduce_scatter | solution.py:15
Sparse Core Ops, SparseCore 0:
  295.6 95.0 reduce-scatter.1
where the time goes:
time: 467 us; the launch traced here: 466 us
  blocking collectives  341 us (73%)
  waiting for transfers between devices  95.2 us (20%)
  between operations  13.4 us (3%)
  local copies, waits for them, and re-layouts  9.52 us (2%)
    all_to_all x1, blocking collectives, body(): lax.all_to_all(chosen, 'pair', split_axis=0, concat_axis=0, tiled=True)  274 us
    reduce_scatter x1, waiting for transfers between devices, body(): lax.psum_scatter(products.reshape(-1, local_pairs).astype(jnp.bfloat16),...  95.2 us
    all_to_all x1, blocking collectives, body(): lax.all_to_all(rounded, 'pair', split_axis=1, concat_axis=1, tiled=True)  66.7 us
  transfers between devices with their start and end apart: 1, of which 1 were waited for; matrix products, arithmetic and copies ran while one was open for 0% of the time, Pallas kernels for 0%

commit v1 on v0

v1 whole, which is shorter than its diff:
```python
import jax
import jax.numpy as jnp
from jax import lax
from jax.sharding import Mesh
from jax.sharding import PartitionSpec as P


def body(trial_slab, ladder, range_irreps):
    chips = lax.axis_size("z")
    cores = lax.axis_size("core")
    narrow_count = lax.axis_size("narrow")
    pair_count = chips * cores
    rows_out = trial_slab.shape[1] // narrow_count
    local_rows = trial_slab.shape[1]
    local_pairs = ladder.shape[0]
    core = lax.axis_index("core")
    me = lax.axis_index("z") * cores + core
    partner = me + 1 - 2 * core
    gathered = lax.all_gather(trial_slab, "z", axis=0, tiled=False)
    mine = jnp.take(gathered, range_irreps[me], axis=1)
    theirs = jnp.take(gathered, range_irreps[partner], axis=1)
    received = lax.ppermute(theirs, "core", [(0, 1), (1, 0)])
    low = jnp.where(core == 0, mine, received)
    high = jnp.where(core == 0, received, mine)
    arrived = jnp.stack([low, high], axis=1).reshape(pair_count, local_rows, -1)
    products = jnp.einsum("pmc,ac->mpa", arrived, ladder, preferred_element_type=jnp.float32)
    summed = lax.psum_scatter(
        products.reshape(-1, local_pairs).astype(jnp.bfloat16),
        "narrow",
        scatter_dimension=0,
        tiled=True,
    )
    rounded = summed.reshape(rows_out, pair_count, local_pairs)
    owned = lax.all_to_all(rounded, ("z", "core"), split_axis=1, concat_axis=1, tiled=True)
    return owned.reshape(rows_out, pair_count * local_pairs)


def solution(mesh):
    pair_count = mesh.shape["pair"]
    narrow_count = mesh.shape["narrow"]
    split = Mesh(mesh.devices.reshape(pair_count // 2, 2, narrow_count), ("z", "core", "narrow"))
    placed = (P(None, ("z", "core"), "narrow"), P(("z", "core"), "narrow"), P())
    return jax.shard_map(
        body, mesh=split, in_specs=placed, out_specs=P(("z", "core", "narrow"), None), check_vma=False
    )
```

time: 467 us -> 373 us (0.80)
  blocking collectives: 341 us -> 66.7 us
  waiting for transfers between devices: 95.2 us -> 254 us
  starting transfers between devices: 0.01 us -> 18.9 us
    all_to_all x2 -> x1, blocking collectives: 341 us -> 66.7 us  [body(): lax.all_to_all(rounded, ('z', 'core'), split_axis=1, concat_axis=1, tiled...]
    all_gather x0 -> x1, waiting for transfers between devices: none -> 149 us  [body(): gathered = lax.all_gather(trial_slab, 'z', axis=0, tiled=False)]
    ppermute x0 -> x1, starting transfers between devices: none -> 18.9 us  [body(): received = lax.ppermute(theirs, 'core', [(0, 1), (1, 0)])]
    reduce_scatter x1, waiting for transfers between devices: 95.2 us -> 103 us  [body(): lax.psum_scatter(products.reshape(-1, local_pairs).astype(jnp.bfloat16),...]
  transfers between devices with their start and end apart: 1 -> 3, of which waited for: 1 -> 3; matrix products, arithmetic and copies ran while one was open for 0% -> 0% of each run, Pallas kernels for 0% -> 0%
where the time goes in v1:
time: 373 us; the launch traced here: 372 us
  waiting for transfers between devices  254 us (68%)
  blocking collectives  66.7 us (18%)
  starting transfers between devices  18.9 us (5%)
  between operations  17.5 us (5%)
  local copies, waits for them, and re-layouts  7.6 us (2%)
  other arithmetic  3.79 us (1%)
  matrix products  3.77 us (1%)
    all_gather x1, waiting for transfers between devices, body(): gathered = lax.all_gather(trial_slab, 'z', axis=0, tiled=False)  149 us
    reduce_scatter x1, waiting for transfers between devices, body(): lax.psum_scatter(products.reshape(-1, local_pairs).astype(jnp.bfloat16),...  103 us
    all_to_all x1, blocking collectives, body(): lax.all_to_all(rounded, ('z', 'core'), split_axis=1, concat_axis=1, tiled...  66.7 us
    ppermute x1, starting transfers between devices, body(): received = lax.ppermute(theirs, 'core', [(0, 1), (1, 0)])  18.9 us
  transfers between devices with their start and end apart: 3, of which 3 were waited for; matrix products, arithmetic and copies ran while one was open for 0% of the time, Pallas kernels for 0%

profile of v1, /device:TPU:1, one launch (start us, length us, event | category | flops | bytes accessed | tf_op | source)
XLA Modules:
  0.0 371.9 jit_solution(6466264539903310651)
XLA Ops:
  6.5 0.0 copy-start
  6.5 0.0 all-gather.3.cloned.1.call-start
  6.5 0.7 all-gather.3.cloned.1.call-update
  7.3 0.0 reduce-scatter.2.cloned.1.call-start
  7.3 1.4 fusion.3
  10.8 148.9 %all-gather.3.cloned.1.call-done = bf16[256,32,640]{2,1,0:T(8,128)(2,1)} async-done(((bf16[8,32,640]{2,1,0:T(8,128)(2,1)}), bf16[256,32,640]{2,1,0:T(8,128)(2,1)}) %all-gather.3.cloned.1.call-update) | async-done | bytes 10485776 | tf_op jit(solution)/shard_map/all_gather | solution.py:19
  159.7 1.5 fusion
  161.2 18.9 %collective-permute-start = (bf16[32,32,640]{2,1,0:T(8,128)(2,1)S(1)}, bf16[32,32,640]{2,1,0:T(8,128)(2,1)}, u32[]{:S(2)}, u32[]{:S(2)}) collective-permute-start(bf16[32,32,640]{2,1,0:T(8,128)(2,1)S(1)} %fusion), channel_id=1, source_target_pairs={{0,16},{16,0},{1,17},{17,1},{2,18},{18,2},{3,19},{19,3},{4,20},{20... | collective-permute-start | bytes 3932168 | tf_op jit(solution)/shard_map/ppermute | solution.py:22
  182.0 0.8 collective-permute-done
  182.8 2.1 select_bitcast_fusion.1
  184.9 0.3 pad_maximum_fusion
  185.2 0.0 copy-done
  185.2 3.8 %convert_bitcast_fusion = bf16[32,64,1024]{2,0,1:T(8,128)(2,1)S(1)} fusion(bf16[64,32,640]{2,1,0:T(8,128)(2,1)S(1)} %bitcast.40, bf16[1024,640]{1,0:T(8,128)(2,1)S(1)} %copy-done), kind=kOutput, calls=%fused_computation | convolution fusion | flops 2686451712 | bytes 8126464 | tf_op jit(solution)/shard_map/pmc,ac->mpa/dot_general | solution.py:26
  189.0 4.3 %copy.14 = bf16[32,64,1024]{2,1,0:T(8,128)(2,1)} copy(bf16[32,64,1024]{2,0,1:T(8,128)(2,1)S(1)} %convert_bitcast_fusion) | data formatting | bytes 8388608 | tf_op jit(solution)/shard_map/convert_element_type | solution.py:28
  193.2 0.0 reduce-scatter.2.cloned.1.call-update
  193.2 103.2 %reduce-scatter.2.cloned.1.call-done = bf16[128,1024]{1,0:T(8,128)(2,1)} async-done(((bf16[2048,1024]{1,0:T(8,128)(2,1)}), bf16[128,1024]{1,0:T(8,128)(2,1)}) %reduce-scatter.2.cloned.1.call-update) | async-done | bytes 262160 | tf_op jit(solution)/shard_map/reduce_scatter | solution.py:27
  296.4 1.2 copy.15
  297.7 66.7 %all_to_all.5 = bf16[2,64,1024]{2,0,1:T(2,128)(2,1)S(1)} all-to-all(bf16[2,64,1024]{2,0,1:T(2,128)(2,1)S(1)} %copy.15), channel_id=1, replica_groups=mesh['z'=32,'core'=2,'narrow'=16] {'z','core'}, dimensions={1} | all-to-all | bytes 524288 | tf_op jit(solution)/shard_map/all_to_all | solution.py:34
  364.4 0.7 copy.19
Async XLA Ops:
  6.5 178.6 %copy-start = (bf16[1024,640]{1,0:T(8,128)(2,1)S(1)}, bf16[1024,640]{1,0:T(8,128)(2,1)}, u32[]{:S(2)}) copy-start(bf16[1024,640]{1,0:T(8,128)(2,1)} %param.6) | copy-start | bytes 3932164
  6.5 153.2 %all-gather.3.cloned.1.call-start = ((), (), s32[]{:S(2)}) async-start(), calls=%async_computation.3 | async-start | bytes 10813440 | tf_op jit(solution)/shard_map/all_gather | solution.py:19
  7.3 289.2 %reduce-scatter.2.cloned.1.call-start = ((), (), s32[]{:S(2)}) async-start(), calls=%async_computation.2 | async-start | bytes 4456448 | tf_op jit(solution)/shard_map/reduce_scatter | solution.py:27
  161.2 21.6 %collective-permute-start = (bf16[32,32,640]{2,1,0:T(8,128)(2,1)S(1)}, bf16[32,32,640]{2,1,0:T(8,128)(2,1)}, u32[]{:S(2)}, u32[]{:S(2)}) collective-permute-start(bf16[32,32,640]{2,1,0:T(8,128)(2,1)S(1)} %fusion), channel_id=1, source_target_pairs={{0,16},{16,0},{1,17},{17,1},{2,18},{18,2},{3,19},{19,3},{4,20},{20... | collective-permute-start | bytes 3932168 | tf_op jit(solution)/shard_map/ppermute | solution.py:22
Sparse Core Ops, SparseCore 0:
  10.0 149.6 all-gather.2
  193.4 103.0 reduce-scatter.1

commit v2 on v1

v2 whole, which is shorter than its diff:
```python
import jax
import jax.numpy as jnp
from jax import lax
from jax.sharding import Mesh
from jax.sharding import PartitionSpec as P


def body(trial_slab, ladder, range_irreps):
    chips = lax.axis_size("z")
    cores = lax.axis_size("core")
    narrow_count = lax.axis_size("narrow")
    pair_count = chips * cores
    irreps, local_rows, block = trial_slab.shape
    per_owner = local_rows // narrow_count
    local_pairs = ladder.shape[0]
    core = lax.axis_index("core")
    me = lax.axis_index("z") * cores + core
    partner = me + 1 - 2 * core
    slab = trial_slab.reshape(irreps, narrow_count, per_owner, block)
    pieces = []
    for j in range(per_owner):
        gathered = lax.all_gather(slab[:, :, j, :], "z", axis=0, tiled=False)
        mine = jnp.take(gathered, range_irreps[me], axis=1)
        theirs = jnp.take(gathered, range_irreps[partner], axis=1)
        received = lax.ppermute(theirs, "core", [(0, 1), (1, 0)])
        low = jnp.where(core == 0, mine, received)
        high = jnp.where(core == 0, received, mine)
        arrived = jnp.stack([low, high], axis=1).reshape(pair_count, narrow_count, block)
        products = jnp.einsum("poc,ac->opa", arrived, ladder, preferred_element_type=jnp.float32)
        exchanged = lax.all_to_all(
            products.astype(jnp.bfloat16), "narrow", split_axis=0, concat_axis=0, tiled=True
        )
        summed = jnp.sum(exchanged.astype(jnp.float32), axis=0).astype(jnp.bfloat16)
        owned = lax.all_to_all(summed, ("z", "core"), split_axis=0, concat_axis=0, tiled=True)
        pieces.append(owned.reshape(pair_count * local_pairs))
    return jnp.stack(pieces, axis=0)


def solution(mesh):
    pair_count = mesh.shape["pair"]
    narrow_count = mesh.shape["narrow"]
    split = Mesh(mesh.devices.reshape(pair_count // 2, 2, narrow_count), ("z", "core", "narrow"))
    placed = (P(None, ("z", "core"), "narrow"), P(("z", "core"), "narrow"), P())
    return jax.shard_map(
        body, mesh=split, in_specs=placed, out_specs=P(("z", "core", "narrow"), None), check_vma=False
    )
```

time: 373 us -> 450 us (1.21)
  blocking collectives: 66.7 us -> 0 us
  waiting for transfers between devices: 254 us -> 315 us
  starting transfers between devices: 18.9 us -> 78.4 us
  local copies, waits for them, and re-layouts: 7.6 us -> 26.9 us
    reduce_scatter x1 -> x0, waiting for transfers between devices: 103 us -> none  [body(): lax.psum_scatter(products.reshape(-1, local_pairs).astype(jnp.bfloat16),...]
    all_to_all x0 -> x4, waiting for transfers between devices: none -> 88 us  [the longest x2 58.1 us: body(): lax.all_to_all(summed, ('z', 'core'), split_axis=0, concat_axis=0, tiled=...]
    all_gather x1 -> x2, waiting for transfers between devices: 149 us -> 225 us  [body(): gathered = lax.all_gather(slab[:, :, j, :], 'z', axis=0, tiled=False)]
    all_to_all x1 -> x0, blocking collectives: 66.7 us -> none  [body(): lax.all_to_all(rounded, ('z', 'core'), split_axis=1, concat_axis=1, tiled...]
    all_to_all x0 -> x4, starting transfers between devices: none -> 32.1 us  [the longest x2 18.9 us: body(): lax.all_to_all(summed, ('z', 'core'), split_axis=0, concat_axis=0, tiled=...]
    ppermute x1 -> x2, starting transfers between devices: 18.9 us -> 46.2 us  [body(): received = lax.ppermute(theirs, 'core', [(0, 1), (1, 0)])]
    another operation x0 -> x4, local copies, waits for them, and re-layouts: none -> 11.6 us  [the longest x2 11.4 us: body(): mine = jnp.take(gathered, range_irreps[me], axis=1)]
    all_gather x0 -> x1, local copies, waits for them, and re-layouts: none -> 5.5 us  [body(): gathered = lax.all_gather(slab[:, :, j, :], 'z', axis=0, tiled=False)]
  transfers between devices with their start and end apart: 3 -> 8, of which waited for: 3 -> 6; matrix products, arithmetic and copies ran while one was open for 0% -> 8% of each run, Pallas kernels for 0% -> 0%
where the time goes in v2:
time: 450 us
  waiting for transfers between devices  315 us (70%)
  starting transfers between devices  78.4 us (17%)
  local copies, waits for them, and re-layouts  26.9 us (6%)
  between operations  17.5 us (4%)
  other arithmetic  7.79 us (2%)
    all_gather x2, waiting for transfers between devices, body(): gathered = lax.all_gather(slab[:, :, j, :], 'z', axis=0, tiled=False)  225 us
    all_to_all x2, waiting for transfers between devices, body(): lax.all_to_all(summed, ('z', 'core'), split_axis=0, concat_axis=0, tiled=...  58.1 us
    ppermute x2, starting transfers between devices, body(): received = lax.ppermute(theirs, 'core', [(0, 1), (1, 0)])  46.2 us
    all_to_all x2, waiting for transfers between devices, body(): lax.all_to_all(products.astype(jnp.bfloat16), 'narrow', split_axis=0, con...  29.9 us
    all_to_all x2, starting transfers between devices, body(): lax.all_to_all(summed, ('z', 'core'), split_axis=0, concat_axis=0, tiled=...  18.9 us
    all_to_all x2, starting transfers between devices, body(): lax.all_to_all(products.astype(jnp.bfloat16), 'narrow', split_axis=0, con...  13.2 us
    another operation x2, local copies, waits for them, and re-layouts, body(): mine = jnp.take(gathered, range_irreps[me], axis=1)  11.4 us
  transfers between devices with their start and end apart: 8, of which 6 were waited for; matrix products, arithmetic and copies ran while one was open for 8% of the time, Pallas kernels for 0%

profile of v2, /device:TPU:1, one launch (start us, length us, event | category | flops | bytes accessed | tf_op | source)
XLA Modules:
  0.0 449.7 jit_solution(7717655818630713100)
XLA Ops:
  6.5 0.0 copy-start
  6.5 0.0 all-gather.5.cloned.1.call-start
  6.5 1.2 copy.29
  7.7 0.7 fusion.5
  8.5 0.0 all-gather.5.cloned.1.call-update
  8.5 0.0 all-gather.7.cloned.1.call-start
  8.6 0.7 all-gather.7.cloned.1.call-update
  9.3 0.0 copy-done.1
  9.3 0.7 fusion.6
  11.8 132.5 %all-gather.5.cloned.1.call-done = bf16[256,16,1,640]{3,0,2,1:T(8,128)(2,1)} async-done(((bf16[8,16,1,640]{3,0,2,1:T(8,128)(2,1)}), bf16[256,16,1,640]{3,0,2,1:T(8,128)(2,1)}) %all-gather.5.cloned.1.call-update) | async-done | bytes 5242896 | tf_op jit(solution)/shard_map/all_gather | solution.py:22
  144.3 5.5 %copy.30 = bf16[256,16,1,640]{3,1,0,2:T(8,128)(2,1)S(1)} copy(bf16[256,16,1,640]{3,0,2,1:T(8,128)(2,1)} %all-gather.5.cloned.1.call-done) | data formatting | bytes 10485760 | tf_op jit(solution)/shard_map/all_gather | solution.py:22
  149.8 0.1 select_bitcast_fusion
  149.9 23.1 %collective-permute-start = (bf16[32,16,640]{2,1,0:T(8,128)(2,1)S(1)}, bf16[32,16,640]{2,1,0:T(8,128)(2,1)S(1)}, u32[]{:S(2)}, u32[]{:S(2)}) collective-permute-start(bf16[32,16,640]{2,1,0:T(8,128)(2,1)S(1)} %select_bitcast_fusion), channel_id=1, source_target_pairs={{0,16},{16,0},{1,17},{17,1},{2,18},{18,2},{3,19},{19,3},{4,20},{20... | collective-permute-start | bytes 1966088 | tf_op jit(solution)/shard_map/ppermute | solution.py:25
  175.1 4.0 constant_dynamic-slice_fusion.2
  179.1 0.0 collective-permute-done
  179.1 0.8 select_bitcast_fusion.4
  179.9 0.1 pad_maximum_fusion
  180.1 0.1 copy.32
  180.2 1.8 convert_bitcast_fusion.1
  182.1 2.5 copy.33
  184.6 6.6 %all-to-all-start = ((bf16[16,64,1024]{2,1,0:T(8,128)(2,1)}), bf16[16,64,1024]{2,1,0:T(8,128)(2,1)S(1)}, u32[]{:S(2)}, u32[]{:S(2)}) async-start(bf16[16,64,1024]{2,1,0:T(8,128)(2,1)} %copy.33), calls=%async_computation | async-start | bytes 4194304 | tf_op jit(solution)/shard_map/all_to_all | solution.py:30
  191.1 92.6 %all-gather.7.cloned.1.call-done = bf16[256,16,1,640]{3,0,2,1:T(8,128)(2,1)} async-done(((bf16[8,16,1,640]{3,0,2,1:T(8,128)(2,1)}), bf16[256,16,1,640]{3,0,2,1:T(8,128)(2,1)}) %all-gather.7.cloned.1.call-update) | async-done | bytes 5242896 | tf_op jit(solution)/shard_map/all_gather | solution.py:22
  283.7 7.3 %constant_dynamic-slice_fusion = (bf16[32,1,16,640]{3,1,0,2:T(2,128)(2,1)S(1)}, bf16[32,1,16,640]{3,1,0,2:T(2,128)(2,1)S(1)}) fusion(bf16[32,8,16,640]{3,1,0,2:T(8,128)(2,1)} %bitcast.54, s32[]{:T(128)S(6)} %select_n.56, s32[]{:T(128)S(6)} %select_n.58), kind=kLoop, calls=%fused_computation.18 | loop fusion | bytes 2621448 | tf_op jit(solution)/shard_map/jit(_take) | solution.py:23
  291.0 0.8 fusion.2
  291.8 23.1 %collective-permute-start.1 = (bf16[32,16,640]{2,1,0:T(8,128)(2,1)S(1)}, bf16[32,16,640]{2,1,0:T(8,128)(2,1)S(1)}, u32[]{:S(2)}, u32[]{:S(2)}) collective-permute-start(bf16[32,16,640]{2,1,0:T(8,128)(2,1)S(1)} %fusion.2), channel_id=1, source_target_pairs={{0,16},{16,0},{1,17},{17,1},{2,18},{18,2},{3,19},{19,3},{4,20},{20... | collective-permute-start | bytes 1966088 | tf_op jit(solution)/shard_map/ppermute | solution.py:25
  314.9 1.7 collective-permute-done.1
  316.6 0.8 select_bitcast_fusion.2
  317.4 0.1 pad_maximum_fusion.1
  317.6 0.1 copy.38
  317.7 1.8 convert_bitcast_fusion
  319.5 2.5 copy.39
  322.0 0.0 all-to-all-done
  322.0 6.7 %all-to-all-start.2 = ((bf16[16,64,1024]{2,1,0:T(8,128)(2,1)}), bf16[16,64,1024]{2,1,0:T(8,128)(2,1)}, u32[]{:S(2)}, u32[]{:S(2)}) async-start(bf16[16,64,1024]{2,1,0:T(8,128)(2,1)} %copy.39), calls=%async_computation.2 | async-start | bytes 4194304 | tf_op jit(solution)/shard_map/all_to_all | solution.py:30
  328.7 0.4 reduce_sum.24
  329.1 0.5 broadcast.81
  329.6 0.7 reduce.3
  330.3 0.7 reshape.121
  331.0 29.9 %all-to-all-done.2 = bf16[16,64,1024]{2,1,0:T(8,128)(2,1)} async-done(((bf16[16,64,1024]{2,1,0:T(8,128)(2,1)}), bf16[16,64,1024]{2,1,0:T(8,128)(2,1)}, u32[]{:S(2)}, u32[]{:S(2)}) %all-to-all-start.2) | async-done | bytes 2097184 | tf_op jit(solution)/shard_map/all_to_all | solution.py:30
  360.9 13.4 %all-to-all-start.1 = ((bf16[64,2,512]{2,1,0:T(2,128)(2,1)}), bf16[64,2,512]{2,1,0:T(2,128)(2,1)S(1)}, u32[]{:S(2)}, u32[]{:S(2)}) async-start(bf16[64,2,512]{2,1,0:T(2,128)(2,1)} %reshape.121), calls=%async_computation.1 | async-start | bytes 262144 | tf_op jit(solution)/shard_map/all_to_all | solution.py:34
  374.3 2.0 reduce_sum.25
  376.3 0.7 reduce.2
  377.0 0.7 reshape.119
  377.7 27.3 %all-to-all-done.1 = bf16[64,2,512]{2,1,0:T(2,128)(2,1)S(1)} async-done(((bf16[64,2,512]{2,1,0:T(2,128)(2,1)}), bf16[64,2,512]{2,1,0:T(2,128)(2,1)S(1)}, u32[]{:S(2)}, u32[]{:S(2)}) %all-to-all-start.1) | async-done | bytes 131104 | tf_op jit(solution)/shard_map/all_to_all | solution.py:34
  405.0 5.4 %all-to-all-start.3 = ((bf16[64,2,512]{2,1,0:T(2,128)(2,1)}), bf16[64,2,512]{2,1,0:T(2,128)(2,1)S(1)}, u32[]{:S(2)}, u32[]{:S(2)}) async-start(bf16[64,2,512]{2,1,0:T(2,128)(2,1)} %reshape.119), calls=%async_computation.3 | async-start | bytes 262144 | tf_op jit(solution)/shard_map/all_to_all | solution.py:34
  410.4 0.1 reshape.122
  410.6 30.9 %all-to-all-done.3 = bf16[64,2,512]{2,1,0:T(2,128)(2,1)S(1)} async-done(((bf16[64,2,512]{2,1,0:T(2,128)(2,1)}), bf16[64,2,512]{2,1,0:T(2,128)(2,1)S(1)}, u32[]{:S(2)}, u32[]{:S(2)}) %all-to-all-start.3) | async-done | bytes 131104 | tf_op jit(solution)/shard_map/all_to_all | solution.py:34
  441.4 0.1 reshape.120
  441.5 1.3 pad_maximum_fusion.2
  (2 shorter events, 0.0 us)
Async XLA Ops:
  6.5 173.7 %copy-start = (bf16[1024,640]{1,0:T(8,128)(2,1)S(1)}, bf16[1024,640]{1,0:T(8,128)(2,1)}, u32[]{:S(2)}) copy-start(bf16[1024,640]{1,0:T(8,128)(2,1)} %param.6) | copy-start | bytes 3932164
  6.5 2.7 copy-start.1
  6.5 137.7 %all-gather.5.cloned.1.call-start = ((), (), s32[]{:S(2)}) async-start(), calls=%async_computation.4 | async-start | bytes 5406720 | tf_op jit(solution)/shard_map/all_gather | solution.py:22
  8.5 275.2 %all-gather.7.cloned.1.call-start = ((), (), s32[]{:S(2)}) async-start(), calls=%async_computation.5 | async-start | bytes 5406720 | tf_op jit(solution)/shard_map/all_gather | solution.py:22
  149.9 29.2 %collective-permute-start = (bf16[32,16,640]{2,1,0:T(8,128)(2,1)S(1)}, bf16[32,16,640]{2,1,0:T(8,128)(2,1)S(1)}, u32[]{:S(2)}, u32[]{:S(2)}) collective-permute-start(bf16[32,16,640]{2,1,0:T(8,128)(2,1)S(1)} %select_bitcast_fusion), channel_id=1, source_target_pairs={{0,16},{16,0},{1,17},{17,1},{2,18},{18,2},{3,19},{19,3},{4,20},{20... | collective-permute-start | bytes 1966088 | tf_op jit(solution)/shard_map/ppermute | solution.py:25
  184.6 137.5 %all-to-all-start = ((bf16[16,64,1024]{2,1,0:T(8,128)(2,1)}), bf16[16,64,1024]{2,1,0:T(8,128)(2,1)S(1)}, u32[]{:S(2)}, u32[]{:S(2)}) async-start(bf16[16,64,1024]{2,1,0:T(8,128)(2,1)} %copy.33), calls=%async_computation | async-start | bytes 4194304 | tf_op jit(solution)/shard_map/all_to_all | solution.py:30
  291.8 24.8 %collective-permute-start.1 = (bf16[32,16,640]{2,1,0:T(8,128)(2,1)S(1)}, bf16[32,16,640]{2,1,0:T(8,128)(2,1)S(1)}, u32[]{:S(2)}, u32[]{:S(2)}) collective-permute-start(bf16[32,16,640]{2,1,0:T(8,128)(2,1)S(1)} %fusion.2), channel_id=1, source_target_pairs={{0,16},{16,0},{1,17},{17,1},{2,18},{18,2},{3,19},{19,3},{4,20},{20... | collective-permute-start | bytes 1966088 | tf_op jit(solution)/shard_map/ppermute | solution.py:25
  322.0 38.9 %all-to-all-start.2 = ((bf16[16,64,1024]{2,1,0:T(8,128)(2,1)}), bf16[16,64,1024]{2,1,0:T(8,128)(2,1)}, u32[]{:S(2)}, u32[]{:S(2)}) async-start(bf16[16,64,1024]{2,1,0:T(8,128)(2,1)} %copy.39), calls=%async_computation.2 | async-start | bytes 4194304 | tf_op jit(solution)/shard_map/all_to_all | solution.py:30
  360.9 44.1 %all-to-all-start.1 = ((bf16[64,2,512]{2,1,0:T(2,128)(2,1)}), bf16[64,2,512]{2,1,0:T(2,128)(2,1)S(1)}, u32[]{:S(2)}, u32[]{:S(2)}) async-start(bf16[64,2,512]{2,1,0:T(2,128)(2,1)} %reshape.121), calls=%async_computation.1 | async-start | bytes 262144 | tf_op jit(solution)/shard_map/all_to_all | solution.py:34
  405.0 36.4 %all-to-all-start.3 = ((bf16[64,2,512]{2,1,0:T(2,128)(2,1)}), bf16[64,2,512]{2,1,0:T(2,128)(2,1)S(1)}, u32[]{:S(2)}, u32[]{:S(2)}) async-start(bf16[64,2,512]{2,1,0:T(2,128)(2,1)} %reshape.119), calls=%async_computation.3 | async-start | bytes 262144 | tf_op jit(solution)/shard_map/all_to_all | solution.py:34
Sparse Core Ops, SparseCore 0:
  10.0 134.2 all-gather.4
  146.9 136.6 all-gather.6

commit v3 on v2

--- a/solution.py
+++ b/solution.py
@@ -16,17 +16,18 @@
     core = lax.axis_index("core")
     me = lax.axis_index("z") * cores + core
     partner = me + 1 - 2 * core
-    slab = trial_slab.reshape(irreps, narrow_count, per_owner, block)
+    gathered = lax.all_gather(trial_slab, "z", axis=0, tiled=False)
+    mine = jnp.take(gathered, range_irreps[me], axis=1)
+    theirs = jnp.take(gathered, range_irreps[partner], axis=1)
+    received = lax.ppermute(theirs, "core", [(0, 1), (1, 0)])
+    low = jnp.where(core == 0, mine, received)
+    high = jnp.where(core == 0, received, mine)
+    arrived = jnp.stack([low, high], axis=1).reshape(pair_count, narrow_count, per_owner, block)
     pieces = []
     for j in range(per_owner):
-        gathered = lax.all_gather(slab[:, :, j, :], "z", axis=0, tiled=False)
-        mine = jnp.take(gathered, range_irreps[me], axis=1)
-        theirs = jnp.take(gathered, range_irreps[partner], axis=1)
-        received = lax.ppermute(theirs, "core", [(0, 1), (1, 0)])
-        low = jnp.where(core == 0, mine, received)
-        high = jnp.where(core == 0, received, mine)
-        arrived = jnp.stack([low, high], axis=1).reshape(pair_count, narrow_count, block)
-        products = jnp.einsum("poc,ac->opa", arrived, ladder, preferred_element_type=jnp.float32)
+        products = jnp.einsum(
+            "poc,ac->opa", arrived[:, :, j, :], ladder, preferred_element_type=jnp.float32
+        )
         exchanged = lax.all_to_all(
             products.astype(jnp.bfloat16), "narrow", split_axis=0, concat_axis=0, tiled=True
         )

time: 450 us -> 370 us (0.82)
  waiting for transfers between devices: 315 us -> 259 us
  starting transfers between devices: 78.4 us -> 49.8 us
  other arithmetic: 7.79 us -> 12.5 us
    all_gather x2 -> x1, waiting for transfers between devices: 225 us -> 149 us  [body(): gathered = lax.all_gather(trial_slab, 'z', axis=0, tiled=False)]
    ppermute x2 -> x1, starting transfers between devices: 46.2 us -> 18.9 us  [body(): received = lax.ppermute(theirs, 'core', [(0, 1), (1, 0)])]
    all_to_all x2, waiting for transfers between devices: 29.9 us -> 49.7 us  [body(): lax.all_to_all(products.astype(jnp.bfloat16), 'narrow', split_axis=0, con...]
    another operation x4 -> x0, local copies, waits for them, and re-layouts: 11.6 us -> none  [the longest x2 11.4 us: body(): mine = jnp.take(gathered, range_irreps[me], axis=1)]
    slice x1, local copies, waits for them, and re-layouts: 0.74 us -> 7.78 us  [body(): arrived[:, :, j, :]]
    reshape x0 -> x1, local copies, waits for them, and re-layouts: none -> 6.44 us  [body(): jnp.stack([low, high], axis=1)]
    all_gather x1 -> x0, local copies, waits for them, and re-layouts: 5.5 us -> none  [body(): gathered = lax.all_gather(slab[:, :, j, :], 'z', axis=0, tiled=False)]
  transfers between devices with their start and end apart: 8 -> 6, of which waited for: 6 -> 6; matrix products, arithmetic and copies ran while one was open for 8% -> 4% of each run, Pallas kernels for 0% -> 0%
where the time goes in v3:
time: 370 us; the launch traced here: 369 us
  waiting for transfers between devices  259 us (70%)
  starting transfers between devices  49.8 us (13%)
  local copies, waits for them, and re-layouts  25 us (7%)
  between operations  17.3 us (5%)
  other arithmetic  12.5 us (3%)
  matrix products  5.39 us (1%)
    all_gather x1, waiting for transfers between devices, body(): gathered = lax.all_gather(trial_slab, 'z', axis=0, tiled=False)  149 us
    all_to_all x2, waiting for transfers between devices, body(): lax.all_to_all(summed, ('z', 'core'), split_axis=0, concat_axis=0, tiled=...  58.2 us
    all_to_all x2, waiting for transfers between devices, body(): lax.all_to_all(products.astype(jnp.bfloat16), 'narrow', split_axis=0, con...  49.7 us
    all_to_all x2, starting transfers between devices, body(): lax.all_to_all(summed, ('z', 'core'), split_axis=0, concat_axis=0, tiled=...  20.8 us
    ppermute x1, starting transfers between devices, body(): received = lax.ppermute(theirs, 'core', [(0, 1), (1, 0)])  18.9 us
    all_to_all x2, starting transfers between devices, body(): lax.all_to_all(products.astype(jnp.bfloat16), 'narrow', split_axis=0, con...  10.1 us
    slice x1, local copies, waits for them, and re-layouts, body(): arrived[:, :, j, :]  7.78 us
  transfers between devices with their start and end apart: 6, of which 6 were waited for; matrix products, arithmetic and copies ran while one was open for 4% of the time, Pallas kernels for 0%

profile of v3, /device:TPU:1, one launch (start us, length us, event | category | flops | bytes accessed | tf_op | source)
XLA Modules:
  0.0 368.7 jit_solution(6696260208206895495)
XLA Ops:
  6.5 0.0 copy-start
  6.5 0.0 all-gather.3.cloned.1.call-start
  6.5 0.7 all-gather.3.cloned.1.call-update
  7.3 1.3 fusion.5
  10.5 149.3 %all-gather.3.cloned.1.call-done = bf16[256,32,640]{2,1,0:T(8,128)(2,1)} async-done(((bf16[8,32,640]{2,1,0:T(8,128)(2,1)}), bf16[256,32,640]{2,1,0:T(8,128)(2,1)}) %all-gather.3.cloned.1.call-update) | async-done | bytes 10485776 | tf_op jit(solution)/shard_map/all_gather | solution.py:19
  159.7 1.5 fusion
  161.2 18.9 %collective-permute-start = (bf16[32,32,640]{2,1,0:T(8,128)(2,1)S(1)}, bf16[32,32,640]{2,1,0:T(8,128)(2,1)}, u32[]{:S(2)}, u32[]{:S(2)}) collective-permute-start(bf16[32,32,640]{2,1,0:T(8,128)(2,1)S(1)} %fusion), channel_id=1, source_target_pairs={{0,16},{16,0},{1,17},{17,1},{2,18},{18,2},{3,19},{19,3},{4,20},{20... | collective-permute-start | bytes 3932168 | tf_op jit(solution)/shard_map/ppermute | solution.py:22
  182.0 0.8 collective-permute-done
  182.8 2.1 select_bitcast_fusion.1
  184.9 1.8 pad_maximum_fusion
  186.7 6.4 %reshape.10 = bf16[64,16,2,640]{3,2,1,0:T(2,128)(2,1)} reshape(bf16[32,2,32,640]{3,2,1,0:T(8,128)(2,1)} %pad_maximum_fusion) | data formatting | bytes 5242880 | tf_op jit(solution)/shard_map/reshape | solution.py:25
  193.1 7.8 %fusion.4 = (bf16[64,16,1,640]{3,2,1,0:T(2,128)(2,1)S(1)}, bf16[64,16,1,640]{3,2,1,0:T(2,128)(2,1)}) fusion(bf16[64,16,2,640]{3,2,1,0:T(2,128)(2,1)} %reshape.10), kind=kLoop, calls=%fused_computation.14 | loop fusion | bytes 5242880 | tf_op jit(solution)/shard_map/slice | solution.py:29
  200.9 0.0 copy-done
  200.9 1.8 convert_bitcast_fusion.1
  202.7 2.5 copy.21
  205.2 6.4 %all-to-all-start = ((bf16[16,64,1024]{2,1,0:T(8,128)(2,1)}), bf16[16,64,1024]{2,1,0:T(8,128)(2,1)S(1)}, u32[]{:S(2)}, u32[]{:S(2)}) async-start(bf16[16,64,1024]{2,1,0:T(8,128)(2,1)} %copy.21), calls=%async_computation | async-start | bytes 4194304 | tf_op jit(solution)/shard_map/all_to_all | solution.py:31
  211.7 3.6 convert_bitcast_fusion
  215.2 2.5 copy.24
  217.7 26.0 %all-to-all-done = bf16[16,64,1024]{2,1,0:T(8,128)(2,1)S(1)} async-done(((bf16[16,64,1024]{2,1,0:T(8,128)(2,1)}), bf16[16,64,1024]{2,1,0:T(8,128)(2,1)S(1)}, u32[]{:S(2)}, u32[]{:S(2)}) %all-to-all-start) | async-done | bytes 2097184 | tf_op jit(solution)/shard_map/all_to_all | solution.py:31
  243.8 0.0 copy-start.1
  243.8 1.3 copy-done.1
  245.1 3.7 %all-to-all-start.2 = ((bf16[16,64,1024]{2,1,0:T(8,128)(2,1)}), bf16[16,64,1024]{2,1,0:T(8,128)(2,1)S(1)}, u32[]{:S(2)}, u32[]{:S(2)}) async-start(bf16[16,64,1024]{2,1,0:T(8,128)(2,1)} %copy.24), calls=%async_computation.2 | async-start | bytes 4194304 | tf_op jit(solution)/shard_map/all_to_all | solution.py:31
  248.8 2.0 reduce_sum.24
  250.8 0.5 broadcast.46
  251.3 1.3 reduce.3
  252.6 1.6 reshape.74
  254.3 23.7 %all-to-all-done.2 = bf16[16,64,1024]{2,1,0:T(8,128)(2,1)S(1)} async-done(((bf16[16,64,1024]{2,1,0:T(8,128)(2,1)}), bf16[16,64,1024]{2,1,0:T(8,128)(2,1)S(1)}, u32[]{:S(2)}, u32[]{:S(2)}) %all-to-all-start.2) | async-done | bytes 2097184 | tf_op jit(solution)/shard_map/all_to_all | solution.py:31
  278.0 15.4 %all-to-all-start.1 = ((bf16[64,2,512]{2,1,0:T(2,128)(2,1)}), bf16[64,2,512]{2,1,0:T(2,128)(2,1)S(1)}, u32[]{:S(2)}, u32[]{:S(2)}) async-start(bf16[64,2,512]{2,1,0:T(2,128)(2,1)} %reshape.74), calls=%async_computation.1 | async-start | bytes 262144 | tf_op jit(solution)/shard_map/all_to_all | solution.py:35
  293.4 1.1 reduce_sum.25
  294.4 1.6 reduce.2
  296.0 0.7 reshape.72
  296.7 27.3 %all-to-all-done.1 = bf16[64,2,512]{2,1,0:T(2,128)(2,1)S(1)} async-done(((bf16[64,2,512]{2,1,0:T(2,128)(2,1)}), bf16[64,2,512]{2,1,0:T(2,128)(2,1)S(1)}, u32[]{:S(2)}, u32[]{:S(2)}) %all-to-all-start.1) | async-done | bytes 131104 | tf_op jit(solution)/shard_map/all_to_all | solution.py:35
  324.0 5.4 %all-to-all-start.3 = ((bf16[64,2,512]{2,1,0:T(2,128)(2,1)}), bf16[64,2,512]{2,1,0:T(2,128)(2,1)S(1)}, u32[]{:S(2)}, u32[]{:S(2)}) async-start(bf16[64,2,512]{2,1,0:T(2,128)(2,1)} %reshape.72), calls=%async_computation.3 | async-start | bytes 262144 | tf_op jit(solution)/shard_map/all_to_all | solution.py:35
  329.5 0.1 reshape.75
  329.6 30.9 %all-to-all-done.3 = bf16[64,2,512]{2,1,0:T(2,128)(2,1)S(1)} async-done(((bf16[64,2,512]{2,1,0:T(2,128)(2,1)}), bf16[64,2,512]{2,1,0:T(2,128)(2,1)S(1)}, u32[]{:S(2)}, u32[]{:S(2)}) %all-to-all-start.3) | async-done | bytes 131104 | tf_op jit(solution)/shard_map/all_to_all | solution.py:35
  360.5 0.1 reshape.73
  360.6 1.3 pad_maximum_fusion.1
Async XLA Ops:
  6.5 194.4 %copy-start = (bf16[1024,640]{1,0:T(8,128)(2,1)S(1)}, bf16[1024,640]{1,0:T(8,128)(2,1)}, u32[]{:S(2)}) copy-start(bf16[1024,640]{1,0:T(8,128)(2,1)} %param.6) | copy-start | bytes 3932164
  6.5 153.2 %all-gather.3.cloned.1.call-start = ((), (), s32[]{:S(2)}) async-start(), calls=%async_computation.4 | async-start | bytes 10813440 | tf_op jit(solution)/shard_map/all_gather | solution.py:19
  161.2 21.6 %collective-permute-start = (bf16[32,32,640]{2,1,0:T(8,128)(2,1)S(1)}, bf16[32,32,640]{2,1,0:T(8,128)(2,1)}, u32[]{:S(2)}, u32[]{:S(2)}) collective-permute-start(bf16[32,32,640]{2,1,0:T(8,128)(2,1)S(1)} %fusion), channel_id=1, source_target_pairs={{0,16},{16,0},{1,17},{17,1},{2,18},{18,2},{3,19},{19,3},{4,20},{20... | collective-permute-start | bytes 3932168 | tf_op jit(solution)/shard_map/ppermute | solution.py:22
  205.2 38.5 %all-to-all-start = ((bf16[16,64,1024]{2,1,0:T(8,128)(2,1)}), bf16[16,64,1024]{2,1,0:T(8,128)(2,1)S(1)}, u32[]{:S(2)}, u32[]{:S(2)}) async-start(bf16[16,64,1024]{2,1,0:T(8,128)(2,1)} %copy.21), calls=%async_computation | async-start | bytes 4194304 | tf_op jit(solution)/shard_map/all_to_all | solution.py:31
  243.8 1.3 copy-start.1
  245.1 32.9 %all-to-all-start.2 = ((bf16[16,64,1024]{2,1,0:T(8,128)(2,1)}), bf16[16,64,1024]{2,1,0:T(8,128)(2,1)S(1)}, u32[]{:S(2)}, u32[]{:S(2)}) async-start(bf16[16,64,1024]{2,1,0:T(8,128)(2,1)} %copy.24), calls=%async_computation.2 | async-start | bytes 4194304 | tf_op jit(solution)/shard_map/all_to_all | solution.py:31
  278.0 46.1 %all-to-all-start.1 = ((bf16[64,2,512]{2,1,0:T(2,128)(2,1)}), bf16[64,2,512]{2,1,0:T(2,128)(2,1)S(1)}, u32[]{:S(2)}, u32[]{:S(2)}) async-start(bf16[64,2,512]{2,1,0:T(2,128)(2,1)} %reshape.74), calls=%async_computation.1 | async-start | bytes 262144 | tf_op jit(solution)/shard_map/all_to_all | solution.py:35
  324.0 36.4 %all-to-all-start.3 = ((bf16[64,2,512]{2,1,0:T(2,128)(2,1)}), bf16[64,2,512]{2,1,0:T(2,128)(2,1)S(1)}, u32[]{:S(2)}, u32[]{:S(2)}) async-start(bf16[64,2,512]{2,1,0:T(2,128)(2,1)} %reshape.72), calls=%async_computation.3 | async-start | bytes 262144 | tf_op jit(solution)/shard_map/all_to_all | solution.py:35
Sparse Core Ops, SparseCore 0:
  10.0 149.6 all-gather.2

commit v4 on v3

v4 whole, which is shorter than its diff:
```python
import jax
import jax.numpy as jnp
from jax import lax
from jax.sharding import Mesh
from jax.sharding import PartitionSpec as P

Z_HI = 4


def body(trial_slab, ladder, range_irreps):
    z_lo_count = lax.axis_size("z_lo")
    chips = lax.axis_size("z_hi") * z_lo_count
    cores = lax.axis_size("core")
    narrow_count = lax.axis_size("narrow")
    pair_count = chips * cores
    irreps, local_rows, block = trial_slab.shape
    per_owner = local_rows // narrow_count
    local_pairs = ladder.shape[0]
    core = lax.axis_index("core")
    chip = lax.axis_index("z_hi") * z_lo_count + lax.axis_index("z_lo")
    me = chip * cores + core
    partner = me + 1 - 2 * core
    near = lax.all_gather(trial_slab, "z_lo", axis=0, tiled=True)
    gathered = lax.all_gather(near, "z_hi", axis=0, tiled=True).reshape(chips, irreps, local_rows, block)
    mine = jnp.take(gathered, range_irreps[me], axis=1)
    theirs = jnp.take(gathered, range_irreps[partner], axis=1)
    received = lax.ppermute(theirs, "core", [(0, 1), (1, 0)])
    products = jnp.stack(
        [
            jnp.einsum("zmc,ac->mza", rows, ladder, preferred_element_type=jnp.float32)
            for rows in (mine, received)
        ],
        axis=1,
    )
    partial = products.astype(jnp.bfloat16).reshape(narrow_count, per_owner, cores, chips, local_pairs)
    exchanged = lax.all_to_all(partial, "narrow", split_axis=0, concat_axis=0, tiled=True)
    summed = jnp.sum(exchanged.astype(jnp.float32), axis=0).astype(jnp.bfloat16)
    by_core = jnp.where(core == 0, summed, summed[:, ::-1])
    by_device = jnp.transpose(by_core, (0, 2, 1, 3)).reshape(per_owner, pair_count, local_pairs)
    owned = lax.all_to_all(by_device, ("z_hi", "z_lo", "core"), split_axis=1, concat_axis=1, tiled=True)
    return owned.reshape(per_owner, pair_count * local_pairs)


def solution(mesh):
    pair_count = mesh.shape["pair"]
    narrow_count = mesh.shape["narrow"]
    devices = mesh.devices.reshape(Z_HI, pair_count // (2 * Z_HI), 2, narrow_count)
    split = Mesh(devices, ("z_hi", "z_lo", "core", "narrow"))
    pair = ("z_hi", "z_lo", "core")
    placed = (P(None, pair, "narrow"), P(pair, "narrow"), P())
    return jax.shard_map(
        body, mesh=split, in_specs=placed, out_specs=P(pair + ("narrow",), None), check_vma=False
    )
```

time: 370 us -> 1020 us (2.76)
  waiting for transfers between devices: 259 us -> 875 us
  blocking collectives: 0 us -> 77.7 us
  starting transfers between devices: 49.8 us -> 9.38 us
  local copies, waits for them, and re-layouts: 25 us -> 12.4 us
    all_gather x1 -> x2, waiting for transfers between devices: 149 us -> 811 us  [the longest x1 715 us: body(): lax.all_gather(near, 'z_hi', axis=0, tiled=True)]
    all_to_all x0 -> x1, blocking collectives: none -> 77.7 us  [body(): lax.all_to_all(by_device, ('z_hi', 'z_lo', 'core'), split_axis=1, concat_...]
    all_to_all x4 -> x1, waiting for transfers between devices: 108 us -> 63.5 us  [body(): lax.all_to_all(partial, 'narrow', split_axis=0, concat_axis=0, tiled=True)]
    all_to_all x4 -> x1, starting transfers between devices: 30.9 us -> 6.6 us  [body(): lax.all_to_all(partial, 'narrow', split_axis=0, concat_axis=0, tiled=True)]
    ppermute x1, starting transfers between devices: 18.9 us -> 2.74 us  [body(): received = lax.ppermute(theirs, 'core', [(0, 1), (1, 0)])]
    another operation x0 -> x3, local copies, waits for them, and re-layouts: none -> 10.9 us  [body(): jnp.stack([jnp.einsum('zmc,ac->mza', rows, ladder, preferred_element_type...]
  transfers between devices with their start and end apart: 6 -> 4, of which waited for: 6 -> 3; matrix products, arithmetic and copies ran while one was open for 4% -> 1% of each run, Pallas kernels for 0% -> 0%
where the time goes in v4:
time: 1020 us
  waiting for transfers between devices  875 us (86%)
  blocking collectives  77.7 us (8%)
  other arithmetic  17.6 us (2%)
  between operations  17.3 us (2%)
  local copies, waits for them, and re-layouts  12.4 us (1%)
    all_gather x1, waiting for transfers between devices, body(): lax.all_gather(near, 'z_hi', axis=0, tiled=True)  715 us
    all_gather x1, waiting for transfers between devices, body(): near = lax.all_gather(trial_slab, 'z_lo', axis=0, tiled=True)  95.3 us
    all_to_all x1, blocking collectives, body(): lax.all_to_all(by_device, ('z_hi', 'z_lo', 'core'), split_axis=1, concat_...  77.7 us
    all_to_all x1, waiting for transfers between devices, body(): lax.all_to_all(partial, 'narrow', split_axis=0, concat_axis=0, tiled=True)  63.5 us
  transfers between devices with their start and end apart: 4, of which 3 were waited for; matrix products, arithmetic and copies ran while one was open for 1% of the time, Pallas kernels for 0%

profile of v4, /device:TPU:1, one launch (start us, length us, event | category | flops | bytes accessed | tf_op | source)
XLA Modules:
  0.0 1015.4 jit_solution(8191606426872747006)
XLA Ops:
  6.5 0.0 copy-start
  6.5 0.0 copy-start.1
  6.5 0.0 all-gather.3.cloned.1.call-start
  6.5 0.7 all-gather.3.cloned.1.call-update
  7.3 0.0 all-gather.5.cloned.1.call-start
  7.3 95.3 %all-gather.3.cloned.1.call-done = bf16[64,32,640]{2,1,0:T(8,128)(2,1)} async-done(((bf16[8,32,640]{2,1,0:T(8,128)(2,1)}), bf16[64,32,640]{2,1,0:T(8,128)(2,1)}) %all-gather.3.cloned.1.call-update) | async-done | bytes 2621456 | tf_op jit(solution)/shard_map/all_gather | solution.py:23
  102.6 0.0 all-gather.5.cloned.1.call-update
  102.7 0.0 copy-done.1
  102.7 0.6 fusion.11
  105.1 715.4 %all-gather.5.cloned.1.call-done = bf16[256,32,640]{2,1,0:T(8,128)(2,1)} async-done(((bf16[64,32,640]{2,1,0:T(8,128)(2,1)}), bf16[256,32,640]{2,1,0:T(8,128)(2,1)}) %all-gather.5.cloned.1.call-update) | async-done | bytes 10485776 | tf_op jit(solution)/shard_map/all_gather | solution.py:24
  820.5 2.5 fusion
  823.1 2.7 collective-permute-start
  827.8 0.0 copy-done
  827.8 3.1 convert_bitcast_fusion.1
  830.9 2.2 stack.9
  833.2 0.0 collective-permute-done
  833.2 3.1 convert_bitcast_fusion
  836.3 2.2 stack.10
  838.5 8.5 pad_maximum_fusion
  847.0 6.4 copy.17
  853.5 6.6 all-to-all-start
  860.1 63.5 %all-to-all-done = bf16[16,2,2,32,1024]{4,1,3,2,0:T(2,128)(2,1)} async-done(((bf16[16,2,2,32,1024]{4,1,3,2,0:T(2,128)(2,1)}), bf16[16,2,2,32,1024]{4,1,3,2,0:T(2,128)(2,1)}, u32[]{:S(2)}, u32[]{:S(2)}) %all-to-all-start) | async-done | bytes 4194336 | tf_op jit(solution)/shard_map/all_to_all | solution.py:36
  923.5 6.3 reduce_sum.12
  929.8 0.2 fusion.8
  930.0 0.2 copy.16
  930.2 77.7 %all_to_all.10 = bf16[2,64,1024]{2,0,1:T(2,128)(2,1)S(1)} all-to-all(bf16[2,64,1024]{2,0,1:T(2,128)(2,1)S(1)} %bitcast.35), channel_id=1, replica_groups=mesh['z_hi'=4,'z_lo'=8,'core'=2,'narrow'=16] {'z_hi','z_lo','core'}, dimensions={1} | all-to-all | bytes 524288 | tf_op jit(solution)/shard_map/all_to_all | solution.py:40
  1007.9 0.7 copy.22
Async XLA Ops:
  6.5 821.2 %copy-start = (bf16[1024,640]{1,0:T(8,128)(2,1)S(1)}, bf16[1024,640]{1,0:T(8,128)(2,1)}, u32[]{:S(2)}) copy-start(bf16[1024,640]{1,0:T(8,128)(2,1)} %param.6) | copy-start | bytes 3932164
  6.5 96.1 %copy-start.1 = (s32[64]{0:T(128)S(1)}, s32[64]{0:T(128)}, u32[]{:S(2)}) copy-start(s32[64]{0:T(128)} %param.7) | copy-start | bytes 772
  6.5 96.1 %all-gather.3.cloned.1.call-start = ((), (), s32[]{:S(2)}) async-start(), calls=%async_computation.2 | async-start | bytes 2949120 | tf_op jit(solution)/shard_map/all_gather | solution.py:23
  7.3 813.3 %all-gather.5.cloned.1.call-start = ((), (), s32[]{:S(2)}) async-start(), calls=%async_computation.3 | async-start | bytes 13107200 | tf_op jit(solution)/shard_map/all_gather | solution.py:24
  823.1 10.1 collective-permute-start
  853.5 70.1 %all-to-all-start = ((bf16[16,2,2,32,1024]{4,1,3,2,0:T(2,128)(2,1)}), bf16[16,2,2,32,1024]{4,1,3,2,0:T(2,128)(2,1)}, u32[]{:S(2)}, u32[]{:S(2)}) async-start(bf16[16,2,2,32,1024]{4,1,3,2,0:T(2,128)(2,1)} %copy.17), calls=%async_computation | async-start | bytes 8388608 | tf_op jit(solution)/shard_map/all_to_all | solution.py:36
Sparse Core Ops, SparseCore 0:
  10.0 92.5 all-gather.2
  105.3 715.1 all-gather.4

commit v5 on v3

--- a/solution.py
+++ b/solution.py
@@ -23,18 +23,15 @@
     low = jnp.where(core == 0, mine, received)
     high = jnp.where(core == 0, received, mine)
     arrived = jnp.stack([low, high], axis=1).reshape(pair_count, narrow_count, per_owner, block)
-    pieces = []
+    products = jnp.einsum("pojc,ac->jopa", arrived, ladder, preferred_element_type=jnp.float32)
+    partial = products.astype(jnp.bfloat16)
+    sums = []
     for j in range(per_owner):
-        products = jnp.einsum(
-            "poc,ac->opa", arrived[:, :, j, :], ladder, preferred_element_type=jnp.float32
-        )
-        exchanged = lax.all_to_all(
-            products.astype(jnp.bfloat16), "narrow", split_axis=0, concat_axis=0, tiled=True
-        )
-        summed = jnp.sum(exchanged.astype(jnp.float32), axis=0).astype(jnp.bfloat16)
-        owned = lax.all_to_all(summed, ("z", "core"), split_axis=0, concat_axis=0, tiled=True)
-        pieces.append(owned.reshape(pair_count * local_pairs))
-    return jnp.stack(pieces, axis=0)
+        exchanged = lax.all_to_all(partial[j], "narrow", split_axis=0, concat_axis=0, tiled=True)
+        sums.append(jnp.sum(exchanged.astype(jnp.float32), axis=0).astype(jnp.bfloat16))
+    summed = jnp.stack(sums, axis=0)
+    owned = lax.all_to_all(summed, ("z", "core"), split_axis=1, concat_axis=1, tiled=True)
+    return owned.reshape(per_owner, pair_count * local_pairs)
 
 
 def solution(mesh):

time: 370 us -> 342 us (0.924)
  blocking collectives: 0 us -> 56.4 us
  waiting for transfers between devices: 259 us -> 208 us
  starting transfers between devices: 49.8 us -> 29.7 us
  local copies, waits for them, and re-layouts: 25 us -> 17.3 us
  other arithmetic: 12.5 us -> 7.73 us
    all_to_all x0 -> x1, blocking collectives: none -> 56.4 us  [body(): lax.all_to_all(summed, ('z', 'core'), split_axis=1, concat_axis=1, tiled=...]
    all_to_all x4 -> x2, waiting for transfers between devices: 108 us -> 56.9 us  [body(): lax.all_to_all(partial[j], 'narrow', split_axis=0, concat_axis=0, tiled=T...]
    all_to_all x4 -> x2, starting transfers between devices: 30.9 us -> 10.8 us  [body(): lax.all_to_all(partial[j], 'narrow', split_axis=0, concat_axis=0, tiled=T...]
    squeeze x0 -> x3, local copies, waits for them, and re-layouts: none -> 8.5 us  [body(): partial[j]]
    slice x1 -> x0, local copies, waits for them, and re-layouts: 7.78 us -> none  [body(): arrived[:, :, j, :]]
    convert_element_type x2 -> x0, local copies, waits for them, and re-layouts: 5.01 us -> none  [body(): products.astype(jnp.bfloat16)]
  transfers between devices with their start and end apart: 6 -> 4, of which waited for: 6 -> 4; matrix products, arithmetic and copies ran while one was open for 4% -> 2% of each run, Pallas kernels for 0% -> 0%
where the time goes in v5:
time: 342 us
  waiting for transfers between devices  208 us (61%)
  blocking collectives  56.4 us (16%)
  starting transfers between devices  29.7 us (9%)
  local copies, waits for them, and re-layouts  17.3 us (5%)
  between operations  17.1 us (5%)
  other arithmetic  7.73 us (2%)
  matrix products  5.44 us (2%)
    all_gather x1, waiting for transfers between devices, body(): gathered = lax.all_gather(trial_slab, 'z', axis=0, tiled=False)  149 us
    all_to_all x2, waiting for transfers between devices, body(): lax.all_to_all(partial[j], 'narrow', split_axis=0, concat_axis=0, tiled=T...  56.9 us
    all_to_all x1, blocking collectives, body(): lax.all_to_all(summed, ('z', 'core'), split_axis=1, concat_axis=1, tiled=...  56.4 us
    ppermute x1, starting transfers between devices, body(): received = lax.ppermute(theirs, 'core', [(0, 1), (1, 0)])  18.9 us
    all_to_all x2, starting transfers between devices, body(): lax.all_to_all(partial[j], 'narrow', split_axis=0, concat_axis=0, tiled=T...  10.8 us
    squeeze x3, local copies, waits for them, and re-layouts, body(): partial[j]  8.5 us
  transfers between devices with their start and end apart: 4, of which 4 were waited for; matrix products, arithmetic and copies ran while one was open for 2% of the time, Pallas kernels for 0%

profile of v5, /device:TPU:1, one launch (start us, length us, event | category | flops | bytes accessed | tf_op | source)
XLA Modules:
  0.0 341.5 jit_solution(17561830954902826478)
XLA Ops:
  6.5 0.0 copy-start
  6.5 0.0 all-gather.3.cloned.1.call-start
  6.5 0.7 all-gather.3.cloned.1.call-update
  7.3 1.3 fusion.4
  10.3 149.4 %all-gather.3.cloned.1.call-done = bf16[256,32,640]{2,1,0:T(8,128)(2,1)} async-done(((bf16[8,32,640]{2,1,0:T(8,128)(2,1)}), bf16[256,32,640]{2,1,0:T(8,128)(2,1)}) %all-gather.3.cloned.1.call-update) | async-done | bytes 10485776 | tf_op jit(solution)/shard_map/all_gather | solution.py:19
  159.7 1.5 fusion.1
  161.2 18.9 %collective-permute-start = (bf16[32,32,640]{2,1,0:T(8,128)(2,1)S(1)}, bf16[32,32,640]{2,1,0:T(8,128)(2,1)}, u32[]{:S(2)}, u32[]{:S(2)}) collective-permute-start(bf16[32,32,640]{2,1,0:T(8,128)(2,1)S(1)} %fusion.1), channel_id=1, source_target_pairs={{0,16},{16,0},{1,17},{17,1},{2,18},{18,2},{3,19},{19,3},{4,20},{20... | collective-permute-start | bytes 3932168 | tf_op jit(solution)/shard_map/ppermute | solution.py:22
  182.0 0.8 collective-permute-done
  182.8 2.1 select_bitcast_fusion.1
  184.9 1.8 pad_maximum_fusion
  186.7 6.5 %reshape.7 = bf16[64,16,2,640]{3,2,1,0:T(2,128)(2,1)} reshape(bf16[32,2,32,640]{3,2,1,0:T(8,128)(2,1)} %pad_maximum_fusion) | data formatting | bytes 5242880 | tf_op jit(solution)/shard_map/reshape | solution.py:25
  193.1 0.0 copy-done
  193.1 5.4 %convert_bitcast_fusion = bf16[2,16,64,1024]{3,1,0,2:T(8,128)(2,1)S(1)} fusion(bf16[64,16,2,640]{3,2,1,0:T(2,128)(2,1)} %reshape.7, bf16[1024,640]{1,0:T(8,128)(2,1)S(1)} %copy-done), kind=kOutput, calls=%fused_computation | convolution fusion | flops 2686451712 | bytes 8126464 | tf_op jit(solution)/shard_map/pojc,ac->jopa/dot_general | solution.py:26
  198.6 1.9 slice_bitcast_fusion.1
  200.5 2.5 copy.19
  203.0 6.4 %all-to-all-start = ((bf16[16,64,1024]{2,1,0:T(8,128)(2,1)}), bf16[16,64,1024]{2,1,0:T(8,128)(2,1)S(1)}, u32[]{:S(2)}, u32[]{:S(2)}) async-start(bf16[16,64,1024]{2,1,0:T(8,128)(2,1)} %copy.19), calls=%async_computation | async-start | bytes 4194304 | tf_op jit(solution)/shard_map/all_to_all | solution.py:30
  209.4 4.1 %copy.20 = bf16[16,64,1024]{2,1,0:T(8,128)(2,1)} copy(bf16[16,64,1024]{2,0,1:T(8,128)(2,1)} %get-tuple-element.20) | data formatting | bytes 4194304 | tf_op jit(solution)/shard_map/squeeze | solution.py:30
  213.5 28.0 %all-to-all-done = bf16[16,64,1024]{2,1,0:T(8,128)(2,1)S(1)} async-done(((bf16[16,64,1024]{2,1,0:T(8,128)(2,1)}), bf16[16,64,1024]{2,1,0:T(8,128)(2,1)S(1)}, u32[]{:S(2)}, u32[]{:S(2)}) %all-to-all-start) | async-done | bytes 2097184 | tf_op jit(solution)/shard_map/all_to_all | solution.py:30
  241.5 4.4 %all-to-all-start.1 = ((bf16[16,64,1024]{2,1,0:T(8,128)(2,1)}), bf16[16,64,1024]{2,1,0:T(8,128)(2,1)}, u32[]{:S(2)}, u32[]{:S(2)}) async-start(bf16[16,64,1024]{2,1,0:T(8,128)(2,1)} %copy.20), calls=%async_computation.1 | async-start | bytes 4194304 | tf_op jit(solution)/shard_map/all_to_all | solution.py:30
  246.0 0.4 reduce_sum.24
  246.4 28.8 %all-to-all-done.1 = bf16[16,64,1024]{2,1,0:T(8,128)(2,1)} async-done(((bf16[16,64,1024]{2,1,0:T(8,128)(2,1)}), bf16[16,64,1024]{2,1,0:T(8,128)(2,1)}, u32[]{:S(2)}, u32[]{:S(2)}) %all-to-all-start.1) | async-done | bytes 2097184 | tf_op jit(solution)/shard_map/all_to_all | solution.py:30
  275.2 2.0 reduce_sum.25
  277.3 0.3 copy.21
  277.5 56.4 %all_to_all.15 = bf16[2,64,1024]{2,0,1:T(2,128)(2,1)S(1)} all-to-all(bf16[2,64,1024]{2,0,1:T(2,128)(2,1)S(1)} %copy.21), channel_id=1, replica_groups=mesh['z'=32,'core'=2,'narrow'=16] {'z','core'}, dimensions={1} | all-to-all | bytes 524288 | tf_op jit(solution)/shard_map/all_to_all | solution.py:33
  334.0 0.7 copy.28
  (1 shorter events, 0.0 us)
Async XLA Ops:
  6.5 186.6 %copy-start = (bf16[1024,640]{1,0:T(8,128)(2,1)S(1)}, bf16[1024,640]{1,0:T(8,128)(2,1)}, u32[]{:S(2)}) copy-start(bf16[1024,640]{1,0:T(8,128)(2,1)} %param.6) | copy-start | bytes 3932164
  6.5 153.2 %all-gather.3.cloned.1.call-start = ((), (), s32[]{:S(2)}) async-start(), calls=%async_computation.3 | async-start | bytes 10813440 | tf_op jit(solution)/shard_map/all_gather | solution.py:19
  161.2 21.6 %collective-permute-start = (bf16[32,32,640]{2,1,0:T(8,128)(2,1)S(1)}, bf16[32,32,640]{2,1,0:T(8,128)(2,1)}, u32[]{:S(2)}, u32[]{:S(2)}) collective-permute-start(bf16[32,32,640]{2,1,0:T(8,128)(2,1)S(1)} %fusion.1), channel_id=1, source_target_pairs={{0,16},{16,0},{1,17},{17,1},{2,18},{18,2},{3,19},{19,3},{4,20},{20... | collective-permute-start | bytes 3932168 | tf_op jit(solution)/shard_map/ppermute | solution.py:22
  203.0 38.5 %all-to-all-start = ((bf16[16,64,1024]{2,1,0:T(8,128)(2,1)}), bf16[16,64,1024]{2,1,0:T(8,128)(2,1)S(1)}, u32[]{:S(2)}, u32[]{:S(2)}) async-start(bf16[16,64,1024]{2,1,0:T(8,128)(2,1)} %copy.19), calls=%async_computation | async-start | bytes 4194304 | tf_op jit(solution)/shard_map/all_to_all | solution.py:30
  241.5 33.7 %all-to-all-start.1 = ((bf16[16,64,1024]{2,1,0:T(8,128)(2,1)}), bf16[16,64,1024]{2,1,0:T(8,128)(2,1)}, u32[]{:S(2)}, u32[]{:S(2)}) async-start(bf16[16,64,1024]{2,1,0:T(8,128)(2,1)} %copy.20), calls=%async_computation.1 | async-start | bytes 4194304 | tf_op jit(solution)/shard_map/all_to_all | solution.py:30
Sparse Core Ops, SparseCore 0:
  10.0 149.6 all-gather.2

commit v6 on v5

v6 whole, which is shorter than its diff:
```python
import jax
import jax.numpy as jnp
from jax import lax
from jax.sharding import Mesh
from jax.sharding import PartitionSpec as P

GROUPS = 4


def body(trial_slab, ladder, range_irreps):
    chips = lax.axis_size("z")
    cores = lax.axis_size("core")
    narrow_count = lax.axis_size("narrow")
    pair_count = chips * cores
    irreps, local_rows, block = trial_slab.shape
    per_owner = local_rows // narrow_count
    local_pairs = ladder.shape[0]
    core = lax.axis_index("core")
    chip = lax.axis_index("z")
    me = chip * cores + core
    partner = me + 1 - 2 * core
    mine_irrep = range_irreps[me]
    partner_irrep = range_irreps[partner]
    up = [(i, (i + 1) % chips) for i in range(chips)]
    down = [(i, (i - 1) % chips) for i in range(chips)]

    arrivals = [(0, trial_slab)]
    going_up = going_down = trial_slab
    for distance in range(1, chips // 2 + 1):
        going_up = lax.ppermute(going_up, "z", up)
        arrivals.append((chips - distance, going_up))
        if distance < chips - distance:
            going_down = lax.ppermute(going_down, "z", down)
            arrivals.append((distance, going_down))

    size = -(-len(arrivals) // GROUPS)
    order, sums = [], []
    for start in range(0, len(arrivals), size):
        group = arrivals[start:start + size]
        order += [r for r, _ in group]
        mine = jnp.stack([jnp.take(b, mine_irrep, axis=0) for _, b in group])
        theirs = jnp.stack([jnp.take(b, partner_irrep, axis=0) for _, b in group])
        received = lax.ppermute(theirs, "core", [(0, 1), (1, 0)])
        rows = jnp.stack([mine, received])
        products = jnp.einsum("snmc,ac->msna", rows, ladder, preferred_element_type=jnp.float32)
        partial = products.astype(jnp.bfloat16).reshape(
            narrow_count, per_owner, cores, len(group), local_pairs
        )
        exchanged = lax.all_to_all(partial, "narrow", split_axis=0, concat_axis=0, tiled=True)
        sums.append(jnp.sum(exchanged.astype(jnp.float32), axis=0).astype(jnp.bfloat16))
    summed = jnp.concatenate(sums, axis=2)
    by_offset = jnp.take(summed, jnp.array([order.index(r) for r in range(chips)]), axis=2)
    by_chip = jnp.roll(by_offset, chip, axis=2)
    by_core = jnp.where(core == 0, by_chip, by_chip[:, ::-1])
    by_device = jnp.transpose(by_core, (0, 2, 1, 3)).reshape(per_owner, pair_count, local_pairs)
    owned = lax.all_to_all(by_device, ("z", "core"), split_axis=1, concat_axis=1, tiled=True)
    return owned.reshape(per_owner, pair_count * local_pairs)


def solution(mesh):
    pair_count = mesh.shape["pair"]
    narrow_count = mesh.shape["narrow"]
    split = Mesh(mesh.devices.reshape(pair_count // 2, 2, narrow_count), ("z", "core", "narrow"))
    placed = (P(None, ("z", "core"), "narrow"), P(("z", "core"), "narrow"), P())
    return jax.shard_map(
        body, mesh=split, in_specs=placed, out_specs=P(("z", "core", "narrow"), None), check_vma=False
    )
```

time: 342 us -> 336 us (0.982)
  waiting for transfers between devices: 208 us -> 37.5 us
  starting transfers between devices: 29.7 us -> 162 us
  other arithmetic: 7.73 us -> 37.8 us
  between operations: 17.1 us -> 4.71 us
  local copies, waits for them, and re-layouts: 17.3 us -> 22.4 us
  matrix products: 5.44 us -> 9.96 us
    all_gather x1 -> x0, waiting for transfers between devices: 149 us -> none  [body(): gathered = lax.all_gather(trial_slab, 'z', axis=0, tiled=False)]
    ppermute x0 -> x31, starting transfers between devices: none -> 114 us  [the longest x15 80.8 us: body(): going_down = lax.ppermute(going_down, 'z', down)]
    all_to_all x2 -> x4, waiting for transfers between devices: 56.9 us -> 11.8 us  [body(): lax.all_to_all(partial, 'narrow', split_axis=0, concat_axis=0, tiled=True)]
    unnamed x0 -> x28, other arithmetic: none -> 24.9 us
    ppermute x0 -> x31, waiting for transfers between devices: none -> 24.4 us  [the longest x16 24.4 us: body(): going_up = lax.ppermute(going_up, 'z', up)]
    all_to_all x2 -> x4, starting transfers between devices: 10.8 us -> 27.1 us  [body(): lax.all_to_all(partial, 'narrow', split_axis=0, concat_axis=0, tiled=True)]
    reshape x1 -> x8, local copies, waits for them, and re-layouts: 6.46 us -> 17.2 us  [body(): products.astype(jnp.bfloat16)]
    squeeze x3 -> x0, local copies, waits for them, and re-layouts: 8.5 us -> none  [body(): partial[j]]
  transfers between devices with their start and end apart: 4 -> 39, of which waited for: 4 -> 11; matrix products, arithmetic and copies ran while one was open for 2% -> 19% of each run, Pallas kernels for 0% -> 0%
where the time goes in v6:
time: 336 us; the launch traced here: 333 us
  starting transfers between devices  162 us (48%)
  blocking collectives  58.2 us (17%)
  other arithmetic  37.8 us (11%)
  waiting for transfers between devices  37.5 us (11%)
  local copies, waits for them, and re-layouts  22.4 us (7%)
  matrix products  9.96 us (3%)
  between operations  4.71 us (1%)
    ppermute x15, starting transfers between devices, body(): going_down = lax.ppermute(going_down, 'z', down)  80.8 us
    all_to_all x1, blocking collectives, body(): lax.all_to_all(by_device, ('z', 'core'), split_axis=1, concat_axis=1, til...  58.2 us
    ppermute x16, starting transfers between devices, body(): going_up = lax.ppermute(going_up, 'z', up)  33.2 us
    all_to_all x4, starting transfers between devices, body(): lax.all_to_all(partial, 'narrow', split_axis=0, concat_axis=0, tiled=True)  27.1 us
    unnamed x28, other arithmetic  24.9 us
    ppermute x16, waiting for transfers between devices, body(): going_up = lax.ppermute(going_up, 'z', up)  24.4 us
    ppermute x4, starting transfers between devices, body(): received = lax.ppermute(theirs, 'core', [(0, 1), (1, 0)])  21.1 us
    reshape x8, local copies, waits for them, and re-layouts, body(): products.astype(jnp.bfloat16)  17.2 us
  transfers between devices with their start and end apart: 39, of which 11 were waited for; matrix products, arithmetic and copies ran while one was open for 19% of the time, Pallas kernels for 0%

profile of v6, /device:TPU:1, one launch (start us, length us, event | category | flops | bytes accessed | tf_op | source)
XLA Modules:
  0.0 332.7 jit_solution(1968083420694842911)
XLA Ops:
  0.0 4.5 %collective-permute-start = (bf16[8,32,640]{2,1,0:T(8,128)(2,1)}, bf16[8,32,640]{2,1,0:T(8,128)(2,1)S(1)}, u32[]{:S(2)}, u32[]{:S(2)}) collective-permute-start(bf16[8,32,640]{2,1,0:T(8,128)(2,1)} %param.6), channel_id=1, source_target_pairs={{0,32},{32,64},{64,96},{96,128},{128,160},{160,192},{192,224},{224... | collective-permute-start | bytes 983048 | tf_op jit(solution)/shard_map/ppermute | solution.py:30
  4.5 16.8 %collective-permute-start.1 = (bf16[8,32,640]{2,1,0:T(8,128)(2,1)}, bf16[8,32,640]{2,1,0:T(8,128)(2,1)S(1)}, u32[]{:S(2)}, u32[]{:S(2)}) collective-permute-start(bf16[8,32,640]{2,1,0:T(8,128)(2,1)} %param.6), channel_id=1, source_target_pairs={{0,992},{32,0},{64,32},{96,64},{128,96},{160,128},{192,160},{224,1... | collective-permute-start | bytes 983048 | tf_op jit(solution)/shard_map/ppermute | solution.py:33
  21.3 5.7 %collective-permute-done = bf16[8,32,640]{2,1,0:T(8,128)(2,1)S(1)} collective-permute-done((bf16[8,32,640]{2,1,0:T(8,128)(2,1)}, bf16[8,32,640]{2,1,0:T(8,128)(2,1)S(1)}, u32[]{:S(2)}, u32[]{:S(2)}) %collective-permute-start) | collective-permute-done | bytes 327712 | tf_op jit(solution)/shard_map/ppermute | solution.py:30
  28.9 4.6 %collective-permute-start.3 = (bf16[8,32,640]{2,1,0:T(8,128)(2,1)S(1)}, bf16[8,32,640]{2,1,0:T(8,128)(2,1)S(1)}, u32[]{:S(2)}, u32[]{:S(2)}) collective-permute-start(bf16[8,32,640]{2,1,0:T(8,128)(2,1)S(1)} %collective-permute-done.1), channel_id=1, source_target_pairs={{0,992},{32,0},{64,32},{96,64},{128,96},{160,128},{192,160},{224,1... | collective-permute-start | bytes 983048 | tf_op jit(solution)/shard_map/ppermute | solution.py:33
  33.5 4.6 %collective-permute-done.2 = bf16[8,32,640]{2,1,0:T(8,128)(2,1)S(1)} collective-permute-done((bf16[8,32,640]{2,1,0:T(8,128)(2,1)S(1)}, bf16[8,32,640]{2,1,0:T(8,128)(2,1)S(1)}, u32[]{:S(2)}, u32[]{:S(2)}) %collective-permute-start.2) | collective-permute-done | bytes 327712 | tf_op jit(solution)/shard_map/ppermute | solution.py:30
  40.0 4.6 %collective-permute-start.5 = (bf16[8,32,640]{2,1,0:T(8,128)(2,1)S(1)}, bf16[8,32,640]{2,1,0:T(8,128)(2,1)S(1)}, u32[]{:S(2)}, u32[]{:S(2)}) collective-permute-start(bf16[8,32,640]{2,1,0:T(8,128)(2,1)S(1)} %collective-permute-done.3), channel_id=1, source_target_pairs={{0,992},{32,0},{64,32},{96,64},{128,96},{160,128},{192,160},{224,1... | collective-permute-start | bytes 983048 | tf_op jit(solution)/shard_map/ppermute | solution.py:33
  50.0 1.9 collective-permute-start.6
  51.9 4.6 %collective-permute-start.8 = (bf16[8,32,640]{2,1,0:T(8,128)(2,1)S(1)}, bf16[8,32,640]{2,1,0:T(8,128)(2,1)S(1)}, u32[]{:S(2)}, u32[]{:S(2)}) collective-permute-start(bf16[8,32,640]{2,1,0:T(8,128)(2,1)S(1)} %collective-permute-done.5), channel_id=1, source_target_pairs={{0,992},{32,0},{64,32},{96,64},{128,96},{160,128},{192,160},{224,1... | collective-permute-start | bytes 983048 | tf_op jit(solution)/shard_map/ppermute | solution.py:33
  57.5 2.2 collective-permute-done.6
  61.6 4.6 %collective-permute-start.10 = (bf16[8,32,640]{2,1,0:T(8,128)(2,1)S(1)}, bf16[8,32,640]{2,1,0:T(8,128)(2,1)S(1)}, u32[]{:S(2)}, u32[]{:S(2)}) collective-permute-start(bf16[8,32,640]{2,1,0:T(8,128)(2,1)S(1)} %collective-permute-done.8), channel_id=1, source_target_pairs={{0,992},{32,0},{64,32},{96,64},{128,96},{160,128},{192,160},{224,1... | collective-permute-start | bytes 983048 | tf_op jit(solution)/shard_map/ppermute | solution.py:33
  66.3 2.4 collective-permute-done.9
  70.6 4.6 %collective-permute-start.12 = (bf16[8,32,640]{2,1,0:T(8,128)(2,1)S(1)}, bf16[8,32,640]{2,1,0:T(8,128)(2,1)S(1)}, u32[]{:S(2)}, u32[]{:S(2)}) collective-permute-start(bf16[8,32,640]{2,1,0:T(8,128)(2,1)S(1)} %collective-permute-done.10), channel_id=1, source_target_pairs={{0,992},{32,0},{64,32},{96,64},{128,96},{160,128},{192,160},{224,1... | collective-permute-start | bytes 983048 | tf_op jit(solution)/shard_map/ppermute | solution.py:33
  75.3 7.1 %collective-permute-start.7 = (bf16[8,32,640]{2,1,0:T(8,128)(2,1)S(1)}, bf16[8,32,640]{2,1,0:T(8,128)(2,1)S(1)}, u32[]{:S(2)}, u32[]{:S(2)}) collective-permute-start(bf16[8,32,640]{2,1,0:T(8,128)(2,1)S(1)} %get-tuple-element.18), channel_id=1, source_target_pairs={{0,16},{16,0},{1,17},{17,1},{2,18},{18,2},{3,19},{19,3},{4,20},{20... | collective-permute-start | bytes 983048 | tf_op jit(solution)/shard_map/ppermute | solution.py:43
  85.0 4.6 %collective-permute-start.14 = (bf16[8,32,640]{2,1,0:T(8,128)(2,1)S(1)}, bf16[8,32,640]{2,1,0:T(8,128)(2,1)S(1)}, u32[]{:S(2)}, u32[]{:S(2)}) collective-permute-start(bf16[8,32,640]{2,1,0:T(8,128)(2,1)S(1)} %collective-permute-done.12), channel_id=1, source_target_pairs={{0,992},{32,0},{64,32},{96,64},{128,96},{160,128},{192,160},{224,1... | collective-permute-start | bytes 983048 | tf_op jit(solution)/shard_map/ppermute | solution.py:33
  91.5 3.5 %collective-permute-done.13 = bf16[8,32,640]{2,1,0:T(8,128)(2,1)S(1)} collective-permute-done((bf16[8,32,640]{2,1,0:T(8,128)(2,1)S(1)}, bf16[8,32,640]{2,1,0:T(8,128)(2,1)S(1)}, u32[]{:S(2)}, u32[]{:S(2)}) %collective-permute-start.13) | collective-permute-done | bytes 327712 | tf_op jit(solution)/shard_map/ppermute | solution.py:30
  95.0 1.9 collective-permute-start.15
  96.9 4.6 %collective-permute-start.17 = (bf16[8,32,640]{2,1,0:T(8,128)(2,1)S(1)}, bf16[8,32,640]{2,1,0:T(8,128)(2,1)}, u32[]{:S(2)}, u32[]{:S(2)}) collective-permute-start(bf16[8,32,640]{2,1,0:T(8,128)(2,1)S(1)} %collective-permute-done.14), channel_id=1, source_target_pairs={{0,992},{32,0},{64,32},{96,64},{128,96},{160,128},{192,160},{224,1... | collective-permute-start | bytes 983048 | tf_op jit(solution)/shard_map/ppermute | solution.py:33
  103.4 2.7 collective-permute-done.15
  108.1 4.6 %collective-permute-start.19 = (bf16[8,32,640]{2,1,0:T(8,128)(2,1)}, bf16[8,32,640]{2,1,0:T(8,128)(2,1)}, u32[]{:S(2)}, u32[]{:S(2)}) collective-permute-start(bf16[8,32,640]{2,1,0:T(8,128)(2,1)} %collective-permute-done.17), channel_id=1, source_target_pairs={{0,992},{32,0},{64,32},{96,64},{128,96},{160,128},{192,160},{224,1... | collective-permute-start | bytes 983048 | tf_op jit(solution)/shard_map/ppermute | solution.py:33
  114.2 4.6 %collective-permute-start.16 = (bf16[8,32,640]{2,1,0:T(8,128)(2,1)}, bf16[8,32,640]{2,1,0:T(8,128)(2,1)}, u32[]{:S(2)}, u32[]{:S(2)}) collective-permute-start(bf16[8,32,640]{2,1,0:T(8,128)(2,1)} %get-tuple-element.34), channel_id=1, source_target_pairs={{0,16},{16,0},{1,17},{17,1},{2,18},{18,2},{3,19},{19,3},{4,20},{20... | collective-permute-start | bytes 983048 | tf_op jit(solution)/shard_map/ppermute | solution.py:43
  120.3 2.1 copy.6
  122.4 6.9 %all-to-all-start = ((bf16[16,2,2,8,1024]{4,1,3,2,0:T(2,128)(2,1)}), bf16[16,2,2,8,1024]{4,1,3,2,0:T(2,128)(2,1)S(1)}, u32[]{:S(2)}, u32[]{:S(2)}) async-start(bf16[16,2,2,8,1024]{4,1,3,2,0:T(2,128)(2,1)} %copy.6), calls=%async_computation | async-start | bytes 2097152 | tf_op jit(solution)/shard_map/all_to_all | solution.py:49
  129.3 1.9 collective-permute-start.20
  131.2 4.6 %collective-permute-start.21 = (bf16[8,32,640]{2,1,0:T(8,128)(2,1)}, bf16[8,32,640]{2,1,0:T(8,128)(2,1)}, u32[]{:S(2)}, u32[]{:S(2)}) collective-permute-start(bf16[8,32,640]{2,1,0:T(8,128)(2,1)} %collective-permute-done.19), channel_id=1, source_target_pairs={{0,992},{32,0},{64,32},{96,64},{128,96},{160,128},{192,160},{224,1... | collective-permute-start | bytes 983048 | tf_op jit(solution)/shard_map/ppermute | solution.py:33
  137.3 3.0 fusion.1
  141.8 2.1 copy.8
  145.9 4.6 %collective-permute-start.23 = (bf16[8,32,640]{2,1,0:T(8,128)(2,1)}, bf16[8,32,640]{2,1,0:T(8,128)(2,1)S(1)}, u32[]{:S(2)}, u32[]{:S(2)}) collective-permute-start(bf16[8,32,640]{2,1,0:T(8,128)(2,1)} %collective-permute-done.21), channel_id=1, source_target_pairs={{0,992},{32,0},{64,32},{96,64},{128,96},{160,128},{192,160},{224,1... | collective-permute-start | bytes 983048 | tf_op jit(solution)/shard_map/ppermute | solution.py:33
  157.6 4.6 %collective-permute-start.26 = (bf16[8,32,640]{2,1,0:T(8,128)(2,1)S(1)}, bf16[8,32,640]{2,1,0:T(8,128)(2,1)}, u32[]{:S(2)}, u32[]{:S(2)}) collective-permute-start(bf16[8,32,640]{2,1,0:T(8,128)(2,1)S(1)} %collective-permute-done.23), channel_id=1, source_target_pairs={{0,992},{32,0},{64,32},{96,64},{128,96},{160,128},{192,160},{224,1... | collective-permute-start | bytes 983048 | tf_op jit(solution)/shard_map/ppermute | solution.py:33
  168.3 4.6 %collective-permute-start.28 = (bf16[8,32,640]{2,1,0:T(8,128)(2,1)}, bf16[8,32,640]{2,1,0:T(8,128)(2,1)}, u32[]{:S(2)}, u32[]{:S(2)}) collective-permute-start(bf16[8,32,640]{2,1,0:T(8,128)(2,1)} %collective-permute-done.26), channel_id=1, source_target_pairs={{0,992},{32,0},{64,32},{96,64},{128,96},{160,128},{192,160},{224,1... | collective-permute-start | bytes 983048 | tf_op jit(solution)/shard_map/ppermute | solution.py:33
  172.9 6.1 %all-to-all-start.1 = ((bf16[16,2,2,8,1024]{4,1,3,2,0:T(2,128)(2,1)}), bf16[16,2,2,8,1024]{4,1,3,2,0:T(2,128)(2,1)S(1)}, u32[]{:S(2)}, u32[]{:S(2)}) async-start(bf16[16,2,2,8,1024]{4,1,3,2,0:T(2,128)(2,1)} %copy.8), calls=%async_computation.1 | async-start | bytes 2097152 | tf_op jit(solution)/shard_map/all_to_all | solution.py:49
  180.6 5.6 %collective-permute-start.25 = (bf16[8,32,640]{2,1,0:T(8,128)(2,1)}, bf16[8,32,640]{2,1,0:T(8,128)(2,1)S(1)}, u32[]{:S(2)}, u32[]{:S(2)}) collective-permute-start(bf16[8,32,640]{2,1,0:T(8,128)(2,1)} %get-tuple-element.50), channel_id=1, source_target_pairs={{0,16},{16,0},{1,17},{17,1},{2,18},{18,2},{3,19},{19,3},{4,20},{20... | collective-permute-start | bytes 983048 | tf_op jit(solution)/shard_map/ppermute | solution.py:43
  186.2 1.9 collective-permute-start.29
  189.6 4.6 %collective-permute-start.30 = (bf16[8,32,640]{2,1,0:T(8,128)(2,1)}, bf16[8,32,640]{2,1,0:T(8,128)(2,1)}, u32[]{:S(2)}, u32[]{:S(2)}) collective-permute-start(bf16[8,32,640]{2,1,0:T(8,128)(2,1)} %collective-permute-done.28), channel_id=1, source_target_pairs={{0,992},{32,0},{64,32},{96,64},{128,96},{160,128},{192,160},{224,1... | collective-permute-start | bytes 983048 | tf_op jit(solution)/shard_map/ppermute | solution.py:33
  194.2 3.0 fusion.2
  197.2 2.2 reshape.26
  199.4 3.3 copy.10
  202.7 1.9 collective-permute-start.31
  207.7 4.6 %collective-permute-start.32 = (bf16[8,32,640]{2,1,0:T(8,128)(2,1)}, bf16[8,32,640]{2,1,0:T(8,128)(2,1)}, u32[]{:S(2)}, u32[]{:S(2)}) collective-permute-start(bf16[8,32,640]{2,1,0:T(8,128)(2,1)} %collective-permute-done.30), channel_id=1, source_target_pairs={{0,992},{32,0},{64,32},{96,64},{128,96},{160,128},{192,160},{224,1... | collective-permute-start | bytes 983048 | tf_op jit(solution)/shard_map/ppermute | solution.py:33
  216.8 7.0 %all-to-all-start.2 = ((bf16[16,2,2,8,1024]{4,1,3,2,0:T(2,128)(2,1)}), bf16[16,2,2,8,1024]{4,1,3,2,0:T(2,128)(2,1)}, u32[]{:S(2)}, u32[]{:S(2)}) async-start(bf16[16,2,2,8,1024]{4,1,3,2,0:T(2,128)(2,1)} %copy.10), calls=%async_computation.2 | async-start | bytes 2097152 | tf_op jit(solution)/shard_map/all_to_all | solution.py:49
  229.8 3.8 %collective-permute-start.34 = (bf16[8,32,640]{2,1,0:T(8,128)(2,1)}, bf16[8,32,640]{2,1,0:T(8,128)(2,1)S(1)}, u32[]{:S(2)}, u32[]{:S(2)}) collective-permute-start(bf16[8,32,640]{2,1,0:T(8,128)(2,1)} %get-tuple-element.66), channel_id=1, source_target_pairs={{0,16},{16,0},{1,17},{17,1},{2,18},{18,2},{3,19},{19,3},{4,20},{20... | collective-permute-start | bytes 983048 | tf_op jit(solution)/shard_map/ppermute | solution.py:43
  234.9 3.0 fusion.3
  237.8 2.3 reshape.27
  240.1 3.3 copy.12
  243.4 7.1 %all-to-all-start.3 = ((bf16[16,2,2,8,1024]{4,1,3,2,0:T(2,128)(2,1)}), bf16[16,2,2,8,1024]{4,1,3,2,0:T(2,128)(2,1)}, u32[]{:S(2)}, u32[]{:S(2)}) async-start(bf16[16,2,2,8,1024]{4,1,3,2,0:T(2,128)(2,1)} %copy.12), calls=%async_computation.3 | async-start | bytes 2097152 | tf_op jit(solution)/shard_map/all_to_all | solution.py:49
  252.7 2.2 reduce_sum.50
  255.0 11.8 %all-to-all-done.3 = bf16[16,2,2,8,1024]{4,1,3,2,0:T(2,128)(2,1)} async-done(((bf16[16,2,2,8,1024]{4,1,3,2,0:T(2,128)(2,1)}), bf16[16,2,2,8,1024]{4,1,3,2,0:T(2,128)(2,1)}, u32[]{:S(2)}, u32[]{:S(2)}) %all-to-all-start.3) | async-done | bytes 1048608 | tf_op jit(solution)/shard_map/all_to_all | solution.py:49
  266.9 2.2 reduce_sum.51
  273.7 58.2 %all_to_all.25 = bf16[2,64,1024]{2,0,1:T(2,128)(2,1)S(1)} all-to-all(bf16[2,64,1024]{2,0,1:T(2,128)(2,1)S(1)} %bitcast.116), channel_id=1, replica_groups=mesh['z'=32,'core'=2,'narrow'=16] {'z','core'}, dimensions={1} | all-to-all | bytes 524288 | tf_op jit(solution)/shard_map/all_to_all | solution.py:56
  (100 shorter events, 65.0 us)
Async XLA Ops:
  0.0 118.8 %copy-start = (bf16[1024,640]{1,0:T(8,128)(2,1)S(1)}, bf16[1024,640]{1,0:T(8,128)(2,1)}, u32[]{:S(2)}) copy-start(bf16[1024,640]{1,0:T(8,128)(2,1)} %param.7) | copy-start | bytes 3932164
  0.0 27.0 %collective-permute-start = (bf16[8,32,640]{2,1,0:T(8,128)(2,1)}, bf16[8,32,640]{2,1,0:T(8,128)(2,1)S(1)}, u32[]{:S(2)}, u32[]{:S(2)}) collective-permute-start(bf16[8,32,640]{2,1,0:T(8,128)(2,1)} %param.6), channel_id=1, source_target_pairs={{0,32},{32,64},{64,96},{96,128},{128,160},{160,192},{192,224},{224... | collective-permute-start | bytes 983048 | tf_op jit(solution)/shard_map/ppermute | solution.py:30
  4.5 24.4 %collective-permute-start.1 = (bf16[8,32,640]{2,1,0:T(8,128)(2,1)}, bf16[8,32,640]{2,1,0:T(8,128)(2,1)S(1)}, u32[]{:S(2)}, u32[]{:S(2)}) collective-permute-start(bf16[8,32,640]{2,1,0:T(8,128)(2,1)} %param.6), channel_id=1, source_target_pairs={{0,992},{32,0},{64,32},{96,64},{128,96},{160,128},{192,160},{224,1... | collective-permute-start | bytes 983048 | tf_op jit(solution)/shard_map/ppermute | solution.py:33
  27.0 11.1 %collective-permute-start.2 = (bf16[8,32,640]{2,1,0:T(8,128)(2,1)S(1)}, bf16[8,32,640]{2,1,0:T(8,128)(2,1)S(1)}, u32[]{:S(2)}, u32[]{:S(2)}) collective-permute-start(bf16[8,32,640]{2,1,0:T(8,128)(2,1)S(1)} %collective-permute-done), channel_id=1, source_target_pairs={{0,32},{32,64},{64,96},{96,128},{128,160},{160,192},{192,224},{224... | collective-permute-start | bytes 983048 | tf_op jit(solution)/shard_map/ppermute | solution.py:30
  28.9 11.1 %collective-permute-start.3 = (bf16[8,32,640]{2,1,0:T(8,128)(2,1)S(1)}, bf16[8,32,640]{2,1,0:T(8,128)(2,1)S(1)}, u32[]{:S(2)}, u32[]{:S(2)}) collective-permute-start(bf16[8,32,640]{2,1,0:T(8,128)(2,1)S(1)} %collective-permute-done.1), channel_id=1, source_target_pairs={{0,992},{32,0},{64,32},{96,64},{128,96},{160,128},{192,160},{224,1... | collective-permute-start | bytes 983048 | tf_op jit(solution)/shard_map/ppermute | solution.py:33
  38.1 11.9 %collective-permute-start.4 = (bf16[8,32,640]{2,1,0:T(8,128)(2,1)S(1)}, bf16[8,32,640]{2,1,0:T(8,128)(2,1)S(1)}, u32[]{:S(2)}, u32[]{:S(2)}) collective-permute-start(bf16[8,32,640]{2,1,0:T(8,128)(2,1)S(1)} %collective-permute-done.2), channel_id=1, source_target_pairs={{0,32},{32,64},{64,96},{96,128},{128,160},{160,192},{192,224},{224... | collective-permute-start | bytes 983048 | tf_op jit(solution)/shard_map/ppermute | solution.py:30
  40.0 11.9 %collective-permute-start.5 = (bf16[8,32,640]{2,1,0:T(8,128)(2,1)S(1)}, bf16[8,32,640]{2,1,0:T(8,128)(2,1)S(1)}, u32[]{:S(2)}, u32[]{:S(2)}) collective-permute-start(bf16[8,32,640]{2,1,0:T(8,128)(2,1)S(1)} %collective-permute-done.3), channel_id=1, source_target_pairs={{0,992},{32,0},{64,32},{96,64},{128,96},{160,128},{192,160},{224,1... | collective-permute-start | bytes 983048 | tf_op jit(solution)/shard_map/ppermute | solution.py:33
  50.0 9.7 %collective-permute-start.6 = (bf16[8,32,640]{2,1,0:T(8,128)(2,1)S(1)}, bf16[8,32,640]{2,1,0:T(8,128)(2,1)S(1)}, u32[]{:S(2)}, u32[]{:S(2)}) collective-permute-start(bf16[8,32,640]{2,1,0:T(8,128)(2,1)S(1)} %collective-permute-done.4), channel_id=1, source_target_pairs={{0,32},{32,64},{64,96},{96,128},{128,160},{160,192},{192,224},{224... | collective-permute-start | bytes 983048 | tf_op jit(solution)/shard_map/ppermute | solution.py:30
  51.9 9.7 %collective-permute-start.8 = (bf16[8,32,640]{2,1,0:T(8,128)(2,1)S(1)}, bf16[8,32,640]{2,1,0:T(8,128)(2,1)S(1)}, u32[]{:S(2)}, u32[]{:S(2)}) collective-permute-start(bf16[8,32,640]{2,1,0:T(8,128)(2,1)S(1)} %collective-permute-done.5), channel_id=1, source_target_pairs={{0,992},{32,0},{64,32},{96,64},{128,96},{160,128},{192,160},{224,1... | collective-permute-start | bytes 983048 | tf_op jit(solution)/shard_map/ppermute | solution.py:33
  59.7 9.0 %collective-permute-start.9 = (bf16[8,32,640]{2,1,0:T(8,128)(2,1)S(1)}, bf16[8,32,640]{2,1,0:T(8,128)(2,1)S(1)}, u32[]{:S(2)}, u32[]{:S(2)}) collective-permute-start(bf16[8,32,640]{2,1,0:T(8,128)(2,1)S(1)} %collective-permute-done.6), channel_id=1, source_target_pairs={{0,32},{32,64},{64,96},{96,128},{128,160},{160,192},{192,224},{224... | collective-permute-start | bytes 983048 | tf_op jit(solution)/shard_map/ppermute | solution.py:30
  61.6 9.0 %collective-permute-start.10 = (bf16[8,32,640]{2,1,0:T(8,128)(2,1)S(1)}, bf16[8,32,640]{2,1,0:T(8,128)(2,1)S(1)}, u32[]{:S(2)}, u32[]{:S(2)}) collective-permute-start(bf16[8,32,640]{2,1,0:T(8,128)(2,1)S(1)} %collective-permute-done.8), channel_id=1, source_target_pairs={{0,992},{32,0},{64,32},{96,64},{128,96},{160,128},{192,160},{224,1... | collective-permute-start | bytes 983048 | tf_op jit(solution)/shard_map/ppermute | solution.py:33
  68.7 14.4 %collective-permute-start.11 = (bf16[8,32,640]{2,1,0:T(8,128)(2,1)S(1)}, bf16[8,32,640]{2,1,0:T(8,128)(2,1)S(1)}, u32[]{:S(2)}, u32[]{:S(2)}) collective-permute-start(bf16[8,32,640]{2,1,0:T(8,128)(2,1)S(1)} %collective-permute-done.9), channel_id=1, source_target_pairs={{0,32},{32,64},{64,96},{96,128},{128,160},{160,192},{192,224},{224... | collective-permute-start | bytes 983048 | tf_op jit(solution)/shard_map/ppermute | solution.py:30
  70.6 14.4 %collective-permute-start.12 = (bf16[8,32,640]{2,1,0:T(8,128)(2,1)S(1)}, bf16[8,32,640]{2,1,0:T(8,128)(2,1)S(1)}, u32[]{:S(2)}, u32[]{:S(2)}) collective-permute-start(bf16[8,32,640]{2,1,0:T(8,128)(2,1)S(1)} %collective-permute-done.10), channel_id=1, source_target_pairs={{0,992},{32,0},{64,32},{96,64},{128,96},{160,128},{192,160},{224,1... | collective-permute-start | bytes 983048 | tf_op jit(solution)/shard_map/ppermute | solution.py:33
  75.3 43.5 %collective-permute-start.7 = (bf16[8,32,640]{2,1,0:T(8,128)(2,1)S(1)}, bf16[8,32,640]{2,1,0:T(8,128)(2,1)S(1)}, u32[]{:S(2)}, u32[]{:S(2)}) collective-permute-start(bf16[8,32,640]{2,1,0:T(8,128)(2,1)S(1)} %get-tuple-element.18), channel_id=1, source_target_pairs={{0,16},{16,0},{1,17},{17,1},{2,18},{18,2},{3,19},{19,3},{4,20},{20... | collective-permute-start | bytes 983048 | tf_op jit(solution)/shard_map/ppermute | solution.py:43
  83.1 11.9 %collective-permute-start.13 = (bf16[8,32,640]{2,1,0:T(8,128)(2,1)S(1)}, bf16[8,32,640]{2,1,0:T(8,128)(2,1)S(1)}, u32[]{:S(2)}, u32[]{:S(2)}) collective-permute-start(bf16[8,32,640]{2,1,0:T(8,128)(2,1)S(1)} %collective-permute-done.11), channel_id=1, source_target_pairs={{0,32},{32,64},{64,96},{96,128},{128,160},{160,192},{192,224},{224... | collective-permute-start | bytes 983048 | tf_op jit(solution)/shard_map/ppermute | solution.py:30
  85.0 11.9 %collective-permute-start.14 = (bf16[8,32,640]{2,1,0:T(8,128)(2,1)S(1)}, bf16[8,32,640]{2,1,0:T(8,128)(2,1)S(1)}, u32[]{:S(2)}, u32[]{:S(2)}) collective-permute-start(bf16[8,32,640]{2,1,0:T(8,128)(2,1)S(1)} %collective-permute-done.12), channel_id=1, source_target_pairs={{0,992},{32,0},{64,32},{96,64},{128,96},{160,128},{192,160},{224,1... | collective-permute-start | bytes 983048 | tf_op jit(solution)/shard_map/ppermute | solution.py:33
  95.0 11.2 %collective-permute-start.15 = (bf16[8,32,640]{2,1,0:T(8,128)(2,1)S(1)}, bf16[8,32,640]{2,1,0:T(8,128)(2,1)}, u32[]{:S(2)}, u32[]{:S(2)}) collective-permute-start(bf16[8,32,640]{2,1,0:T(8,128)(2,1)S(1)} %collective-permute-done.13), channel_id=1, source_target_pairs={{0,32},{32,64},{64,96},{96,128},{128,160},{160,192},{192,224},{224... | collective-permute-start | bytes 983048 | tf_op jit(solution)/shard_map/ppermute | solution.py:30
  96.9 11.1 %collective-permute-start.17 = (bf16[8,32,640]{2,1,0:T(8,128)(2,1)S(1)}, bf16[8,32,640]{2,1,0:T(8,128)(2,1)}, u32[]{:S(2)}, u32[]{:S(2)}) collective-permute-start(bf16[8,32,640]{2,1,0:T(8,128)(2,1)S(1)} %collective-permute-done.14), channel_id=1, source_target_pairs={{0,992},{32,0},{64,32},{96,64},{128,96},{160,128},{192,160},{224,1... | collective-permute-start | bytes 983048 | tf_op jit(solution)/shard_map/ppermute | solution.py:33
  106.2 23.1 %collective-permute-start.18 = (bf16[8,32,640]{2,1,0:T(8,128)(2,1)}, bf16[8,32,640]{2,1,0:T(8,128)(2,1)}, u32[]{:S(2)}, u32[]{:S(2)}) collective-permute-start(bf16[8,32,640]{2,1,0:T(8,128)(2,1)} %collective-permute-done.15), channel_id=1, source_target_pairs={{0,32},{32,64},{64,96},{96,128},{128,160},{160,192},{192,224},{224... | collective-permute-start | bytes 983048 | tf_op jit(solution)/shard_map/ppermute | solution.py:30
  108.1 23.2 %collective-permute-start.19 = (bf16[8,32,640]{2,1,0:T(8,128)(2,1)}, bf16[8,32,640]{2,1,0:T(8,128)(2,1)}, u32[]{:S(2)}, u32[]{:S(2)}) collective-permute-start(bf16[8,32,640]{2,1,0:T(8,128)(2,1)} %collective-permute-done.17), channel_id=1, source_target_pairs={{0,992},{32,0},{64,32},{96,64},{128,96},{160,128},{192,160},{224,1... | collective-permute-start | bytes 983048 | tf_op jit(solution)/shard_map/ppermute | solution.py:33
  114.2 4.7 %copy-start.1 = (bf16[8,32,640]{2,1,0:T(8,128)(2,1)}, bf16[8,32,640]{2,1,0:T(8,128)(2,1)S(1)}, u32[]{:S(2)}) copy-start(bf16[8,32,640]{2,1,0:T(8,128)(2,1)S(1)} %get-tuple-element.33) | copy-start | bytes 983044
  114.2 23.2 %collective-permute-start.16 = (bf16[8,32,640]{2,1,0:T(8,128)(2,1)}, bf16[8,32,640]{2,1,0:T(8,128)(2,1)}, u32[]{:S(2)}, u32[]{:S(2)}) collective-permute-start(bf16[8,32,640]{2,1,0:T(8,128)(2,1)} %get-tuple-element.34), channel_id=1, source_target_pairs={{0,16},{16,0},{1,17},{17,1},{2,18},{18,2},{3,19},{19,3},{4,20},{20... | collective-permute-start | bytes 983048 | tf_op jit(solution)/shard_map/ppermute | solution.py:43
  122.4 14.9 %copy-start.2 = (bf16[8,32,640]{2,1,0:T(8,128)(2,1)S(1)}, bf16[8,32,640]{2,1,0:T(8,128)(2,1)}, u32[]{:S(2)}) copy-start(bf16[8,32,640]{2,1,0:T(8,128)(2,1)} %copy-done.1) | copy-start | bytes 983044
  122.4 50.5 %all-to-all-start = ((bf16[16,2,2,8,1024]{4,1,3,2,0:T(2,128)(2,1)}), bf16[16,2,2,8,1024]{4,1,3,2,0:T(2,128)(2,1)S(1)}, u32[]{:S(2)}, u32[]{:S(2)}) async-start(bf16[16,2,2,8,1024]{4,1,3,2,0:T(2,128)(2,1)} %copy.6), calls=%async_computation | async-start | bytes 2097152 | tf_op jit(solution)/shard_map/all_to_all | solution.py:49
  129.3 14.6 %collective-permute-start.20 = (bf16[8,32,640]{2,1,0:T(8,128)(2,1)}, bf16[8,32,640]{2,1,0:T(8,128)(2,1)}, u32[]{:S(2)}, u32[]{:S(2)}) collective-permute-start(bf16[8,32,640]{2,1,0:T(8,128)(2,1)} %collective-permute-done.18), channel_id=1, source_target_pairs={{0,32},{32,64},{64,96},{96,128},{128,160},{160,192},{192,224},{224... | collective-permute-start | bytes 983048 | tf_op jit(solution)/shard_map/ppermute | solution.py:30
  131.2 14.6 %collective-permute-start.21 = (bf16[8,32,640]{2,1,0:T(8,128)(2,1)}, bf16[8,32,640]{2,1,0:T(8,128)(2,1)}, u32[]{:S(2)}, u32[]{:S(2)}) collective-permute-start(bf16[8,32,640]{2,1,0:T(8,128)(2,1)} %collective-permute-done.19), channel_id=1, source_target_pairs={{0,992},{32,0},{64,32},{96,64},{128,96},{160,128},{192,160},{224,1... | collective-permute-start | bytes 983048 | tf_op jit(solution)/shard_map/ppermute | solution.py:33
  143.9 11.7 %collective-permute-start.22 = (bf16[8,32,640]{2,1,0:T(8,128)(2,1)}, bf16[8,32,640]{2,1,0:T(8,128)(2,1)S(1)}, u32[]{:S(2)}, u32[]{:S(2)}) collective-permute-start(bf16[8,32,640]{2,1,0:T(8,128)(2,1)} %collective-permute-done.20), channel_id=1, source_target_pairs={{0,32},{32,64},{64,96},{96,128},{128,160},{160,192},{192,224},{224... | collective-permute-start | bytes 983048 | tf_op jit(solution)/shard_map/ppermute | solution.py:30
  145.9 11.7 %collective-permute-start.23 = (bf16[8,32,640]{2,1,0:T(8,128)(2,1)}, bf16[8,32,640]{2,1,0:T(8,128)(2,1)S(1)}, u32[]{:S(2)}, u32[]{:S(2)}) collective-permute-start(bf16[8,32,640]{2,1,0:T(8,128)(2,1)} %collective-permute-done.21), channel_id=1, source_target_pairs={{0,992},{32,0},{64,32},{96,64},{128,96},{160,128},{192,160},{224,1... | collective-permute-start | bytes 983048 | tf_op jit(solution)/shard_map/ppermute | solution.py:33
  155.7 10.8 %collective-permute-start.24 = (bf16[8,32,640]{2,1,0:T(8,128)(2,1)S(1)}, bf16[8,32,640]{2,1,0:T(8,128)(2,1)}, u32[]{:S(2)}, u32[]{:S(2)}) collective-permute-start(bf16[8,32,640]{2,1,0:T(8,128)(2,1)S(1)} %collective-permute-done.22), channel_id=1, source_target_pairs={{0,32},{32,64},{64,96},{96,128},{128,160},{160,192},{192,224},{224... | collective-permute-start | bytes 983048 | tf_op jit(solution)/shard_map/ppermute | solution.py:30
  157.6 10.8 %collective-permute-start.26 = (bf16[8,32,640]{2,1,0:T(8,128)(2,1)S(1)}, bf16[8,32,640]{2,1,0:T(8,128)(2,1)}, u32[]{:S(2)}, u32[]{:S(2)}) collective-permute-start(bf16[8,32,640]{2,1,0:T(8,128)(2,1)S(1)} %collective-permute-done.23), channel_id=1, source_target_pairs={{0,992},{32,0},{64,32},{96,64},{128,96},{160,128},{192,160},{224,1... | collective-permute-start | bytes 983048 | tf_op jit(solution)/shard_map/ppermute | solution.py:33
  166.4 19.7 %collective-permute-start.27 = (bf16[8,32,640]{2,1,0:T(8,128)(2,1)}, bf16[8,32,640]{2,1,0:T(8,128)(2,1)}, u32[]{:S(2)}, u32[]{:S(2)}) collective-permute-start(bf16[8,32,640]{2,1,0:T(8,128)(2,1)} %collective-permute-done.24), channel_id=1, source_target_pairs={{0,32},{32,64},{64,96},{96,128},{128,160},{160,192},{192,224},{224... | collective-permute-start | bytes 983048 | tf_op jit(solution)/shard_map/ppermute | solution.py:30
  168.3 21.3 %collective-permute-start.28 = (bf16[8,32,640]{2,1,0:T(8,128)(2,1)}, bf16[8,32,640]{2,1,0:T(8,128)(2,1)}, u32[]{:S(2)}, u32[]{:S(2)}) collective-permute-start(bf16[8,32,640]{2,1,0:T(8,128)(2,1)} %collective-permute-done.26), channel_id=1, source_target_pairs={{0,992},{32,0},{64,32},{96,64},{128,96},{160,128},{192,160},{224,1... | collective-permute-start | bytes 983048 | tf_op jit(solution)/shard_map/ppermute | solution.py:33
  172.9 43.8 %all-to-all-start.1 = ((bf16[16,2,2,8,1024]{4,1,3,2,0:T(2,128)(2,1)}), bf16[16,2,2,8,1024]{4,1,3,2,0:T(2,128)(2,1)S(1)}, u32[]{:S(2)}, u32[]{:S(2)}) async-start(bf16[16,2,2,8,1024]{4,1,3,2,0:T(2,128)(2,1)} %copy.8), calls=%async_computation.1 | async-start | bytes 2097152 | tf_op jit(solution)/shard_map/all_to_all | solution.py:49
  180.6 13.6 %collective-permute-start.25 = (bf16[8,32,640]{2,1,0:T(8,128)(2,1)}, bf16[8,32,640]{2,1,0:T(8,128)(2,1)S(1)}, u32[]{:S(2)}, u32[]{:S(2)}) collective-permute-start(bf16[8,32,640]{2,1,0:T(8,128)(2,1)} %get-tuple-element.50), channel_id=1, source_target_pairs={{0,16},{16,0},{1,17},{17,1},{2,18},{18,2},{3,19},{19,3},{4,20},{20... | collective-permute-start | bytes 983048 | tf_op jit(solution)/shard_map/ppermute | solution.py:43
  186.2 16.6 %collective-permute-start.29 = (bf16[8,32,640]{2,1,0:T(8,128)(2,1)}, bf16[8,32,640]{2,1,0:T(8,128)(2,1)}, u32[]{:S(2)}, u32[]{:S(2)}) collective-permute-start(bf16[8,32,640]{2,1,0:T(8,128)(2,1)} %collective-permute-done.27), channel_id=1, source_target_pairs={{0,32},{32,64},{64,96},{96,128},{128,160},{160,192},{192,224},{224... | collective-permute-start | bytes 983048 | tf_op jit(solution)/shard_map/ppermute | solution.py:30
  189.6 18.1 %collective-permute-start.30 = (bf16[8,32,640]{2,1,0:T(8,128)(2,1)}, bf16[8,32,640]{2,1,0:T(8,128)(2,1)}, u32[]{:S(2)}, u32[]{:S(2)}) collective-permute-start(bf16[8,32,640]{2,1,0:T(8,128)(2,1)} %collective-permute-done.28), channel_id=1, source_target_pairs={{0,992},{32,0},{64,32},{96,64},{128,96},{160,128},{192,160},{224,1... | collective-permute-start | bytes 983048 | tf_op jit(solution)/shard_map/ppermute | solution.py:33
  202.7 12.1 %collective-permute-start.31 = (bf16[8,32,640]{2,1,0:T(8,128)(2,1)}, bf16[8,32,640]{2,1,0:T(8,128)(2,1)}, u32[]{:S(2)}, u32[]{:S(2)}) collective-permute-start(bf16[8,32,640]{2,1,0:T(8,128)(2,1)} %collective-permute-done.29), channel_id=1, source_target_pairs={{0,32},{32,64},{64,96},{96,128},{128,160},{160,192},{192,224},{224... | collective-permute-start | bytes 983048 | tf_op jit(solution)/shard_map/ppermute | solution.py:30
  207.7 19.1 %collective-permute-start.32 = (bf16[8,32,640]{2,1,0:T(8,128)(2,1)}, bf16[8,32,640]{2,1,0:T(8,128)(2,1)}, u32[]{:S(2)}, u32[]{:S(2)}) collective-permute-start(bf16[8,32,640]{2,1,0:T(8,128)(2,1)} %collective-permute-done.30), channel_id=1, source_target_pairs={{0,992},{32,0},{64,32},{96,64},{128,96},{160,128},{192,160},{224,1... | collective-permute-start | bytes 983048 | tf_op jit(solution)/shard_map/ppermute | solution.py:33
  214.8 13.5 %collective-permute-start.33 = (bf16[8,32,640]{2,1,0:T(8,128)(2,1)}, bf16[8,32,640]{2,1,0:T(8,128)(2,1)}, u32[]{:S(2)}, u32[]{:S(2)}) collective-permute-start(bf16[8,32,640]{2,1,0:T(8,128)(2,1)} %collective-permute-done.31), channel_id=1, source_target_pairs={{0,32},{32,64},{64,96},{96,128},{128,160},{160,192},{192,224},{224... | collective-permute-start | bytes 983048 | tf_op jit(solution)/shard_map/ppermute | solution.py:30
  216.8 26.6 %all-to-all-start.2 = ((bf16[16,2,2,8,1024]{4,1,3,2,0:T(2,128)(2,1)}), bf16[16,2,2,8,1024]{4,1,3,2,0:T(2,128)(2,1)}, u32[]{:S(2)}, u32[]{:S(2)}) async-start(bf16[16,2,2,8,1024]{4,1,3,2,0:T(2,128)(2,1)} %copy.10), calls=%async_computation.2 | async-start | bytes 2097152 | tf_op jit(solution)/shard_map/all_to_all | solution.py:49
  229.8 5.1 %collective-permute-start.34 = (bf16[8,32,640]{2,1,0:T(8,128)(2,1)}, bf16[8,32,640]{2,1,0:T(8,128)(2,1)S(1)}, u32[]{:S(2)}, u32[]{:S(2)}) collective-permute-start(bf16[8,32,640]{2,1,0:T(8,128)(2,1)} %get-tuple-element.66), channel_id=1, source_target_pairs={{0,16},{16,0},{1,17},{17,1},{2,18},{18,2},{3,19},{19,3},{4,20},{20... | collective-permute-start | bytes 983048 | tf_op jit(solution)/shard_map/ppermute | solution.py:43
  243.4 7.1 %copy-start.3 = (s32[32]{0:T(128)S(1)}, s32[32]{0:T(128)}, u32[]{:S(2)}) copy-start(s32[32]{0:T(128)} %constant.229) | copy-start | bytes 388
  243.4 23.5 %all-to-all-start.3 = ((bf16[16,2,2,8,1024]{4,1,3,2,0:T(2,128)(2,1)}), bf16[16,2,2,8,1024]{4,1,3,2,0:T(2,128)(2,1)}, u32[]{:S(2)}, u32[]{:S(2)}) async-start(bf16[16,2,2,8,1024]{4,1,3,2,0:T(2,128)(2,1)} %copy.12), calls=%async_computation.3 | async-start | bytes 2097152 | tf_op jit(solution)/shard_map/all_to_all | solution.py:49

commit v7 on v6

--- a/solution.py
+++ b/solution.py
@@ -38,8 +38,9 @@
     for start in range(0, len(arrivals), size):
         group = arrivals[start:start + size]
         order += [r for r, _ in group]
-        mine = jnp.stack([jnp.take(b, mine_irrep, axis=0) for _, b in group])
-        theirs = jnp.stack([jnp.take(b, partner_irrep, axis=0) for _, b in group])
+        blocks = jnp.stack([b for _, b in group])
+        mine = jnp.take(blocks, mine_irrep, axis=1)
+        theirs = jnp.take(blocks, partner_irrep, axis=1)
         received = lax.ppermute(theirs, "core", [(0, 1), (1, 0)])
         rows = jnp.stack([mine, received])
         products = jnp.einsum("snmc,ac->msna", rows, ladder, preferred_element_type=jnp.float32)

time: 336 us -> 343 us (1.021)
  local copies, waits for them, and re-layouts: 22.4 us -> 57.4 us
  other arithmetic: 37.8 us -> 14.5 us
    unnamed x9 -> x33, local copies, waits for them, and re-layouts: 0.72 us -> 31.6 us
    unnamed x28 -> x0, other arithmetic: 24.9 us -> none
    another operation x0 -> x4, local copies, waits for them, and re-layouts: none -> 4.33 us  [body(): blocks = jnp.stack([b for _, b in group])]
  transfers between devices with their start and end apart: 39 -> 39, of which waited for: 11 -> 13; matrix products, arithmetic and copies ran while one was open for 19% -> 21% of each run, Pallas kernels for 0% -> 0%
where the time goes in v7:
time: 343 us; the launch traced here: 340 us
  starting transfers between devices  163 us (48%)
  blocking collectives  58.2 us (17%)
  local copies, waits for them, and re-layouts  57.4 us (17%)
  waiting for transfers between devices  35.9 us (10%)
  other arithmetic  14.5 us (4%)
  matrix products  7.02 us (2%)
  between operations  4.34 us (1%)
    ppermute x15, starting transfers between devices, body(): going_down = lax.ppermute(going_down, 'z', down)  82.4 us
    all_to_all x1, blocking collectives, body(): lax.all_to_all(by_device, ('z', 'core'), split_axis=1, concat_axis=1, til...  58.2 us
    ppermute x16, starting transfers between devices, body(): going_up = lax.ppermute(going_up, 'z', up)  33.2 us
    unnamed x33, local copies, waits for them, and re-layouts  31.6 us
    all_to_all x4, starting transfers between devices, body(): lax.all_to_all(partial, 'narrow', split_axis=0, concat_axis=0, tiled=True)  26.2 us
    ppermute x16, waiting for transfers between devices, body(): going_up = lax.ppermute(going_up, 'z', up)  23.9 us
    ppermute x4, starting transfers between devices, body(): received = lax.ppermute(theirs, 'core', [(0, 1), (1, 0)])  21 us
    reshape x8, local copies, waits for them, and re-layouts, body(): products.astype(jnp.bfloat16)  17.2 us
  transfers between devices with their start and end apart: 39, of which 13 were waited for; matrix products, arithmetic and copies ran while one was open for 21% of the time, Pallas kernels for 0%

profile of v7, /device:TPU:1, one launch (start us, length us, event | category | flops | bytes accessed | tf_op | source)
XLA Modules:
  0.0 340.3 jit_solution(15752557103335388175)
XLA Ops:
  0.0 4.5 %collective-permute-start = (bf16[8,32,640]{2,1,0:T(8,128)(2,1)}, bf16[8,32,640]{2,1,0:T(8,128)(2,1)S(1)}, u32[]{:S(2)}, u32[]{:S(2)}) collective-permute-start(bf16[8,32,640]{2,1,0:T(8,128)(2,1)} %param.6), channel_id=1, source_target_pairs={{0,32},{32,64},{64,96},{96,128},{128,160},{160,192},{192,224},{224... | collective-permute-start | bytes 983048 | tf_op jit(solution)/shard_map/ppermute | solution.py:30
  4.5 16.8 %collective-permute-start.1 = (bf16[8,32,640]{2,1,0:T(8,128)(2,1)}, bf16[8,32,640]{2,1,0:T(8,128)(2,1)S(1)}, u32[]{:S(2)}, u32[]{:S(2)}) collective-permute-start(bf16[8,32,640]{2,1,0:T(8,128)(2,1)} %param.6), channel_id=1, source_target_pairs={{0,992},{32,0},{64,32},{96,64},{128,96},{160,128},{192,160},{224,1... | collective-permute-start | bytes 983048 | tf_op jit(solution)/shard_map/ppermute | solution.py:33
  27.3 1.9 collective-permute-start.2
  29.2 4.6 %collective-permute-start.3 = (bf16[8,32,640]{2,1,0:T(8,128)(2,1)S(1)}, bf16[8,32,640]{2,1,0:T(8,128)(2,1)S(1)}, u32[]{:S(2)}, u32[]{:S(2)}) collective-permute-start(bf16[8,32,640]{2,1,0:T(8,128)(2,1)S(1)} %collective-permute-done.1), channel_id=1, source_target_pairs={{0,992},{32,0},{64,32},{96,64},{128,96},{160,128},{192,160},{224,1... | collective-permute-start | bytes 983048 | tf_op jit(solution)/shard_map/ppermute | solution.py:33
  33.9 4.8 %collective-permute-done.2 = bf16[8,32,640]{2,1,0:T(8,128)(2,1)S(1)} collective-permute-done((bf16[8,32,640]{2,1,0:T(8,128)(2,1)S(1)}, bf16[8,32,640]{2,1,0:T(8,128)(2,1)S(1)}, u32[]{:S(2)}, u32[]{:S(2)}) %collective-permute-start.2) | collective-permute-done | bytes 327712 | tf_op jit(solution)/shard_map/ppermute | solution.py:30
  40.6 4.6 %collective-permute-start.5 = (bf16[8,32,640]{2,1,0:T(8,128)(2,1)S(1)}, bf16[8,32,640]{2,1,0:T(8,128)(2,1)S(1)}, u32[]{:S(2)}, u32[]{:S(2)}) collective-permute-start(bf16[8,32,640]{2,1,0:T(8,128)(2,1)S(1)} %collective-permute-done.3), channel_id=1, source_target_pairs={{0,992},{32,0},{64,32},{96,64},{128,96},{160,128},{192,160},{224,1... | collective-permute-start | bytes 983048 | tf_op jit(solution)/shard_map/ppermute | solution.py:33
  45.3 3.9 %collective-permute-done.4 = bf16[8,32,640]{2,1,0:T(8,128)(2,1)S(1)} collective-permute-done((bf16[8,32,640]{2,1,0:T(8,128)(2,1)S(1)}, bf16[8,32,640]{2,1,0:T(8,128)(2,1)S(1)}, u32[]{:S(2)}, u32[]{:S(2)}) %collective-permute-start.4) | collective-permute-done | bytes 327712 | tf_op jit(solution)/shard_map/ppermute | solution.py:30
  51.2 4.6 %collective-permute-start.8 = (bf16[8,32,640]{2,1,0:T(8,128)(2,1)S(1)}, bf16[8,32,640]{2,1,0:T(8,128)(2,1)}, u32[]{:S(2)}, u32[]{:S(2)}) collective-permute-start(bf16[8,32,640]{2,1,0:T(8,128)(2,1)S(1)} %collective-permute-done.5), channel_id=1, source_target_pairs={{0,992},{32,0},{64,32},{96,64},{128,96},{160,128},{192,160},{224,1... | collective-permute-start | bytes 983048 | tf_op jit(solution)/shard_map/ppermute | solution.py:33
  55.8 3.2 collective-permute-done.6
  60.2 5.4 %collective-permute-start.7 = (bf16[8,32,640]{2,1,0:T(8,128)(2,1)S(1)}, bf16[8,32,640]{2,1,0:T(8,128)(2,1)S(1)}, u32[]{:S(2)}, u32[]{:S(2)}) collective-permute-start(bf16[8,32,640]{2,1,0:T(8,128)(2,1)S(1)} %get-tuple-element.18), channel_id=1, source_target_pairs={{0,16},{16,0},{1,17},{17,1},{2,18},{18,2},{3,19},{19,3},{4,20},{20... | collective-permute-start | bytes 983048 | tf_op jit(solution)/shard_map/ppermute | solution.py:44
  65.6 1.9 collective-permute-start.9
  69.3 4.6 %collective-permute-start.10 = (bf16[8,32,640]{2,1,0:T(8,128)(2,1)}, bf16[8,32,640]{2,1,0:T(8,128)(2,1)}, u32[]{:S(2)}, u32[]{:S(2)}) collective-permute-start(bf16[8,32,640]{2,1,0:T(8,128)(2,1)} %collective-permute-done.8), channel_id=1, source_target_pairs={{0,992},{32,0},{64,32},{96,64},{128,96},{160,128},{192,160},{224,1... | collective-permute-start | bytes 983048 | tf_op jit(solution)/shard_map/ppermute | solution.py:33
  75.3 2.1 copy.39
  77.4 6.8 %all-to-all-start = ((bf16[16,2,2,8,1024]{4,1,3,2,0:T(2,128)(2,1)}), bf16[16,2,2,8,1024]{4,1,3,2,0:T(2,128)(2,1)S(1)}, u32[]{:S(2)}, u32[]{:S(2)}) async-start(bf16[16,2,2,8,1024]{4,1,3,2,0:T(2,128)(2,1)} %copy.39), calls=%async_computation | async-start | bytes 2097152 | tf_op jit(solution)/shard_map/all_to_all | solution.py:50
  84.2 1.9 collective-permute-start.11
  87.9 4.6 %collective-permute-start.12 = (bf16[8,32,640]{2,1,0:T(8,128)(2,1)}, bf16[8,32,640]{2,1,0:T(8,128)(2,1)S(1)}, u32[]{:S(2)}, u32[]{:S(2)}) collective-permute-start(bf16[8,32,640]{2,1,0:T(8,128)(2,1)} %collective-permute-done.10), channel_id=1, source_target_pairs={{0,992},{32,0},{64,32},{96,64},{128,96},{160,128},{192,160},{224,1... | collective-permute-start | bytes 983048 | tf_op jit(solution)/shard_map/ppermute | solution.py:33
  98.7 5.2 %collective-permute-start.14 = (bf16[8,32,640]{2,1,0:T(8,128)(2,1)S(1)}, bf16[8,32,640]{2,1,0:T(8,128)(2,1)S(1)}, u32[]{:S(2)}, u32[]{:S(2)}) collective-permute-start(bf16[8,32,640]{2,1,0:T(8,128)(2,1)S(1)} %collective-permute-done.12), channel_id=1, source_target_pairs={{0,992},{32,0},{64,32},{96,64},{128,96},{160,128},{192,160},{224,1... | collective-permute-start | bytes 983048 | tf_op jit(solution)/shard_map/ppermute | solution.py:33
  104.6 2.0 collective-permute-done.13
  109.2 5.0 %collective-permute-start.17 = (bf16[8,32,640]{2,1,0:T(8,128)(2,1)S(1)}, bf16[8,32,640]{2,1,0:T(8,128)(2,1)S(1)}, u32[]{:S(2)}, u32[]{:S(2)}) collective-permute-start(bf16[8,32,640]{2,1,0:T(8,128)(2,1)S(1)} %collective-permute-done.14), channel_id=1, source_target_pairs={{0,992},{32,0},{64,32},{96,64},{128,96},{160,128},{192,160},{224,1... | collective-permute-start | bytes 983048 | tf_op jit(solution)/shard_map/ppermute | solution.py:33
  118.2 5.3 %collective-permute-start.16 = (bf16[8,32,640]{2,1,0:T(8,128)(2,1)S(1)}, bf16[8,32,640]{2,1,0:T(8,128)(2,1)S(1)}, u32[]{:S(2)}, u32[]{:S(2)}) collective-permute-start(bf16[8,32,640]{2,1,0:T(8,128)(2,1)S(1)} %select_bitcast_fusion.2), channel_id=1, source_target_pairs={{0,16},{16,0},{1,17},{17,1},{2,18},{18,2},{3,19},{19,3},{4,20},{20... | collective-permute-start | bytes 983048 | tf_op jit(solution)/shard_map/ppermute | solution.py:44
  123.5 1.9 collective-permute-start.18
  127.2 4.6 %collective-permute-start.19 = (bf16[8,32,640]{2,1,0:T(8,128)(2,1)S(1)}, bf16[8,32,640]{2,1,0:T(8,128)(2,1)}, u32[]{:S(2)}, u32[]{:S(2)}) collective-permute-start(bf16[8,32,640]{2,1,0:T(8,128)(2,1)S(1)} %collective-permute-done.17), channel_id=1, source_target_pairs={{0,992},{32,0},{64,32},{96,64},{128,96},{160,128},{192,160},{224,1... | collective-permute-start | bytes 983048 | tf_op jit(solution)/shard_map/ppermute | solution.py:33
  131.8 2.0 fusion.1
  133.8 2.2 collective-permute-done.18
  139.6 4.6 %collective-permute-start.21 = (bf16[8,32,640]{2,1,0:T(8,128)(2,1)}, bf16[8,32,640]{2,1,0:T(8,128)(2,1)}, u32[]{:S(2)}, u32[]{:S(2)}) collective-permute-start(bf16[8,32,640]{2,1,0:T(8,128)(2,1)} %collective-permute-done.19), channel_id=1, source_target_pairs={{0,992},{32,0},{64,32},{96,64},{128,96},{160,128},{192,160},{224,1... | collective-permute-start | bytes 983048 | tf_op jit(solution)/shard_map/ppermute | solution.py:33
  147.4 2.1 copy.42
  153.2 4.6 %collective-permute-start.23 = (bf16[8,32,640]{2,1,0:T(8,128)(2,1)}, bf16[8,32,640]{2,1,0:T(8,128)(2,1)S(1)}, u32[]{:S(2)}, u32[]{:S(2)}) collective-permute-start(bf16[8,32,640]{2,1,0:T(8,128)(2,1)} %collective-permute-done.21), channel_id=1, source_target_pairs={{0,992},{32,0},{64,32},{96,64},{128,96},{160,128},{192,160},{224,1... | collective-permute-start | bytes 983048 | tf_op jit(solution)/shard_map/ppermute | solution.py:33
  163.4 5.2 %collective-permute-start.26 = (bf16[8,32,640]{2,1,0:T(8,128)(2,1)S(1)}, bf16[8,32,640]{2,1,0:T(8,128)(2,1)}, u32[]{:S(2)}, u32[]{:S(2)}) collective-permute-start(bf16[8,32,640]{2,1,0:T(8,128)(2,1)S(1)} %collective-permute-done.23), channel_id=1, source_target_pairs={{0,992},{32,0},{64,32},{96,64},{128,96},{160,128},{192,160},{224,1... | collective-permute-start | bytes 983048 | tf_op jit(solution)/shard_map/ppermute | solution.py:33
  172.5 5.1 %collective-permute-start.25 = (bf16[8,32,640]{2,1,0:T(8,128)(2,1)S(1)}, bf16[8,32,640]{2,1,0:T(8,128)(2,1)S(1)}, u32[]{:S(2)}, u32[]{:S(2)}) collective-permute-start(bf16[8,32,640]{2,1,0:T(8,128)(2,1)S(1)} %select_bitcast_fusion.1), channel_id=1, source_target_pairs={{0,16},{16,0},{1,17},{17,1},{2,18},{18,2},{3,19},{19,3},{4,20},{20... | collective-permute-start | bytes 983048 | tf_op jit(solution)/shard_map/ppermute | solution.py:44
  177.6 1.9 collective-permute-start.27
  182.3 4.6 %collective-permute-start.28 = (bf16[8,32,640]{2,1,0:T(8,128)(2,1)}, bf16[8,32,640]{2,1,0:T(8,128)(2,1)}, u32[]{:S(2)}, u32[]{:S(2)}) collective-permute-start(bf16[8,32,640]{2,1,0:T(8,128)(2,1)} %collective-permute-done.26), channel_id=1, source_target_pairs={{0,992},{32,0},{64,32},{96,64},{128,96},{160,128},{192,160},{224,1... | collective-permute-start | bytes 983048 | tf_op jit(solution)/shard_map/ppermute | solution.py:33
  186.9 2.0 fusion.2
  192.0 6.1 %all-to-all-start.1 = ((bf16[16,2,2,8,1024]{4,1,3,2,0:T(2,128)(2,1)}), bf16[16,2,2,8,1024]{4,1,3,2,0:T(2,128)(2,1)S(1)}, u32[]{:S(2)}, u32[]{:S(2)}) async-start(bf16[16,2,2,8,1024]{4,1,3,2,0:T(2,128)(2,1)} %copy.42), calls=%async_computation.1 | async-start | bytes 2097152 | tf_op jit(solution)/shard_map/all_to_all | solution.py:50
  199.8 4.6 %collective-permute-start.30 = (bf16[8,32,640]{2,1,0:T(8,128)(2,1)}, bf16[8,32,640]{2,1,0:T(8,128)(2,1)}, u32[]{:S(2)}, u32[]{:S(2)}) collective-permute-start(bf16[8,32,640]{2,1,0:T(8,128)(2,1)} %collective-permute-done.28), channel_id=1, source_target_pairs={{0,992},{32,0},{64,32},{96,64},{128,96},{160,128},{192,160},{224,1... | collective-permute-start | bytes 983048 | tf_op jit(solution)/shard_map/ppermute | solution.py:33
  206.2 2.3 reshape.26
  208.4 3.3 copy.45
  211.7 1.9 collective-permute-start.31
  215.4 4.6 %collective-permute-start.32 = (bf16[8,32,640]{2,1,0:T(8,128)(2,1)}, bf16[8,32,640]{2,1,0:T(8,128)(2,1)}, u32[]{:S(2)}, u32[]{:S(2)}) collective-permute-start(bf16[8,32,640]{2,1,0:T(8,128)(2,1)} %collective-permute-done.30), channel_id=1, source_target_pairs={{0,992},{32,0},{64,32},{96,64},{128,96},{160,128},{192,160},{224,1... | collective-permute-start | bytes 983048 | tf_op jit(solution)/shard_map/ppermute | solution.py:33
  226.3 6.4 %all-to-all-start.2 = ((bf16[16,2,2,8,1024]{4,1,3,2,0:T(2,128)(2,1)}), bf16[16,2,2,8,1024]{4,1,3,2,0:T(2,128)(2,1)}, u32[]{:S(2)}, u32[]{:S(2)}) async-start(bf16[16,2,2,8,1024]{4,1,3,2,0:T(2,128)(2,1)} %copy.45), calls=%async_computation.2 | async-start | bytes 2097152 | tf_op jit(solution)/shard_map/all_to_all | solution.py:50
  237.3 5.2 %collective-permute-start.34 = (bf16[8,32,640]{2,1,0:T(8,128)(2,1)S(1)}, bf16[8,32,640]{2,1,0:T(8,128)(2,1)S(1)}, u32[]{:S(2)}, u32[]{:S(2)}) collective-permute-start(bf16[8,32,640]{2,1,0:T(8,128)(2,1)S(1)} %select_bitcast_fusion), channel_id=1, source_target_pairs={{0,16},{16,0},{1,17},{17,1},{2,18},{18,2},{3,19},{19,3},{4,20},{20... | collective-permute-start | bytes 983048 | tf_op jit(solution)/shard_map/ppermute | solution.py:44
  243.6 2.0 fusion.3
  245.6 2.2 reshape.27
  247.8 3.3 copy.48
  251.1 6.9 %all-to-all-start.3 = ((bf16[16,2,2,8,1024]{4,1,3,2,0:T(2,128)(2,1)}), bf16[16,2,2,8,1024]{4,1,3,2,0:T(2,128)(2,1)}, u32[]{:S(2)}, u32[]{:S(2)}) async-start(bf16[16,2,2,8,1024]{4,1,3,2,0:T(2,128)(2,1)} %copy.48), calls=%async_computation.3 | async-start | bytes 2097152 | tf_op jit(solution)/shard_map/all_to_all | solution.py:50
  260.3 2.2 reduce_sum.50
  262.6 11.8 %all-to-all-done.3 = bf16[16,2,2,8,1024]{4,1,3,2,0:T(2,128)(2,1)} async-done(((bf16[16,2,2,8,1024]{4,1,3,2,0:T(2,128)(2,1)}), bf16[16,2,2,8,1024]{4,1,3,2,0:T(2,128)(2,1)}, u32[]{:S(2)}, u32[]{:S(2)}) %all-to-all-start.3) | async-done | bytes 1048608 | tf_op jit(solution)/shard_map/all_to_all | solution.py:50
  274.5 2.2 reduce_sum.51
  281.3 58.2 %all_to_all.25 = bf16[2,64,1024]{2,0,1:T(2,128)(2,1)S(1)} all-to-all(bf16[2,64,1024]{2,0,1:T(2,128)(2,1)S(1)} %bitcast.156), channel_id=1, replica_groups=mesh['z'=32,'core'=2,'narrow'=16] {'z','core'}, dimensions={1} | all-to-all | bytes 524288 | tf_op jit(solution)/shard_map/all_to_all | solution.py:57
  (103 shorter events, 78.4 us)
Async XLA Ops:
  0.0 73.8 %copy-start = (bf16[1024,640]{1,0:T(8,128)(2,1)S(1)}, bf16[1024,640]{1,0:T(8,128)(2,1)}, u32[]{:S(2)}) copy-start(bf16[1024,640]{1,0:T(8,128)(2,1)} %param.7) | copy-start | bytes 3932164
  0.0 27.3 %collective-permute-start = (bf16[8,32,640]{2,1,0:T(8,128)(2,1)}, bf16[8,32,640]{2,1,0:T(8,128)(2,1)S(1)}, u32[]{:S(2)}, u32[]{:S(2)}) collective-permute-start(bf16[8,32,640]{2,1,0:T(8,128)(2,1)} %param.6), channel_id=1, source_target_pairs={{0,32},{32,64},{64,96},{96,128},{128,160},{160,192},{192,224},{224... | collective-permute-start | bytes 983048 | tf_op jit(solution)/shard_map/ppermute | solution.py:30
  4.5 24.7 %collective-permute-start.1 = (bf16[8,32,640]{2,1,0:T(8,128)(2,1)}, bf16[8,32,640]{2,1,0:T(8,128)(2,1)S(1)}, u32[]{:S(2)}, u32[]{:S(2)}) collective-permute-start(bf16[8,32,640]{2,1,0:T(8,128)(2,1)} %param.6), channel_id=1, source_target_pairs={{0,992},{32,0},{64,32},{96,64},{128,96},{160,128},{192,160},{224,1... | collective-permute-start | bytes 983048 | tf_op jit(solution)/shard_map/ppermute | solution.py:33
  27.3 11.4 %collective-permute-start.2 = (bf16[8,32,640]{2,1,0:T(8,128)(2,1)S(1)}, bf16[8,32,640]{2,1,0:T(8,128)(2,1)S(1)}, u32[]{:S(2)}, u32[]{:S(2)}) collective-permute-start(bf16[8,32,640]{2,1,0:T(8,128)(2,1)S(1)} %collective-permute-done), channel_id=1, source_target_pairs={{0,32},{32,64},{64,96},{96,128},{128,160},{160,192},{192,224},{224... | collective-permute-start | bytes 983048 | tf_op jit(solution)/shard_map/ppermute | solution.py:30
  29.2 11.4 %collective-permute-start.3 = (bf16[8,32,640]{2,1,0:T(8,128)(2,1)S(1)}, bf16[8,32,640]{2,1,0:T(8,128)(2,1)S(1)}, u32[]{:S(2)}, u32[]{:S(2)}) collective-permute-start(bf16[8,32,640]{2,1,0:T(8,128)(2,1)S(1)} %collective-permute-done.1), channel_id=1, source_target_pairs={{0,992},{32,0},{64,32},{96,64},{128,96},{160,128},{192,160},{224,1... | collective-permute-start | bytes 983048 | tf_op jit(solution)/shard_map/ppermute | solution.py:33
  38.7 10.6 %collective-permute-start.4 = (bf16[8,32,640]{2,1,0:T(8,128)(2,1)S(1)}, bf16[8,32,640]{2,1,0:T(8,128)(2,1)S(1)}, u32[]{:S(2)}, u32[]{:S(2)}) collective-permute-start(bf16[8,32,640]{2,1,0:T(8,128)(2,1)S(1)} %collective-permute-done.2), channel_id=1, source_target_pairs={{0,32},{32,64},{64,96},{96,128},{128,160},{160,192},{192,224},{224... | collective-permute-start | bytes 983048 | tf_op jit(solution)/shard_map/ppermute | solution.py:30
  40.6 10.5 %collective-permute-start.5 = (bf16[8,32,640]{2,1,0:T(8,128)(2,1)S(1)}, bf16[8,32,640]{2,1,0:T(8,128)(2,1)S(1)}, u32[]{:S(2)}, u32[]{:S(2)}) collective-permute-start(bf16[8,32,640]{2,1,0:T(8,128)(2,1)S(1)} %collective-permute-done.3), channel_id=1, source_target_pairs={{0,992},{32,0},{64,32},{96,64},{128,96},{160,128},{192,160},{224,1... | collective-permute-start | bytes 983048 | tf_op jit(solution)/shard_map/ppermute | solution.py:33
  49.2 9.8 %collective-permute-start.6 = (bf16[8,32,640]{2,1,0:T(8,128)(2,1)S(1)}, bf16[8,32,640]{2,1,0:T(8,128)(2,1)}, u32[]{:S(2)}, u32[]{:S(2)}) collective-permute-start(bf16[8,32,640]{2,1,0:T(8,128)(2,1)S(1)} %collective-permute-done.4), channel_id=1, source_target_pairs={{0,32},{32,64},{64,96},{96,128},{128,160},{160,192},{192,224},{224... | collective-permute-start | bytes 983048 | tf_op jit(solution)/shard_map/ppermute | solution.py:30
  51.2 16.4 %collective-permute-start.8 = (bf16[8,32,640]{2,1,0:T(8,128)(2,1)S(1)}, bf16[8,32,640]{2,1,0:T(8,128)(2,1)}, u32[]{:S(2)}, u32[]{:S(2)}) collective-permute-start(bf16[8,32,640]{2,1,0:T(8,128)(2,1)S(1)} %collective-permute-done.5), channel_id=1, source_target_pairs={{0,992},{32,0},{64,32},{96,64},{128,96},{160,128},{192,160},{224,1... | collective-permute-start | bytes 983048 | tf_op jit(solution)/shard_map/ppermute | solution.py:33
  60.2 13.7 %collective-permute-start.7 = (bf16[8,32,640]{2,1,0:T(8,128)(2,1)S(1)}, bf16[8,32,640]{2,1,0:T(8,128)(2,1)S(1)}, u32[]{:S(2)}, u32[]{:S(2)}) collective-permute-start(bf16[8,32,640]{2,1,0:T(8,128)(2,1)S(1)} %get-tuple-element.18), channel_id=1, source_target_pairs={{0,16},{16,0},{1,17},{17,1},{2,18},{18,2},{3,19},{19,3},{4,20},{20... | collective-permute-start | bytes 983048 | tf_op jit(solution)/shard_map/ppermute | solution.py:44
  65.6 18.6 %collective-permute-start.9 = (bf16[8,32,640]{2,1,0:T(8,128)(2,1)}, bf16[8,32,640]{2,1,0:T(8,128)(2,1)}, u32[]{:S(2)}, u32[]{:S(2)}) collective-permute-start(bf16[8,32,640]{2,1,0:T(8,128)(2,1)} %collective-permute-done.6), channel_id=1, source_target_pairs={{0,32},{32,64},{64,96},{96,128},{128,160},{160,192},{192,224},{224... | collective-permute-start | bytes 983048 | tf_op jit(solution)/shard_map/ppermute | solution.py:30
  69.3 18.6 %collective-permute-start.10 = (bf16[8,32,640]{2,1,0:T(8,128)(2,1)}, bf16[8,32,640]{2,1,0:T(8,128)(2,1)}, u32[]{:S(2)}, u32[]{:S(2)}) collective-permute-start(bf16[8,32,640]{2,1,0:T(8,128)(2,1)} %collective-permute-done.8), channel_id=1, source_target_pairs={{0,992},{32,0},{64,32},{96,64},{128,96},{160,128},{192,160},{224,1... | collective-permute-start | bytes 983048 | tf_op jit(solution)/shard_map/ppermute | solution.py:33
  77.4 114.6 %all-to-all-start = ((bf16[16,2,2,8,1024]{4,1,3,2,0:T(2,128)(2,1)}), bf16[16,2,2,8,1024]{4,1,3,2,0:T(2,128)(2,1)S(1)}, u32[]{:S(2)}, u32[]{:S(2)}) async-start(bf16[16,2,2,8,1024]{4,1,3,2,0:T(2,128)(2,1)} %copy.39), calls=%async_computation | async-start | bytes 2097152 | tf_op jit(solution)/shard_map/all_to_all | solution.py:50
  84.2 11.7 %collective-permute-start.11 = (bf16[8,32,640]{2,1,0:T(8,128)(2,1)}, bf16[8,32,640]{2,1,0:T(8,128)(2,1)S(1)}, u32[]{:S(2)}, u32[]{:S(2)}) collective-permute-start(bf16[8,32,640]{2,1,0:T(8,128)(2,1)} %collective-permute-done.9), channel_id=1, source_target_pairs={{0,32},{32,64},{64,96},{96,128},{128,160},{160,192},{192,224},{224... | collective-permute-start | bytes 983048 | tf_op jit(solution)/shard_map/ppermute | solution.py:30
  87.9 10.8 %collective-permute-start.12 = (bf16[8,32,640]{2,1,0:T(8,128)(2,1)}, bf16[8,32,640]{2,1,0:T(8,128)(2,1)S(1)}, u32[]{:S(2)}, u32[]{:S(2)}) collective-permute-start(bf16[8,32,640]{2,1,0:T(8,128)(2,1)} %collective-permute-done.10), channel_id=1, source_target_pairs={{0,992},{32,0},{64,32},{96,64},{128,96},{160,128},{192,160},{224,1... | collective-permute-start | bytes 983048 | tf_op jit(solution)/shard_map/ppermute | solution.py:33
  95.9 10.7 %collective-permute-start.13 = (bf16[8,32,640]{2,1,0:T(8,128)(2,1)S(1)}, bf16[8,32,640]{2,1,0:T(8,128)(2,1)S(1)}, u32[]{:S(2)}, u32[]{:S(2)}) collective-permute-start(bf16[8,32,640]{2,1,0:T(8,128)(2,1)S(1)} %collective-permute-done.11), channel_id=1, source_target_pairs={{0,32},{32,64},{64,96},{96,128},{128,160},{160,192},{192,224},{224... | collective-permute-start | bytes 983048 | tf_op jit(solution)/shard_map/ppermute | solution.py:30
  98.7 10.6 %collective-permute-start.14 = (bf16[8,32,640]{2,1,0:T(8,128)(2,1)S(1)}, bf16[8,32,640]{2,1,0:T(8,128)(2,1)S(1)}, u32[]{:S(2)}, u32[]{:S(2)}) collective-permute-start(bf16[8,32,640]{2,1,0:T(8,128)(2,1)S(1)} %collective-permute-done.12), channel_id=1, source_target_pairs={{0,992},{32,0},{64,32},{96,64},{128,96},{160,128},{192,160},{224,1... | collective-permute-start | bytes 983048 | tf_op jit(solution)/shard_map/ppermute | solution.py:33
  106.6 9.8 %collective-permute-start.15 = (bf16[8,32,640]{2,1,0:T(8,128)(2,1)S(1)}, bf16[8,32,640]{2,1,0:T(8,128)(2,1)S(1)}, u32[]{:S(2)}, u32[]{:S(2)}) collective-permute-start(bf16[8,32,640]{2,1,0:T(8,128)(2,1)S(1)} %collective-permute-done.13), channel_id=1, source_target_pairs={{0,32},{32,64},{64,96},{96,128},{128,160},{160,192},{192,224},{224... | collective-permute-start | bytes 983048 | tf_op jit(solution)/shard_map/ppermute | solution.py:30
  109.2 16.2 %collective-permute-start.17 = (bf16[8,32,640]{2,1,0:T(8,128)(2,1)S(1)}, bf16[8,32,640]{2,1,0:T(8,128)(2,1)S(1)}, u32[]{:S(2)}, u32[]{:S(2)}) collective-permute-start(bf16[8,32,640]{2,1,0:T(8,128)(2,1)S(1)} %collective-permute-done.14), channel_id=1, source_target_pairs={{0,992},{32,0},{64,32},{96,64},{128,96},{160,128},{192,160},{224,1... | collective-permute-start | bytes 983048 | tf_op jit(solution)/shard_map/ppermute | solution.py:33
  118.2 13.6 %collective-permute-start.16 = (bf16[8,32,640]{2,1,0:T(8,128)(2,1)S(1)}, bf16[8,32,640]{2,1,0:T(8,128)(2,1)S(1)}, u32[]{:S(2)}, u32[]{:S(2)}) collective-permute-start(bf16[8,32,640]{2,1,0:T(8,128)(2,1)S(1)} %select_bitcast_fusion.2), channel_id=1, source_target_pairs={{0,16},{16,0},{1,17},{17,1},{2,18},{18,2},{3,19},{19,3},{4,20},{20... | collective-permute-start | bytes 983048 | tf_op jit(solution)/shard_map/ppermute | solution.py:44
  123.5 12.5 %collective-permute-start.18 = (bf16[8,32,640]{2,1,0:T(8,128)(2,1)S(1)}, bf16[8,32,640]{2,1,0:T(8,128)(2,1)}, u32[]{:S(2)}, u32[]{:S(2)}) collective-permute-start(bf16[8,32,640]{2,1,0:T(8,128)(2,1)S(1)} %collective-permute-done.15), channel_id=1, source_target_pairs={{0,32},{32,64},{64,96},{96,128},{128,160},{160,192},{192,224},{224... | collective-permute-start | bytes 983048 | tf_op jit(solution)/shard_map/ppermute | solution.py:30
  127.2 12.4 %collective-permute-start.19 = (bf16[8,32,640]{2,1,0:T(8,128)(2,1)S(1)}, bf16[8,32,640]{2,1,0:T(8,128)(2,1)}, u32[]{:S(2)}, u32[]{:S(2)}) collective-permute-start(bf16[8,32,640]{2,1,0:T(8,128)(2,1)S(1)} %collective-permute-done.17), channel_id=1, source_target_pairs={{0,992},{32,0},{64,32},{96,64},{128,96},{160,128},{192,160},{224,1... | collective-permute-start | bytes 983048 | tf_op jit(solution)/shard_map/ppermute | solution.py:33
  136.0 13.6 %collective-permute-start.20 = (bf16[8,32,640]{2,1,0:T(8,128)(2,1)}, bf16[8,32,640]{2,1,0:T(8,128)(2,1)}, u32[]{:S(2)}, u32[]{:S(2)}) collective-permute-start(bf16[8,32,640]{2,1,0:T(8,128)(2,1)} %collective-permute-done.18), channel_id=1, source_target_pairs={{0,32},{32,64},{64,96},{96,128},{128,160},{160,192},{192,224},{224... | collective-permute-start | bytes 983048 | tf_op jit(solution)/shard_map/ppermute | solution.py:30
  139.6 13.5 %collective-permute-start.21 = (bf16[8,32,640]{2,1,0:T(8,128)(2,1)}, bf16[8,32,640]{2,1,0:T(8,128)(2,1)}, u32[]{:S(2)}, u32[]{:S(2)}) collective-permute-start(bf16[8,32,640]{2,1,0:T(8,128)(2,1)} %collective-permute-done.19), channel_id=1, source_target_pairs={{0,992},{32,0},{64,32},{96,64},{128,96},{160,128},{192,160},{224,1... | collective-permute-start | bytes 983048 | tf_op jit(solution)/shard_map/ppermute | solution.py:33
  149.5 11.1 %collective-permute-start.22 = (bf16[8,32,640]{2,1,0:T(8,128)(2,1)}, bf16[8,32,640]{2,1,0:T(8,128)(2,1)S(1)}, u32[]{:S(2)}, u32[]{:S(2)}) collective-permute-start(bf16[8,32,640]{2,1,0:T(8,128)(2,1)} %collective-permute-done.20), channel_id=1, source_target_pairs={{0,32},{32,64},{64,96},{96,128},{128,160},{160,192},{192,224},{224... | collective-permute-start | bytes 983048 | tf_op jit(solution)/shard_map/ppermute | solution.py:30
  153.2 10.2 %collective-permute-start.23 = (bf16[8,32,640]{2,1,0:T(8,128)(2,1)}, bf16[8,32,640]{2,1,0:T(8,128)(2,1)S(1)}, u32[]{:S(2)}, u32[]{:S(2)}) collective-permute-start(bf16[8,32,640]{2,1,0:T(8,128)(2,1)} %collective-permute-done.21), channel_id=1, source_target_pairs={{0,992},{32,0},{64,32},{96,64},{128,96},{160,128},{192,160},{224,1... | collective-permute-start | bytes 983048 | tf_op jit(solution)/shard_map/ppermute | solution.py:33
  160.7 10.1 %collective-permute-start.24 = (bf16[8,32,640]{2,1,0:T(8,128)(2,1)S(1)}, bf16[8,32,640]{2,1,0:T(8,128)(2,1)S(1)}, u32[]{:S(2)}, u32[]{:S(2)}) collective-permute-start(bf16[8,32,640]{2,1,0:T(8,128)(2,1)S(1)} %collective-permute-done.22), channel_id=1, source_target_pairs={{0,32},{32,64},{64,96},{96,128},{128,160},{160,192},{192,224},{224... | collective-permute-start | bytes 983048 | tf_op jit(solution)/shard_map/ppermute | solution.py:30
  163.4 16.1 %collective-permute-start.26 = (bf16[8,32,640]{2,1,0:T(8,128)(2,1)S(1)}, bf16[8,32,640]{2,1,0:T(8,128)(2,1)}, u32[]{:S(2)}, u32[]{:S(2)}) collective-permute-start(bf16[8,32,640]{2,1,0:T(8,128)(2,1)S(1)} %collective-permute-done.23), channel_id=1, source_target_pairs={{0,992},{32,0},{64,32},{96,64},{128,96},{160,128},{192,160},{224,1... | collective-permute-start | bytes 983048 | tf_op jit(solution)/shard_map/ppermute | solution.py:33
  172.5 14.3 %collective-permute-start.25 = (bf16[8,32,640]{2,1,0:T(8,128)(2,1)S(1)}, bf16[8,32,640]{2,1,0:T(8,128)(2,1)S(1)}, u32[]{:S(2)}, u32[]{:S(2)}) collective-permute-start(bf16[8,32,640]{2,1,0:T(8,128)(2,1)S(1)} %select_bitcast_fusion.1), channel_id=1, source_target_pairs={{0,16},{16,0},{1,17},{17,1},{2,18},{18,2},{3,19},{19,3},{4,20},{20... | collective-permute-start | bytes 983048 | tf_op jit(solution)/shard_map/ppermute | solution.py:44
  177.6 12.5 %collective-permute-start.27 = (bf16[8,32,640]{2,1,0:T(8,128)(2,1)S(1)}, bf16[8,32,640]{2,1,0:T(8,128)(2,1)}, u32[]{:S(2)}, u32[]{:S(2)}) collective-permute-start(bf16[8,32,640]{2,1,0:T(8,128)(2,1)S(1)} %collective-permute-done.24), channel_id=1, source_target_pairs={{0,32},{32,64},{64,96},{96,128},{128,160},{160,192},{192,224},{224... | collective-permute-start | bytes 983048 | tf_op jit(solution)/shard_map/ppermute | solution.py:30
  182.3 17.5 %collective-permute-start.28 = (bf16[8,32,640]{2,1,0:T(8,128)(2,1)}, bf16[8,32,640]{2,1,0:T(8,128)(2,1)}, u32[]{:S(2)}, u32[]{:S(2)}) collective-permute-start(bf16[8,32,640]{2,1,0:T(8,128)(2,1)} %collective-permute-done.26), channel_id=1, source_target_pairs={{0,992},{32,0},{64,32},{96,64},{128,96},{160,128},{192,160},{224,1... | collective-permute-start | bytes 983048 | tf_op jit(solution)/shard_map/ppermute | solution.py:33
  190.1 21.7 %collective-permute-start.29 = (bf16[8,32,640]{2,1,0:T(8,128)(2,1)}, bf16[8,32,640]{2,1,0:T(8,128)(2,1)}, u32[]{:S(2)}, u32[]{:S(2)}) collective-permute-start(bf16[8,32,640]{2,1,0:T(8,128)(2,1)} %collective-permute-done.27), channel_id=1, source_target_pairs={{0,32},{32,64},{64,96},{96,128},{128,160},{160,192},{192,224},{224... | collective-permute-start | bytes 983048 | tf_op jit(solution)/shard_map/ppermute | solution.py:30
  192.0 34.4 %all-to-all-start.1 = ((bf16[16,2,2,8,1024]{4,1,3,2,0:T(2,128)(2,1)}), bf16[16,2,2,8,1024]{4,1,3,2,0:T(2,128)(2,1)S(1)}, u32[]{:S(2)}, u32[]{:S(2)}) async-start(bf16[16,2,2,8,1024]{4,1,3,2,0:T(2,128)(2,1)} %copy.42), calls=%async_computation.1 | async-start | bytes 2097152 | tf_op jit(solution)/shard_map/all_to_all | solution.py:50
  199.8 15.6 %collective-permute-start.30 = (bf16[8,32,640]{2,1,0:T(8,128)(2,1)}, bf16[8,32,640]{2,1,0:T(8,128)(2,1)}, u32[]{:S(2)}, u32[]{:S(2)}) collective-permute-start(bf16[8,32,640]{2,1,0:T(8,128)(2,1)} %collective-permute-done.28), channel_id=1, source_target_pairs={{0,992},{32,0},{64,32},{96,64},{128,96},{160,128},{192,160},{224,1... | collective-permute-start | bytes 983048 | tf_op jit(solution)/shard_map/ppermute | solution.py:33
  211.7 11.0 %collective-permute-start.31 = (bf16[8,32,640]{2,1,0:T(8,128)(2,1)}, bf16[8,32,640]{2,1,0:T(8,128)(2,1)}, u32[]{:S(2)}, u32[]{:S(2)}) collective-permute-start(bf16[8,32,640]{2,1,0:T(8,128)(2,1)} %collective-permute-done.29), channel_id=1, source_target_pairs={{0,32},{32,64},{64,96},{96,128},{128,160},{160,192},{192,224},{224... | collective-permute-start | bytes 983048 | tf_op jit(solution)/shard_map/ppermute | solution.py:30
  215.4 17.4 %collective-permute-start.32 = (bf16[8,32,640]{2,1,0:T(8,128)(2,1)}, bf16[8,32,640]{2,1,0:T(8,128)(2,1)}, u32[]{:S(2)}, u32[]{:S(2)}) collective-permute-start(bf16[8,32,640]{2,1,0:T(8,128)(2,1)} %collective-permute-done.30), channel_id=1, source_target_pairs={{0,992},{32,0},{64,32},{96,64},{128,96},{160,128},{192,160},{224,1... | collective-permute-start | bytes 983048 | tf_op jit(solution)/shard_map/ppermute | solution.py:33
  222.7 11.8 %collective-permute-start.33 = (bf16[8,32,640]{2,1,0:T(8,128)(2,1)}, bf16[8,32,640]{2,1,0:T(8,128)(2,1)}, u32[]{:S(2)}, u32[]{:S(2)}) collective-permute-start(bf16[8,32,640]{2,1,0:T(8,128)(2,1)} %collective-permute-done.31), channel_id=1, source_target_pairs={{0,32},{32,64},{64,96},{96,128},{128,160},{160,192},{192,224},{224... | collective-permute-start | bytes 983048 | tf_op jit(solution)/shard_map/ppermute | solution.py:30
  226.3 24.8 %all-to-all-start.2 = ((bf16[16,2,2,8,1024]{4,1,3,2,0:T(2,128)(2,1)}), bf16[16,2,2,8,1024]{4,1,3,2,0:T(2,128)(2,1)}, u32[]{:S(2)}, u32[]{:S(2)}) async-start(bf16[16,2,2,8,1024]{4,1,3,2,0:T(2,128)(2,1)} %copy.45), calls=%async_computation.2 | async-start | bytes 2097152 | tf_op jit(solution)/shard_map/all_to_all | solution.py:50
  237.3 6.3 %collective-permute-start.34 = (bf16[8,32,640]{2,1,0:T(8,128)(2,1)S(1)}, bf16[8,32,640]{2,1,0:T(8,128)(2,1)S(1)}, u32[]{:S(2)}, u32[]{:S(2)}) collective-permute-start(bf16[8,32,640]{2,1,0:T(8,128)(2,1)S(1)} %select_bitcast_fusion), channel_id=1, source_target_pairs={{0,16},{16,0},{1,17},{17,1},{2,18},{18,2},{3,19},{19,3},{4,20},{20... | collective-permute-start | bytes 983048 | tf_op jit(solution)/shard_map/ppermute | solution.py:44
  247.8 10.3 %copy-start.1 = (s32[32]{0:T(128)S(1)}, s32[32]{0:T(128)}, u32[]{:S(2)}) copy-start(s32[32]{0:T(128)} %constant.117) | copy-start | bytes 388
  251.1 23.3 %all-to-all-start.3 = ((bf16[16,2,2,8,1024]{4,1,3,2,0:T(2,128)(2,1)}), bf16[16,2,2,8,1024]{4,1,3,2,0:T(2,128)(2,1)}, u32[]{:S(2)}, u32[]{:S(2)}) async-start(bf16[16,2,2,8,1024]{4,1,3,2,0:T(2,128)(2,1)} %copy.48), calls=%async_computation.3 | async-start | bytes 2097152 | tf_op jit(solution)/shard_map/all_to_all | solution.py:50

commit v8 on v6

--- a/solution.py
+++ b/solution.py
@@ -21,17 +21,15 @@
     partner = me + 1 - 2 * core
     mine_irrep = range_irreps[me]
     partner_irrep = range_irreps[partner]
-    up = [(i, (i + 1) % chips) for i in range(chips)]
-    down = [(i, (i - 1) % chips) for i in range(chips)]
+    step = [
+        (z * cores + c, ((z + 1 - 2 * c) % chips) * cores + c) for z in range(chips) for c in range(cores)
+    ]
 
     arrivals = [(0, trial_slab)]
-    going_up = going_down = trial_slab
-    for distance in range(1, chips // 2 + 1):
-        going_up = lax.ppermute(going_up, "z", up)
-        arrivals.append((chips - distance, going_up))
-        if distance < chips - distance:
-            going_down = lax.ppermute(going_down, "z", down)
-            arrivals.append((distance, going_down))
+    going = trial_slab
+    for distance in range(1, chips):
+        going = lax.ppermute(going, ("z", "core"), step)
+        arrivals.append((distance, going))
 
     size = -(-len(arrivals) // GROUPS)
     order, sums = [], []
@@ -49,10 +47,13 @@
         exchanged = lax.all_to_all(partial, "narrow", split_axis=0, concat_axis=0, tiled=True)
         sums.append(jnp.sum(exchanged.astype(jnp.float32), axis=0).astype(jnp.bfloat16))
     summed = jnp.concatenate(sums, axis=2)
-    by_offset = jnp.take(summed, jnp.array([order.index(r) for r in range(chips)]), axis=2)
-    by_chip = jnp.roll(by_offset, chip, axis=2)
-    by_core = jnp.where(core == 0, by_chip, by_chip[:, ::-1])
-    by_device = jnp.transpose(by_core, (0, 2, 1, 3)).reshape(per_owner, pair_count, local_pairs)
+    by_distance = jnp.take(summed, jnp.array([order.index(d) for d in range(chips)]), axis=2)
+    by_core = jnp.where(core == 0, by_distance, by_distance[:, ::-1])
+    from_below = jnp.take(by_core[:, 0], jnp.array([(-d) % chips for d in range(chips)]), axis=1)
+    by_chip = jnp.stack(
+        [jnp.roll(from_below, chip, axis=1), jnp.roll(by_core[:, 1], chip, axis=1)], axis=1
+    )
+    by_device = jnp.transpose(by_chip, (0, 2, 1, 3)).reshape(per_owner, pair_count, local_pairs)
     owned = lax.all_to_all(by_device, ("z", "core"), split_axis=1, concat_axis=1, tiled=True)
     return owned.reshape(per_owner, pair_count * local_pairs)
 

time: 336 us -> 455 us (1.35)
  waiting for transfers between devices: 37.5 us -> 101 us
  starting transfers between devices: 162 us -> 212 us
    ppermute x31, waiting for transfers between devices: 24.4 us -> 87.4 us  [body(): going = lax.ppermute(going, ('z', 'core'), step)]
    ppermute x31, starting transfers between devices: 114 us -> 148 us  [body(): going = lax.ppermute(going, ('z', 'core'), step)]
    ppermute x4, starting transfers between devices: 21.1 us -> 36.9 us  [body(): received = lax.ppermute(theirs, 'core', [(0, 1), (1, 0)])]
  transfers between devices with their start and end apart: 39 -> 39, of which waited for: 11 -> 24; matrix products, arithmetic and copies ran while one was open for 19% -> 14% of each run, Pallas kernels for 0% -> 0%
where the time goes in v8:
time: 455 us; the launch traced here: 451 us
  starting transfers between devices  212 us (47%)
  waiting for transfers between devices  101 us (22%)
  blocking collectives  59.9 us (13%)
  other arithmetic  39.4 us (9%)
  local copies, waits for them, and re-layouts  25.3 us (6%)
  matrix products  9.02 us (2%)
  between operations  4.72 us (1%)
    ppermute x31, starting transfers between devices, body(): going = lax.ppermute(going, ('z', 'core'), step)  148 us
    ppermute x31, waiting for transfers between devices, body(): going = lax.ppermute(going, ('z', 'core'), step)  87.4 us
    all_to_all x1, blocking collectives, body(): lax.all_to_all(by_device, ('z', 'core'), split_axis=1, concat_axis=1, til...  59.9 us
    ppermute x4, starting transfers between devices, body(): received = lax.ppermute(theirs, 'core', [(0, 1), (1, 0)])  36.9 us
    unnamed x28, other arithmetic  28.2 us
    all_to_all x4, starting transfers between devices, body(): lax.all_to_all(partial, 'narrow', split_axis=0, concat_axis=0, tiled=True)  27.5 us
    reshape x8, local copies, waits for them, and re-layouts, body(): products.astype(jnp.bfloat16)  17.1 us
    all_to_all x4, waiting for transfers between devices, body(): lax.all_to_all(partial, 'narrow', split_axis=0, concat_axis=0, tiled=True)  11.8 us
  transfers between devices with their start and end apart: 39, of which 24 were waited for; matrix products, arithmetic and copies ran while one was open for 14% of the time, Pallas kernels for 0%

profile of v8, /device:TPU:1, one launch (start us, length us, event | category | flops | bytes accessed | tf_op | source)
XLA Modules:
  0.0 451.3 jit_solution(5099334031416361768)
XLA Ops:
  0.0 19.3 %collective-permute-start = (bf16[8,32,640]{2,1,0:T(8,128)(2,1)}, bf16[8,32,640]{2,1,0:T(8,128)(2,1)S(1)}, u32[]{:S(2)}, u32[]{:S(2)}) collective-permute-start(bf16[8,32,640]{2,1,0:T(8,128)(2,1)} %param.9), channel_id=1, source_target_pairs={{0,32},{16,1008},{32,64},{48,16},{64,96},{80,48},{96,128},{112,80}... | collective-permute-start | bytes 983048 | tf_op jit(solution)/shard_map/ppermute | solution.py:31
  19.3 4.3 collective-permute-done
  23.7 4.9 %collective-permute-start.1 = (bf16[8,32,640]{2,1,0:T(8,128)(2,1)S(1)}, bf16[8,32,640]{2,1,0:T(8,128)(2,1)S(1)}, u32[]{:S(2)}, u32[]{:S(2)}) collective-permute-start(bf16[8,32,640]{2,1,0:T(8,128)(2,1)S(1)} %collective-permute-done), channel_id=1, source_target_pairs={{0,32},{16,1008},{32,64},{48,16},{64,96},{80,48},{96,128},{112,80}... | collective-permute-start | bytes 983048 | tf_op jit(solution)/shard_map/ppermute | solution.py:31
  28.6 4.0 collective-permute-done.1
  32.6 5.0 %collective-permute-start.2 = (bf16[8,32,640]{2,1,0:T(8,128)(2,1)S(1)}, bf16[8,32,640]{2,1,0:T(8,128)(2,1)S(1)}, u32[]{:S(2)}, u32[]{:S(2)}) collective-permute-start(bf16[8,32,640]{2,1,0:T(8,128)(2,1)S(1)} %collective-permute-done.1), channel_id=1, source_target_pairs={{0,32},{16,1008},{32,64},{48,16},{64,96},{80,48},{96,128},{112,80}... | collective-permute-start | bytes 983048 | tf_op jit(solution)/shard_map/ppermute | solution.py:31
  37.6 4.0 collective-permute-done.2
  41.6 5.0 %collective-permute-start.3 = (bf16[8,32,640]{2,1,0:T(8,128)(2,1)S(1)}, bf16[8,32,640]{2,1,0:T(8,128)(2,1)S(1)}, u32[]{:S(2)}, u32[]{:S(2)}) collective-permute-start(bf16[8,32,640]{2,1,0:T(8,128)(2,1)S(1)} %collective-permute-done.2), channel_id=1, source_target_pairs={{0,32},{16,1008},{32,64},{48,16},{64,96},{80,48},{96,128},{112,80}... | collective-permute-start | bytes 983048 | tf_op jit(solution)/shard_map/ppermute | solution.py:31
  46.6 4.0 collective-permute-done.3
  50.6 5.0 %collective-permute-start.4 = (bf16[8,32,640]{2,1,0:T(8,128)(2,1)S(1)}, bf16[8,32,640]{2,1,0:T(8,128)(2,1)S(1)}, u32[]{:S(2)}, u32[]{:S(2)}) collective-permute-start(bf16[8,32,640]{2,1,0:T(8,128)(2,1)S(1)} %collective-permute-done.3), channel_id=1, source_target_pairs={{0,32},{16,1008},{32,64},{48,16},{64,96},{80,48},{96,128},{112,80}... | collective-permute-start | bytes 983048 | tf_op jit(solution)/shard_map/ppermute | solution.py:31
  55.6 4.0 collective-permute-done.4
  59.6 5.0 %collective-permute-start.5 = (bf16[8,32,640]{2,1,0:T(8,128)(2,1)S(1)}, bf16[8,32,640]{2,1,0:T(8,128)(2,1)S(1)}, u32[]{:S(2)}, u32[]{:S(2)}) collective-permute-start(bf16[8,32,640]{2,1,0:T(8,128)(2,1)S(1)} %collective-permute-done.4), channel_id=1, source_target_pairs={{0,32},{16,1008},{32,64},{48,16},{64,96},{80,48},{96,128},{112,80}... | collective-permute-start | bytes 983048 | tf_op jit(solution)/shard_map/ppermute | solution.py:31
  64.7 4.0 collective-permute-done.5
  68.7 5.0 %collective-permute-start.6 = (bf16[8,32,640]{2,1,0:T(8,128)(2,1)S(1)}, bf16[8,32,640]{2,1,0:T(8,128)(2,1)S(1)}, u32[]{:S(2)}, u32[]{:S(2)}) collective-permute-start(bf16[8,32,640]{2,1,0:T(8,128)(2,1)S(1)} %collective-permute-done.5), channel_id=1, source_target_pairs={{0,32},{16,1008},{32,64},{48,16},{64,96},{80,48},{96,128},{112,80}... | collective-permute-start | bytes 983048 | tf_op jit(solution)/shard_map/ppermute | solution.py:31
  73.7 4.0 collective-permute-done.6
  77.7 5.0 %collective-permute-start.8 = (bf16[8,32,640]{2,1,0:T(8,128)(2,1)S(1)}, bf16[8,32,640]{2,1,0:T(8,128)(2,1)S(1)}, u32[]{:S(2)}, u32[]{:S(2)}) collective-permute-start(bf16[8,32,640]{2,1,0:T(8,128)(2,1)S(1)} %collective-permute-done.6), channel_id=1, source_target_pairs={{0,32},{16,1008},{32,64},{48,16},{64,96},{80,48},{96,128},{112,80}... | collective-permute-start | bytes 983048 | tf_op jit(solution)/shard_map/ppermute | solution.py:31
  82.7 4.0 collective-permute-done.8
  86.7 5.0 %collective-permute-start.9 = (bf16[8,32,640]{2,1,0:T(8,128)(2,1)S(1)}, bf16[8,32,640]{2,1,0:T(8,128)(2,1)S(1)}, u32[]{:S(2)}, u32[]{:S(2)}) collective-permute-start(bf16[8,32,640]{2,1,0:T(8,128)(2,1)S(1)} %collective-permute-done.8), channel_id=1, source_target_pairs={{0,32},{16,1008},{32,64},{48,16},{64,96},{80,48},{96,128},{112,80}... | collective-permute-start | bytes 983048 | tf_op jit(solution)/shard_map/ppermute | solution.py:31
  91.7 4.0 collective-permute-done.9
  95.7 5.0 %collective-permute-start.10 = (bf16[8,32,640]{2,1,0:T(8,128)(2,1)S(1)}, bf16[8,32,640]{2,1,0:T(8,128)(2,1)S(1)}, u32[]{:S(2)}, u32[]{:S(2)}) collective-permute-start(bf16[8,32,640]{2,1,0:T(8,128)(2,1)S(1)} %collective-permute-done.9), channel_id=1, source_target_pairs={{0,32},{16,1008},{32,64},{48,16},{64,96},{80,48},{96,128},{112,80}... | collective-permute-start | bytes 983048 | tf_op jit(solution)/shard_map/ppermute | solution.py:31
  100.7 4.0 collective-permute-done.10
  104.7 5.0 %collective-permute-start.11 = (bf16[8,32,640]{2,1,0:T(8,128)(2,1)S(1)}, bf16[8,32,640]{2,1,0:T(8,128)(2,1)S(1)}, u32[]{:S(2)}, u32[]{:S(2)}) collective-permute-start(bf16[8,32,640]{2,1,0:T(8,128)(2,1)S(1)} %collective-permute-done.10), channel_id=1, source_target_pairs={{0,32},{16,1008},{32,64},{48,16},{64,96},{80,48},{96,128},{112,80}... | collective-permute-start | bytes 983048 | tf_op jit(solution)/shard_map/ppermute | solution.py:31
  109.8 4.0 collective-permute-done.11
  113.8 5.0 %collective-permute-start.12 = (bf16[8,32,640]{2,1,0:T(8,128)(2,1)S(1)}, bf16[8,32,640]{2,1,0:T(8,128)(2,1)S(1)}, u32[]{:S(2)}, u32[]{:S(2)}) collective-permute-start(bf16[8,32,640]{2,1,0:T(8,128)(2,1)S(1)} %collective-permute-done.11), channel_id=1, source_target_pairs={{0,32},{16,1008},{32,64},{48,16},{64,96},{80,48},{96,128},{112,80}... | collective-permute-start | bytes 983048 | tf_op jit(solution)/shard_map/ppermute | solution.py:31
  118.8 4.0 collective-permute-done.12
  122.8 5.0 %collective-permute-start.13 = (bf16[8,32,640]{2,1,0:T(8,128)(2,1)S(1)}, bf16[8,32,640]{2,1,0:T(8,128)(2,1)S(1)}, u32[]{:S(2)}, u32[]{:S(2)}) collective-permute-start(bf16[8,32,640]{2,1,0:T(8,128)(2,1)S(1)} %collective-permute-done.12), channel_id=1, source_target_pairs={{0,32},{16,1008},{32,64},{48,16},{64,96},{80,48},{96,128},{112,80}... | collective-permute-start | bytes 983048 | tf_op jit(solution)/shard_map/ppermute | solution.py:31
  127.8 4.0 collective-permute-done.13
  131.8 5.0 %collective-permute-start.14 = (bf16[8,32,640]{2,1,0:T(8,128)(2,1)S(1)}, bf16[8,32,640]{2,1,0:T(8,128)(2,1)S(1)}, u32[]{:S(2)}, u32[]{:S(2)}) collective-permute-start(bf16[8,32,640]{2,1,0:T(8,128)(2,1)S(1)} %collective-permute-done.13), channel_id=1, source_target_pairs={{0,32},{16,1008},{32,64},{48,16},{64,96},{80,48},{96,128},{112,80}... | collective-permute-start | bytes 983048 | tf_op jit(solution)/shard_map/ppermute | solution.py:31
  140.8 5.0 %collective-permute-start.15 = (bf16[8,32,640]{2,1,0:T(8,128)(2,1)S(1)}, bf16[8,32,640]{2,1,0:T(8,128)(2,1)S(1)}, u32[]{:S(2)}, u32[]{:S(2)}) collective-permute-start(bf16[8,32,640]{2,1,0:T(8,128)(2,1)S(1)} %collective-permute-done.14), channel_id=1, source_target_pairs={{0,32},{16,1008},{32,64},{48,16},{64,96},{80,48},{96,128},{112,80}... | collective-permute-start | bytes 983048 | tf_op jit(solution)/shard_map/ppermute | solution.py:31
  145.8 4.0 collective-permute-done.15
  149.8 5.0 %collective-permute-start.17 = (bf16[8,32,640]{2,1,0:T(8,128)(2,1)S(1)}, bf16[8,32,640]{2,1,0:T(8,128)(2,1)S(1)}, u32[]{:S(2)}, u32[]{:S(2)}) collective-permute-start(bf16[8,32,640]{2,1,0:T(8,128)(2,1)S(1)} %collective-permute-done.15), channel_id=1, source_target_pairs={{0,32},{16,1008},{32,64},{48,16},{64,96},{80,48},{96,128},{112,80}... | collective-permute-start | bytes 983048 | tf_op jit(solution)/shard_map/ppermute | solution.py:31
  154.9 4.0 collective-permute-done.17
  158.9 5.0 %collective-permute-start.18 = (bf16[8,32,640]{2,1,0:T(8,128)(2,1)S(1)}, bf16[8,32,640]{2,1,0:T(8,128)(2,1)S(1)}, u32[]{:S(2)}, u32[]{:S(2)}) collective-permute-start(bf16[8,32,640]{2,1,0:T(8,128)(2,1)S(1)} %collective-permute-done.17), channel_id=1, source_target_pairs={{0,32},{16,1008},{32,64},{48,16},{64,96},{80,48},{96,128},{112,80}... | collective-permute-start | bytes 983048 | tf_op jit(solution)/shard_map/ppermute | solution.py:31
  167.9 5.0 %collective-permute-start.19 = (bf16[8,32,640]{2,1,0:T(8,128)(2,1)S(1)}, bf16[8,32,640]{2,1,0:T(8,128)(2,1)S(1)}, u32[]{:S(2)}, u32[]{:S(2)}) collective-permute-start(bf16[8,32,640]{2,1,0:T(8,128)(2,1)S(1)} %collective-permute-done.18), channel_id=1, source_target_pairs={{0,32},{16,1008},{32,64},{48,16},{64,96},{80,48},{96,128},{112,80}... | collective-permute-start | bytes 983048 | tf_op jit(solution)/shard_map/ppermute | solution.py:31
  183.7 4.1 collective-permute-done.20
  191.1 4.9 %collective-permute-done.21 = bf16[8,32,640]{2,1,0:T(8,128)(2,1)S(1)} collective-permute-done((bf16[8,32,640]{2,1,0:T(8,128)(2,1)S(1)}, bf16[8,32,640]{2,1,0:T(8,128)(2,1)S(1)}, u32[]{:S(2)}, u32[]{:S(2)}) %collective-permute-start.21) | collective-permute-done | bytes 327712 | tf_op jit(solution)/shard_map/ppermute | solution.py:31
  200.0 22.6 %collective-permute-start.7 = (bf16[8,32,640]{2,1,0:T(8,128)(2,1)S(1)}, bf16[8,32,640]{2,1,0:T(8,128)(2,1)S(1)}, u32[]{:S(2)}, u32[]{:S(2)}) collective-permute-start(bf16[8,32,640]{2,1,0:T(8,128)(2,1)S(1)} %get-tuple-element.19), channel_id=1, source_target_pairs={{0,16},{16,0},{1,17},{17,1},{2,18},{18,2},{3,19},{19,3},{4,20},{20... | collective-permute-start | bytes 983048 | tf_op jit(solution)/shard_map/ppermute | solution.py:41
  222.6 4.9 %collective-permute-start.23 = (bf16[8,32,640]{2,1,0:T(8,128)(2,1)}, bf16[8,32,640]{2,1,0:T(8,128)(2,1)}, u32[]{:S(2)}, u32[]{:S(2)}) collective-permute-start(bf16[8,32,640]{2,1,0:T(8,128)(2,1)} %collective-permute-done.22), channel_id=1, source_target_pairs={{0,32},{16,1008},{32,64},{48,16},{64,96},{80,48},{96,128},{112,80}... | collective-permute-start | bytes 983048 | tf_op jit(solution)/shard_map/ppermute | solution.py:31
  231.1 6.8 %all-to-all-start = ((bf16[16,2,2,8,1024]{4,1,3,2,0:T(2,128)(2,1)}), bf16[16,2,2,8,1024]{4,1,3,2,0:T(2,128)(2,1)S(1)}, u32[]{:S(2)}, u32[]{:S(2)}) async-start(bf16[16,2,2,8,1024]{4,1,3,2,0:T(2,128)(2,1)} %copy.13), calls=%async_computation | async-start | bytes 2097152 | tf_op jit(solution)/shard_map/all_to_all | solution.py:47
  255.9 4.0 collective-permute-start.27
  260.8 7.7 %collective-permute-start.16 = (bf16[8,32,640]{2,1,0:T(8,128)(2,1)S(1)}, bf16[8,32,640]{2,1,0:T(8,128)(2,1)S(1)}, u32[]{:S(2)}, u32[]{:S(2)}) collective-permute-start(bf16[8,32,640]{2,1,0:T(8,128)(2,1)S(1)} %get-tuple-element.35), channel_id=1, source_target_pairs={{0,16},{16,0},{1,17},{17,1},{2,18},{18,2},{3,19},{19,3},{4,20},{20... | collective-permute-start | bytes 983048 | tf_op jit(solution)/shard_map/ppermute | solution.py:41
  272.2 4.8 %collective-permute-start.28 = (bf16[8,32,640]{2,1,0:T(8,128)(2,1)S(1)}, bf16[8,32,640]{2,1,0:T(8,128)(2,1)S(1)}, u32[]{:S(2)}, u32[]{:S(2)}) collective-permute-start(bf16[8,32,640]{2,1,0:T(8,128)(2,1)S(1)} %collective-permute-done.27), channel_id=1, source_target_pairs={{0,32},{16,1008},{32,64},{48,16},{64,96},{80,48},{96,128},{112,80}... | collective-permute-start | bytes 983048 | tf_op jit(solution)/shard_map/ppermute | solution.py:31
  281.6 4.5 %collective-permute-start.29 = (bf16[8,32,640]{2,1,0:T(8,128)(2,1)S(1)}, bf16[8,32,640]{2,1,0:T(8,128)(2,1)}, u32[]{:S(2)}, u32[]{:S(2)}) collective-permute-start(bf16[8,32,640]{2,1,0:T(8,128)(2,1)S(1)} %collective-permute-done.28), channel_id=1, source_target_pairs={{0,32},{16,1008},{32,64},{48,16},{64,96},{80,48},{96,128},{112,80}... | collective-permute-start | bytes 983048 | tf_op jit(solution)/shard_map/ppermute | solution.py:31
  292.3 4.9 %collective-permute-start.30 = (bf16[8,32,640]{2,1,0:T(8,128)(2,1)}, bf16[8,32,640]{2,1,0:T(8,128)(2,1)}, u32[]{:S(2)}, u32[]{:S(2)}) collective-permute-start(bf16[8,32,640]{2,1,0:T(8,128)(2,1)} %collective-permute-done.29), channel_id=1, source_target_pairs={{0,32},{16,1008},{32,64},{48,16},{64,96},{80,48},{96,128},{112,80}... | collective-permute-start | bytes 983048 | tf_op jit(solution)/shard_map/ppermute | solution.py:31
  302.8 6.9 %all-to-all-start.1 = ((bf16[16,2,2,8,1024]{4,1,3,2,0:T(2,128)(2,1)}), bf16[16,2,2,8,1024]{4,1,3,2,0:T(2,128)(2,1)S(1)}, u32[]{:S(2)}, u32[]{:S(2)}) async-start(bf16[16,2,2,8,1024]{4,1,3,2,0:T(2,128)(2,1)} %copy.15), calls=%async_computation.1 | async-start | bytes 2097152 | tf_op jit(solution)/shard_map/all_to_all | solution.py:47
  332.4 6.7 %all-to-all-start.2 = ((bf16[16,2,2,8,1024]{4,1,3,2,0:T(2,128)(2,1)}), bf16[16,2,2,8,1024]{4,1,3,2,0:T(2,128)(2,1)}, u32[]{:S(2)}, u32[]{:S(2)}) async-start(bf16[16,2,2,8,1024]{4,1,3,2,0:T(2,128)(2,1)} %copy.17), calls=%async_computation.2 | async-start | bytes 2097152 | tf_op jit(solution)/shard_map/all_to_all | solution.py:47
  358.9 7.1 %all-to-all-start.3 = ((bf16[16,2,2,8,1024]{4,1,3,2,0:T(2,128)(2,1)}), bf16[16,2,2,8,1024]{4,1,3,2,0:T(2,128)(2,1)}, u32[]{:S(2)}, u32[]{:S(2)}) async-start(bf16[16,2,2,8,1024]{4,1,3,2,0:T(2,128)(2,1)} %copy.19), calls=%async_computation.3 | async-start | bytes 2097152 | tf_op jit(solution)/shard_map/all_to_all | solution.py:47
  370.5 11.8 %all-to-all-done.3 = bf16[16,2,2,8,1024]{4,1,3,2,0:T(2,128)(2,1)} async-done(((bf16[16,2,2,8,1024]{4,1,3,2,0:T(2,128)(2,1)}), bf16[16,2,2,8,1024]{4,1,3,2,0:T(2,128)(2,1)}, u32[]{:S(2)}, u32[]{:S(2)}) %all-to-all-start.3) | async-done | bytes 1048608 | tf_op jit(solution)/shard_map/all_to_all | solution.py:47
  390.7 59.9 %all_to_all.25 = bf16[2,64,1024]{2,0,1:T(2,128)(2,1)S(1)} all-to-all(bf16[2,64,1024]{2,0,1:T(2,128)(2,1)S(1)} %bitcast.129), channel_id=1, replica_groups=mesh['z'=32,'core'=2,'narrow'=16] {'z','core'}, dimensions={1} | all-to-all | bytes 524288 | tf_op jit(solution)/shard_map/all_to_all | solution.py:57
  (151 shorter events, 120.2 us)
Async XLA Ops:
  0.0 227.5 %copy-start = (bf16[1024,640]{1,0:T(8,128)(2,1)S(1)}, bf16[1024,640]{1,0:T(8,128)(2,1)}, u32[]{:S(2)}) copy-start(bf16[1024,640]{1,0:T(8,128)(2,1)} %param.10) | copy-start | bytes 3932164
  0.0 23.7 %collective-permute-start = (bf16[8,32,640]{2,1,0:T(8,128)(2,1)}, bf16[8,32,640]{2,1,0:T(8,128)(2,1)S(1)}, u32[]{:S(2)}, u32[]{:S(2)}) collective-permute-start(bf16[8,32,640]{2,1,0:T(8,128)(2,1)} %param.9), channel_id=1, source_target_pairs={{0,32},{16,1008},{32,64},{48,16},{64,96},{80,48},{96,128},{112,80}... | collective-permute-start | bytes 983048 | tf_op jit(solution)/shard_map/ppermute | solution.py:31
  23.7 8.9 %collective-permute-start.1 = (bf16[8,32,640]{2,1,0:T(8,128)(2,1)S(1)}, bf16[8,32,640]{2,1,0:T(8,128)(2,1)S(1)}, u32[]{:S(2)}, u32[]{:S(2)}) collective-permute-start(bf16[8,32,640]{2,1,0:T(8,128)(2,1)S(1)} %collective-permute-done), channel_id=1, source_target_pairs={{0,32},{16,1008},{32,64},{48,16},{64,96},{80,48},{96,128},{112,80}... | collective-permute-start | bytes 983048 | tf_op jit(solution)/shard_map/ppermute | solution.py:31
  32.6 9.0 %collective-permute-start.2 = (bf16[8,32,640]{2,1,0:T(8,128)(2,1)S(1)}, bf16[8,32,640]{2,1,0:T(8,128)(2,1)S(1)}, u32[]{:S(2)}, u32[]{:S(2)}) collective-permute-start(bf16[8,32,640]{2,1,0:T(8,128)(2,1)S(1)} %collective-permute-done.1), channel_id=1, source_target_pairs={{0,32},{16,1008},{32,64},{48,16},{64,96},{80,48},{96,128},{112,80}... | collective-permute-start | bytes 983048 | tf_op jit(solution)/shard_map/ppermute | solution.py:31
  41.6 41.1 %copy-start.12 = (bf16[8,32,640]{2,1,0:T(8,128)(2,1)}, bf16[8,32,640]{2,1,0:T(8,128)(2,1)S(1)}, u32[]{:S(2)}) copy-start(bf16[8,32,640]{2,1,0:T(8,128)(2,1)S(1)} %collective-permute-done.2) | copy-start | bytes 983044
  41.6 9.0 %collective-permute-start.3 = (bf16[8,32,640]{2,1,0:T(8,128)(2,1)S(1)}, bf16[8,32,640]{2,1,0:T(8,128)(2,1)S(1)}, u32[]{:S(2)}, u32[]{:S(2)}) collective-permute-start(bf16[8,32,640]{2,1,0:T(8,128)(2,1)S(1)} %collective-permute-done.2), channel_id=1, source_target_pairs={{0,32},{16,1008},{32,64},{48,16},{64,96},{80,48},{96,128},{112,80}... | collective-permute-start | bytes 983048 | tf_op jit(solution)/shard_map/ppermute | solution.py:31
  50.6 9.0 %collective-permute-start.4 = (bf16[8,32,640]{2,1,0:T(8,128)(2,1)S(1)}, bf16[8,32,640]{2,1,0:T(8,128)(2,1)S(1)}, u32[]{:S(2)}, u32[]{:S(2)}) collective-permute-start(bf16[8,32,640]{2,1,0:T(8,128)(2,1)S(1)} %collective-permute-done.3), channel_id=1, source_target_pairs={{0,32},{16,1008},{32,64},{48,16},{64,96},{80,48},{96,128},{112,80}... | collective-permute-start | bytes 983048 | tf_op jit(solution)/shard_map/ppermute | solution.py:31
  59.6 9.0 %collective-permute-start.5 = (bf16[8,32,640]{2,1,0:T(8,128)(2,1)S(1)}, bf16[8,32,640]{2,1,0:T(8,128)(2,1)S(1)}, u32[]{:S(2)}, u32[]{:S(2)}) collective-permute-start(bf16[8,32,640]{2,1,0:T(8,128)(2,1)S(1)} %collective-permute-done.4), channel_id=1, source_target_pairs={{0,32},{16,1008},{32,64},{48,16},{64,96},{80,48},{96,128},{112,80}... | collective-permute-start | bytes 983048 | tf_op jit(solution)/shard_map/ppermute | solution.py:31
  68.7 9.0 %collective-permute-start.6 = (bf16[8,32,640]{2,1,0:T(8,128)(2,1)S(1)}, bf16[8,32,640]{2,1,0:T(8,128)(2,1)S(1)}, u32[]{:S(2)}, u32[]{:S(2)}) collective-permute-start(bf16[8,32,640]{2,1,0:T(8,128)(2,1)S(1)} %collective-permute-done.5), channel_id=1, source_target_pairs={{0,32},{16,1008},{32,64},{48,16},{64,96},{80,48},{96,128},{112,80}... | collective-permute-start | bytes 983048 | tf_op jit(solution)/shard_map/ppermute | solution.py:31
  77.7 9.0 %collective-permute-start.8 = (bf16[8,32,640]{2,1,0:T(8,128)(2,1)S(1)}, bf16[8,32,640]{2,1,0:T(8,128)(2,1)S(1)}, u32[]{:S(2)}, u32[]{:S(2)}) collective-permute-start(bf16[8,32,640]{2,1,0:T(8,128)(2,1)S(1)} %collective-permute-done.6), channel_id=1, source_target_pairs={{0,32},{16,1008},{32,64},{48,16},{64,96},{80,48},{96,128},{112,80}... | collective-permute-start | bytes 983048 | tf_op jit(solution)/shard_map/ppermute | solution.py:31
  86.7 9.0 %collective-permute-start.9 = (bf16[8,32,640]{2,1,0:T(8,128)(2,1)S(1)}, bf16[8,32,640]{2,1,0:T(8,128)(2,1)S(1)}, u32[]{:S(2)}, u32[]{:S(2)}) collective-permute-start(bf16[8,32,640]{2,1,0:T(8,128)(2,1)S(1)} %collective-permute-done.8), channel_id=1, source_target_pairs={{0,32},{16,1008},{32,64},{48,16},{64,96},{80,48},{96,128},{112,80}... | collective-permute-start | bytes 983048 | tf_op jit(solution)/shard_map/ppermute | solution.py:31
  95.7 9.0 %collective-permute-start.10 = (bf16[8,32,640]{2,1,0:T(8,128)(2,1)S(1)}, bf16[8,32,640]{2,1,0:T(8,128)(2,1)S(1)}, u32[]{:S(2)}, u32[]{:S(2)}) collective-permute-start(bf16[8,32,640]{2,1,0:T(8,128)(2,1)S(1)} %collective-permute-done.9), channel_id=1, source_target_pairs={{0,32},{16,1008},{32,64},{48,16},{64,96},{80,48},{96,128},{112,80}... | collective-permute-start | bytes 983048 | tf_op jit(solution)/shard_map/ppermute | solution.py:31
  104.7 9.0 %collective-permute-start.11 = (bf16[8,32,640]{2,1,0:T(8,128)(2,1)S(1)}, bf16[8,32,640]{2,1,0:T(8,128)(2,1)S(1)}, u32[]{:S(2)}, u32[]{:S(2)}) collective-permute-start(bf16[8,32,640]{2,1,0:T(8,128)(2,1)S(1)} %collective-permute-done.10), channel_id=1, source_target_pairs={{0,32},{16,1008},{32,64},{48,16},{64,96},{80,48},{96,128},{112,80}... | collective-permute-start | bytes 983048 | tf_op jit(solution)/shard_map/ppermute | solution.py:31
  113.8 9.0 %collective-permute-start.12 = (bf16[8,32,640]{2,1,0:T(8,128)(2,1)S(1)}, bf16[8,32,640]{2,1,0:T(8,128)(2,1)S(1)}, u32[]{:S(2)}, u32[]{:S(2)}) collective-permute-start(bf16[8,32,640]{2,1,0:T(8,128)(2,1)S(1)} %collective-permute-done.11), channel_id=1, source_target_pairs={{0,32},{16,1008},{32,64},{48,16},{64,96},{80,48},{96,128},{112,80}... | collective-permute-start | bytes 983048 | tf_op jit(solution)/shard_map/ppermute | solution.py:31
  122.8 23.1 %copy-start.5 = (bf16[8,32,640]{2,1,0:T(8,128)(2,1)}, bf16[8,32,640]{2,1,0:T(8,128)(2,1)S(1)}, u32[]{:S(2)}) copy-start(bf16[8,32,640]{2,1,0:T(8,128)(2,1)S(1)} %collective-permute-done.12) | copy-start | bytes 983044
  122.8 9.0 %collective-permute-start.13 = (bf16[8,32,640]{2,1,0:T(8,128)(2,1)S(1)}, bf16[8,32,640]{2,1,0:T(8,128)(2,1)S(1)}, u32[]{:S(2)}, u32[]{:S(2)}) collective-permute-start(bf16[8,32,640]{2,1,0:T(8,128)(2,1)S(1)} %collective-permute-done.12), channel_id=1, source_target_pairs={{0,32},{16,1008},{32,64},{48,16},{64,96},{80,48},{96,128},{112,80}... | collective-permute-start | bytes 983048 | tf_op jit(solution)/shard_map/ppermute | solution.py:31
  131.8 9.0 %collective-permute-start.14 = (bf16[8,32,640]{2,1,0:T(8,128)(2,1)S(1)}, bf16[8,32,640]{2,1,0:T(8,128)(2,1)S(1)}, u32[]{:S(2)}, u32[]{:S(2)}) collective-permute-start(bf16[8,32,640]{2,1,0:T(8,128)(2,1)S(1)} %collective-permute-done.13), channel_id=1, source_target_pairs={{0,32},{16,1008},{32,64},{48,16},{64,96},{80,48},{96,128},{112,80}... | collective-permute-start | bytes 983048 | tf_op jit(solution)/shard_map/ppermute | solution.py:31
  140.8 32.1 %copy-start.7 = (bf16[8,32,640]{2,1,0:T(8,128)(2,1)}, bf16[8,32,640]{2,1,0:T(8,128)(2,1)S(1)}, u32[]{:S(2)}) copy-start(bf16[8,32,640]{2,1,0:T(8,128)(2,1)S(1)} %collective-permute-done.14) | copy-start | bytes 983044
  140.8 9.0 %collective-permute-start.15 = (bf16[8,32,640]{2,1,0:T(8,128)(2,1)S(1)}, bf16[8,32,640]{2,1,0:T(8,128)(2,1)S(1)}, u32[]{:S(2)}, u32[]{:S(2)}) collective-permute-start(bf16[8,32,640]{2,1,0:T(8,128)(2,1)S(1)} %collective-permute-done.14), channel_id=1, source_target_pairs={{0,32},{16,1008},{32,64},{48,16},{64,96},{80,48},{96,128},{112,80}... | collective-permute-start | bytes 983048 | tf_op jit(solution)/shard_map/ppermute | solution.py:31
  149.8 18.0 %copy-start.4 = (bf16[8,32,640]{2,1,0:T(8,128)(2,1)}, bf16[8,32,640]{2,1,0:T(8,128)(2,1)S(1)}, u32[]{:S(2)}) copy-start(bf16[8,32,640]{2,1,0:T(8,128)(2,1)S(1)} %collective-permute-done.15) | copy-start | bytes 983044
  149.8 9.0 %collective-permute-start.17 = (bf16[8,32,640]{2,1,0:T(8,128)(2,1)S(1)}, bf16[8,32,640]{2,1,0:T(8,128)(2,1)S(1)}, u32[]{:S(2)}, u32[]{:S(2)}) collective-permute-start(bf16[8,32,640]{2,1,0:T(8,128)(2,1)S(1)} %collective-permute-done.15), channel_id=1, source_target_pairs={{0,32},{16,1008},{32,64},{48,16},{64,96},{80,48},{96,128},{112,80}... | collective-permute-start | bytes 983048 | tf_op jit(solution)/shard_map/ppermute | solution.py:31
  158.9 9.0 %collective-permute-start.18 = (bf16[8,32,640]{2,1,0:T(8,128)(2,1)S(1)}, bf16[8,32,640]{2,1,0:T(8,128)(2,1)S(1)}, u32[]{:S(2)}, u32[]{:S(2)}) collective-permute-start(bf16[8,32,640]{2,1,0:T(8,128)(2,1)S(1)} %collective-permute-done.17), channel_id=1, source_target_pairs={{0,32},{16,1008},{32,64},{48,16},{64,96},{80,48},{96,128},{112,80}... | collective-permute-start | bytes 983048 | tf_op jit(solution)/shard_map/ppermute | solution.py:31
  167.9 59.6 %copy-start.3 = (bf16[8,32,640]{2,1,0:T(8,128)(2,1)}, bf16[8,32,640]{2,1,0:T(8,128)(2,1)S(1)}, u32[]{:S(2)}) copy-start(bf16[8,32,640]{2,1,0:T(8,128)(2,1)S(1)} %collective-permute-done.18) | copy-start | bytes 983044
  167.9 12.1 %collective-permute-start.19 = (bf16[8,32,640]{2,1,0:T(8,128)(2,1)S(1)}, bf16[8,32,640]{2,1,0:T(8,128)(2,1)S(1)}, u32[]{:S(2)}, u32[]{:S(2)}) collective-permute-start(bf16[8,32,640]{2,1,0:T(8,128)(2,1)S(1)} %collective-permute-done.18), channel_id=1, source_target_pairs={{0,32},{16,1008},{32,64},{48,16},{64,96},{80,48},{96,128},{112,80}... | collective-permute-start | bytes 983048 | tf_op jit(solution)/shard_map/ppermute | solution.py:31
  179.9 47.6 %copy-start.1 = (bf16[8,32,640]{2,1,0:T(8,128)(2,1)}, bf16[8,32,640]{2,1,0:T(8,128)(2,1)S(1)}, u32[]{:S(2)}) copy-start(bf16[8,32,640]{2,1,0:T(8,128)(2,1)S(1)} %collective-permute-done.19) | copy-start | bytes 983044
  180.0 7.9 %collective-permute-start.20 = (bf16[8,32,640]{2,1,0:T(8,128)(2,1)S(1)}, bf16[8,32,640]{2,1,0:T(8,128)(2,1)S(1)}, u32[]{:S(2)}, u32[]{:S(2)}) collective-permute-start(bf16[8,32,640]{2,1,0:T(8,128)(2,1)S(1)} %collective-permute-done.19), channel_id=1, source_target_pairs={{0,32},{16,1008},{32,64},{48,16},{64,96},{80,48},{96,128},{112,80}... | collective-permute-start | bytes 983048 | tf_op jit(solution)/shard_map/ppermute | solution.py:31
  187.9 39.6 %copy-start.15 = (bf16[8,32,640]{2,1,0:T(8,128)(2,1)}, bf16[8,32,640]{2,1,0:T(8,128)(2,1)S(1)}, u32[]{:S(2)}) copy-start(bf16[8,32,640]{2,1,0:T(8,128)(2,1)S(1)} %collective-permute-done.20) | copy-start | bytes 983044
  187.9 8.1 %collective-permute-start.21 = (bf16[8,32,640]{2,1,0:T(8,128)(2,1)S(1)}, bf16[8,32,640]{2,1,0:T(8,128)(2,1)S(1)}, u32[]{:S(2)}, u32[]{:S(2)}) collective-permute-start(bf16[8,32,640]{2,1,0:T(8,128)(2,1)S(1)} %collective-permute-done.20), channel_id=1, source_target_pairs={{0,32},{16,1008},{32,64},{48,16},{64,96},{80,48},{96,128},{112,80}... | collective-permute-start | bytes 983048 | tf_op jit(solution)/shard_map/ppermute | solution.py:31
  196.0 31.5 %copy-start.16 = (bf16[8,32,640]{2,1,0:T(8,128)(2,1)}, bf16[8,32,640]{2,1,0:T(8,128)(2,1)S(1)}, u32[]{:S(2)}) copy-start(bf16[8,32,640]{2,1,0:T(8,128)(2,1)S(1)} %collective-permute-done.21) | copy-start | bytes 983044
  196.0 26.6 %collective-permute-start.22 = (bf16[8,32,640]{2,1,0:T(8,128)(2,1)S(1)}, bf16[8,32,640]{2,1,0:T(8,128)(2,1)}, u32[]{:S(2)}, u32[]{:S(2)}) collective-permute-start(bf16[8,32,640]{2,1,0:T(8,128)(2,1)S(1)} %collective-permute-done.21), channel_id=1, source_target_pairs={{0,32},{16,1008},{32,64},{48,16},{64,96},{80,48},{96,128},{112,80}... | collective-permute-start | bytes 983048 | tf_op jit(solution)/shard_map/ppermute | solution.py:31
  200.0 27.5 %collective-permute-start.7 = (bf16[8,32,640]{2,1,0:T(8,128)(2,1)S(1)}, bf16[8,32,640]{2,1,0:T(8,128)(2,1)S(1)}, u32[]{:S(2)}, u32[]{:S(2)}) collective-permute-start(bf16[8,32,640]{2,1,0:T(8,128)(2,1)S(1)} %get-tuple-element.19), channel_id=1, source_target_pairs={{0,16},{16,0},{1,17},{17,1},{2,18},{18,2},{3,19},{19,3},{4,20},{20... | collective-permute-start | bytes 983048 | tf_op jit(solution)/shard_map/ppermute | solution.py:41
  222.6 16.1 %collective-permute-start.23 = (bf16[8,32,640]{2,1,0:T(8,128)(2,1)}, bf16[8,32,640]{2,1,0:T(8,128)(2,1)}, u32[]{:S(2)}, u32[]{:S(2)}) collective-permute-start(bf16[8,32,640]{2,1,0:T(8,128)(2,1)} %collective-permute-done.22), channel_id=1, source_target_pairs={{0,32},{16,1008},{32,64},{48,16},{64,96},{80,48},{96,128},{112,80}... | collective-permute-start | bytes 983048 | tf_op jit(solution)/shard_map/ppermute | solution.py:31
  231.1 71.7 %all-to-all-start = ((bf16[16,2,2,8,1024]{4,1,3,2,0:T(2,128)(2,1)}), bf16[16,2,2,8,1024]{4,1,3,2,0:T(2,128)(2,1)S(1)}, u32[]{:S(2)}, u32[]{:S(2)}) async-start(bf16[16,2,2,8,1024]{4,1,3,2,0:T(2,128)(2,1)} %copy.13), calls=%async_computation | async-start | bytes 2097152 | tf_op jit(solution)/shard_map/all_to_all | solution.py:47
  238.8 8.3 %collective-permute-start.24 = (bf16[8,32,640]{2,1,0:T(8,128)(2,1)}, bf16[8,32,640]{2,1,0:T(8,128)(2,1)S(1)}, u32[]{:S(2)}, u32[]{:S(2)}) collective-permute-start(bf16[8,32,640]{2,1,0:T(8,128)(2,1)} %collective-permute-done.23), channel_id=1, source_target_pairs={{0,32},{16,1008},{32,64},{48,16},{64,96},{80,48},{96,128},{112,80}... | collective-permute-start | bytes 983048 | tf_op jit(solution)/shard_map/ppermute | solution.py:31
  247.1 8.1 %collective-permute-start.26 = (bf16[8,32,640]{2,1,0:T(8,128)(2,1)S(1)}, bf16[8,32,640]{2,1,0:T(8,128)(2,1)S(1)}, u32[]{:S(2)}, u32[]{:S(2)}) collective-permute-start(bf16[8,32,640]{2,1,0:T(8,128)(2,1)S(1)} %collective-permute-done.24), channel_id=1, source_target_pairs={{0,32},{16,1008},{32,64},{48,16},{64,96},{80,48},{96,128},{112,80}... | collective-permute-start | bytes 983048 | tf_op jit(solution)/shard_map/ppermute | solution.py:31
  255.9 15.6 %collective-permute-start.27 = (bf16[8,32,640]{2,1,0:T(8,128)(2,1)S(1)}, bf16[8,32,640]{2,1,0:T(8,128)(2,1)S(1)}, u32[]{:S(2)}, u32[]{:S(2)}) collective-permute-start(bf16[8,32,640]{2,1,0:T(8,128)(2,1)S(1)} %collective-permute-done.26), channel_id=1, source_target_pairs={{0,32},{16,1008},{32,64},{48,16},{64,96},{80,48},{96,128},{112,80}... | collective-permute-start | bytes 983048 | tf_op jit(solution)/shard_map/ppermute | solution.py:31
  260.8 36.3 %collective-permute-start.16 = (bf16[8,32,640]{2,1,0:T(8,128)(2,1)S(1)}, bf16[8,32,640]{2,1,0:T(8,128)(2,1)S(1)}, u32[]{:S(2)}, u32[]{:S(2)}) collective-permute-start(bf16[8,32,640]{2,1,0:T(8,128)(2,1)S(1)} %get-tuple-element.35), channel_id=1, source_target_pairs={{0,16},{16,0},{1,17},{17,1},{2,18},{18,2},{3,19},{19,3},{4,20},{20... | collective-permute-start | bytes 983048 | tf_op jit(solution)/shard_map/ppermute | solution.py:41
  272.2 9.3 %collective-permute-start.28 = (bf16[8,32,640]{2,1,0:T(8,128)(2,1)S(1)}, bf16[8,32,640]{2,1,0:T(8,128)(2,1)S(1)}, u32[]{:S(2)}, u32[]{:S(2)}) collective-permute-start(bf16[8,32,640]{2,1,0:T(8,128)(2,1)S(1)} %collective-permute-done.27), channel_id=1, source_target_pairs={{0,32},{16,1008},{32,64},{48,16},{64,96},{80,48},{96,128},{112,80}... | collective-permute-start | bytes 983048 | tf_op jit(solution)/shard_map/ppermute | solution.py:31
  281.6 10.8 %collective-permute-start.29 = (bf16[8,32,640]{2,1,0:T(8,128)(2,1)S(1)}, bf16[8,32,640]{2,1,0:T(8,128)(2,1)}, u32[]{:S(2)}, u32[]{:S(2)}) collective-permute-start(bf16[8,32,640]{2,1,0:T(8,128)(2,1)S(1)} %collective-permute-done.28), channel_id=1, source_target_pairs={{0,32},{16,1008},{32,64},{48,16},{64,96},{80,48},{96,128},{112,80}... | collective-permute-start | bytes 983048 | tf_op jit(solution)/shard_map/ppermute | solution.py:31
  289.7 21.9 %collective-permute-start.25 = (bf16[8,32,640]{2,1,0:T(8,128)(2,1)}, bf16[8,32,640]{2,1,0:T(8,128)(2,1)}, u32[]{:S(2)}, u32[]{:S(2)}) collective-permute-start(bf16[8,32,640]{2,1,0:T(8,128)(2,1)} %get-tuple-element.51), channel_id=1, source_target_pairs={{0,16},{16,0},{1,17},{17,1},{2,18},{18,2},{3,19},{19,3},{4,20},{20... | collective-permute-start | bytes 983048 | tf_op jit(solution)/shard_map/ppermute | solution.py:41
  292.3 17.4 %collective-permute-start.30 = (bf16[8,32,640]{2,1,0:T(8,128)(2,1)}, bf16[8,32,640]{2,1,0:T(8,128)(2,1)}, u32[]{:S(2)}, u32[]{:S(2)}) collective-permute-start(bf16[8,32,640]{2,1,0:T(8,128)(2,1)} %collective-permute-done.29), channel_id=1, source_target_pairs={{0,32},{16,1008},{32,64},{48,16},{64,96},{80,48},{96,128},{112,80}... | collective-permute-start | bytes 983048 | tf_op jit(solution)/shard_map/ppermute | solution.py:31
  302.8 29.6 %all-to-all-start.1 = ((bf16[16,2,2,8,1024]{4,1,3,2,0:T(2,128)(2,1)}), bf16[16,2,2,8,1024]{4,1,3,2,0:T(2,128)(2,1)S(1)}, u32[]{:S(2)}, u32[]{:S(2)}) async-start(bf16[16,2,2,8,1024]{4,1,3,2,0:T(2,128)(2,1)} %copy.15), calls=%async_computation.1 | async-start | bytes 2097152 | tf_op jit(solution)/shard_map/all_to_all | solution.py:47
  309.7 11.4 %collective-permute-start.31 = (bf16[8,32,640]{2,1,0:T(8,128)(2,1)}, bf16[8,32,640]{2,1,0:T(8,128)(2,1)}, u32[]{:S(2)}, u32[]{:S(2)}) collective-permute-start(bf16[8,32,640]{2,1,0:T(8,128)(2,1)} %collective-permute-done.30), channel_id=1, source_target_pairs={{0,32},{16,1008},{32,64},{48,16},{64,96},{80,48},{96,128},{112,80}... | collective-permute-start | bytes 983048 | tf_op jit(solution)/shard_map/ppermute | solution.py:31
  321.1 8.4 %collective-permute-start.32 = (bf16[8,32,640]{2,1,0:T(8,128)(2,1)}, bf16[8,32,640]{2,1,0:T(8,128)(2,1)}, u32[]{:S(2)}, u32[]{:S(2)}) collective-permute-start(bf16[8,32,640]{2,1,0:T(8,128)(2,1)} %collective-permute-done.31), channel_id=1, source_target_pairs={{0,32},{16,1008},{32,64},{48,16},{64,96},{80,48},{96,128},{112,80}... | collective-permute-start | bytes 983048 | tf_op jit(solution)/shard_map/ppermute | solution.py:31
  329.6 14.1 %collective-permute-start.33 = (bf16[8,32,640]{2,1,0:T(8,128)(2,1)}, bf16[8,32,640]{2,1,0:T(8,128)(2,1)}, u32[]{:S(2)}, u32[]{:S(2)}) collective-permute-start(bf16[8,32,640]{2,1,0:T(8,128)(2,1)} %collective-permute-done.32), channel_id=1, source_target_pairs={{0,32},{16,1008},{32,64},{48,16},{64,96},{80,48},{96,128},{112,80}... | collective-permute-start | bytes 983048 | tf_op jit(solution)/shard_map/ppermute | solution.py:31
  332.4 26.5 %all-to-all-start.2 = ((bf16[16,2,2,8,1024]{4,1,3,2,0:T(2,128)(2,1)}), bf16[16,2,2,8,1024]{4,1,3,2,0:T(2,128)(2,1)}, u32[]{:S(2)}, u32[]{:S(2)}) async-start(bf16[16,2,2,8,1024]{4,1,3,2,0:T(2,128)(2,1)} %copy.17), calls=%async_computation.2 | async-start | bytes 2097152 | tf_op jit(solution)/shard_map/all_to_all | solution.py:47
  345.2 5.2 %collective-permute-start.34 = (bf16[8,32,640]{2,1,0:T(8,128)(2,1)}, bf16[8,32,640]{2,1,0:T(8,128)(2,1)S(1)}, u32[]{:S(2)}, u32[]{:S(2)}) collective-permute-start(bf16[8,32,640]{2,1,0:T(8,128)(2,1)} %get-tuple-element.67), channel_id=1, source_target_pairs={{0,16},{16,0},{1,17},{17,1},{2,18},{18,2},{3,19},{19,3},{4,20},{20... | collective-permute-start | bytes 983048 | tf_op jit(solution)/shard_map/ppermute | solution.py:41
  358.9 23.5 %all-to-all-start.3 = ((bf16[16,2,2,8,1024]{4,1,3,2,0:T(2,128)(2,1)}), bf16[16,2,2,8,1024]{4,1,3,2,0:T(2,128)(2,1)}, u32[]{:S(2)}, u32[]{:S(2)}) async-start(bf16[16,2,2,8,1024]{4,1,3,2,0:T(2,128)(2,1)} %copy.19), calls=%async_computation.3 | async-start | bytes 2097152 | tf_op jit(solution)/shard_map/all_to_all | solution.py:47
  (15 other events, 99.1 us)

commit v9 on v6

--- a/solution.py
+++ b/solution.py
@@ -24,13 +24,14 @@
     up = [(i, (i + 1) % chips) for i in range(chips)]
     down = [(i, (i - 1) % chips) for i in range(chips)]
 
-    arrivals = [(0, trial_slab)]
-    going_up = going_down = trial_slab
+    halves = tuple(jnp.split(trial_slab, 2, axis=1))
+    arrivals = [(0, halves)]
+    going_up = going_down = halves
     for distance in range(1, chips // 2 + 1):
-        going_up = lax.ppermute(going_up, "z", up)
+        going_up = tuple(lax.ppermute(h, "z", up) for h in going_up)
         arrivals.append((chips - distance, going_up))
         if distance < chips - distance:
-            going_down = lax.ppermute(going_down, "z", down)
+            going_down = tuple(lax.ppermute(h, "z", down) for h in going_down)
             arrivals.append((distance, going_down))
 
     size = -(-len(arrivals) // GROUPS)
@@ -38,8 +39,10 @@
     for start in range(0, len(arrivals), size):
         group = arrivals[start:start + size]
         order += [r for r, _ in group]
-        mine = jnp.stack([jnp.take(b, mine_irrep, axis=0) for _, b in group])
-        theirs = jnp.stack([jnp.take(b, partner_irrep, axis=0) for _, b in group])
+        mine = jnp.stack([jnp.concatenate([jnp.take(h, mine_irrep, axis=0) for h in b]) for _, b in group])
+        theirs = jnp.stack(
+            [jnp.concatenate([jnp.take(h, partner_irrep, axis=0) for h in b]) for _, b in group]
+        )
         received = lax.ppermute(theirs, "core", [(0, 1), (1, 0)])
         rows = jnp.stack([mine, received])
         products = jnp.einsum("snmc,ac->msna", rows, ladder, preferred_element_type=jnp.float32)

time: 336 us -> 418 us (1.24)
  starting transfers between devices: 162 us -> 253 us
  waiting for transfers between devices: 37.5 us -> 27.7 us
    ppermute x31 -> x62, starting transfers between devices: 114 us -> 201 us  [the longest x30 125 us: body(): going_down = tuple((lax.ppermute(h, 'z', down) for h in going_down))]
    select_n x0 -> x63, other arithmetic: none -> 20.3 us  [body(): jnp.take(h, mine_irrep, axis=0)]
    unnamed x28 -> x53, other arithmetic: 24.9 us -> 9.73 us
    ppermute x31 -> x62, waiting for transfers between devices: 24.4 us -> 14.8 us  [the longest x30 14.3 us: body(): going_down = tuple((lax.ppermute(h, 'z', down) for h in going_down))]
  transfers between devices with their start and end apart: 39 -> 70, of which waited for: 11 -> 7; matrix products, arithmetic and copies ran while one was open for 19% -> 15% of each run, Pallas kernels for 0% -> 0%
where the time goes in v9:
time: 418 us; the launch traced here: 414 us
  starting transfers between devices  253 us (61%)
  blocking collectives  56.3 us (13%)
  other arithmetic  40.2 us (10%)
  waiting for transfers between devices  27.7 us (7%)
  local copies, waits for them, and re-layouts  23 us (6%)
  matrix products  8.05 us (2%)
  between operations  5.69 us (1%)
    ppermute x30, starting transfers between devices, body(): going_down = tuple((lax.ppermute(h, 'z', down) for h in going_down))  125 us
    ppermute x32, starting transfers between devices, body(): going_up = tuple((lax.ppermute(h, 'z', up) for h in going_up))  75.6 us
    all_to_all x1, blocking collectives, body(): lax.all_to_all(by_device, ('z', 'core'), split_axis=1, concat_axis=1, til...  56.3 us
    all_to_all x4, starting transfers between devices, body(): lax.all_to_all(partial, 'narrow', split_axis=0, concat_axis=0, tiled=True)  27.6 us
    ppermute x4, starting transfers between devices, body(): received = lax.ppermute(theirs, 'core', [(0, 1), (1, 0)])  24.3 us
    select_n x63, other arithmetic, body(): jnp.take(h, mine_irrep, axis=0)  20.3 us
    reshape x8, local copies, waits for them, and re-layouts, body(): products.astype(jnp.bfloat16)  15.3 us
    ppermute x30, waiting for transfers between devices, body(): going_down = tuple((lax.ppermute(h, 'z', down) for h in going_down))  14.3 us
  transfers between devices with their start and end apart: 70, of which 7 were waited for; matrix products, arithmetic and copies ran while one was open for 15% of the time, Pallas kernels for 0%

profile of v9, /device:TPU:1, one launch (start us, length us, event | category | flops | bytes accessed | tf_op | source)
XLA Modules:
  0.0 413.7 jit_solution(17226867508690654030)
XLA Ops:
  1.1 4.4 %collective-permute-start = (bf16[8,16,640]{2,1,0:T(8,128)(2,1)S(1)}, bf16[8,16,640]{2,1,0:T(8,128)(2,1)S(1)}, u32[]{:S(2)}, u32[]{:S(2)}) collective-permute-start(bf16[8,16,640]{2,1,0:T(8,128)(2,1)S(1)} %get-tuple-element.17), channel_id=1, source_target_pairs={{0,32},{32,64},{64,96},{96,128},{128,160},{160,192},{192,224},{224... | collective-permute-start | bytes 491528 | tf_op jit(solution)/shard_map/ppermute | solution.py:31
  5.5 16.8 %collective-permute-start.2 = (bf16[8,16,640]{2,1,0:T(8,128)(2,1)S(1)}, bf16[8,16,640]{2,1,0:T(8,128)(2,1)S(1)}, u32[]{:S(2)}, u32[]{:S(2)}) collective-permute-start(bf16[8,16,640]{2,1,0:T(8,128)(2,1)S(1)} %get-tuple-element.17), channel_id=1, source_target_pairs={{0,992},{32,0},{64,32},{96,64},{128,96},{160,128},{192,160},{224,1... | collective-permute-start | bytes 491528 | tf_op jit(solution)/shard_map/ppermute | solution.py:34
  24.2 4.6 %collective-permute-start.3 = (bf16[8,16,640]{2,1,0:T(8,128)(2,1)S(1)}, bf16[8,16,640]{2,1,0:T(8,128)(2,1)S(1)}, u32[]{:S(2)}, u32[]{:S(2)}) collective-permute-start(bf16[8,16,640]{2,1,0:T(8,128)(2,1)S(1)} %get-tuple-element.18), channel_id=1, source_target_pairs={{0,992},{32,0},{64,32},{96,64},{128,96},{160,128},{192,160},{224,1... | collective-permute-start | bytes 491528 | tf_op jit(solution)/shard_map/ppermute | solution.py:34
  38.1 4.6 %collective-permute-start.6 = (bf16[8,16,640]{2,1,0:T(8,128)(2,1)S(1)}, bf16[8,16,640]{2,1,0:T(8,128)(2,1)S(1)}, u32[]{:S(2)}, u32[]{:S(2)}) collective-permute-start(bf16[8,16,640]{2,1,0:T(8,128)(2,1)S(1)} %collective-permute-done.2), channel_id=1, source_target_pairs={{0,992},{32,0},{64,32},{96,64},{128,96},{160,128},{192,160},{224,1... | collective-permute-start | bytes 491528 | tf_op jit(solution)/shard_map/ppermute | solution.py:34
  42.7 3.4 collective-permute-start.7
  52.8 5.0 %collective-permute-start.10 = (bf16[8,16,640]{2,1,0:T(8,128)(2,1)S(1)}, bf16[8,16,640]{2,1,0:T(8,128)(2,1)S(1)}, u32[]{:S(2)}, u32[]{:S(2)}) collective-permute-start(bf16[8,16,640]{2,1,0:T(8,128)(2,1)S(1)} %collective-permute-done.6), channel_id=1, source_target_pairs={{0,992},{32,0},{64,32},{96,64},{128,96},{160,128},{192,160},{224,1... | collective-permute-start | bytes 491528 | tf_op jit(solution)/shard_map/ppermute | solution.py:34
  57.9 3.4 collective-permute-start.11
  61.4 3.9 collective-permute-done.11
  69.2 5.2 %collective-permute-start.15 = (bf16[8,16,640]{2,1,0:T(8,128)(2,1)S(1)}, bf16[8,16,640]{2,1,0:T(8,128)(2,1)S(1)}, u32[]{:S(2)}, u32[]{:S(2)}) collective-permute-start(bf16[8,16,640]{2,1,0:T(8,128)(2,1)S(1)} %collective-permute-done.10), channel_id=1, source_target_pairs={{0,992},{32,0},{64,32},{96,64},{128,96},{160,128},{192,160},{224,1... | collective-permute-start | bytes 491528 | tf_op jit(solution)/shard_map/ppermute | solution.py:34
  74.4 3.4 collective-permute-start.16
  77.9 5.4 %collective-permute-start.14 = (bf16[8,32,640]{2,1,0:T(8,128)(2,1)S(1)}, bf16[8,32,640]{2,1,0:T(8,128)(2,1)S(1)}, u32[]{:S(2)}, u32[]{:S(2)}) collective-permute-start(bf16[8,32,640]{2,1,0:T(8,128)(2,1)S(1)} %constant_dynamic-update-slice_fusion.8), channel_id=1, source_target_pairs={{0,16},{16,0},{1,17},{17,1},{2,18},{18,2},{3,19},{19,3},{4,20},{20... | collective-permute-start | bytes 983048 | tf_op jit(solution)/shard_map/ppermute | solution.py:46
  87.2 4.6 %collective-permute-start.19 = (bf16[8,16,640]{2,1,0:T(8,128)(2,1)S(1)}, bf16[8,16,640]{2,1,0:T(8,128)(2,1)S(1)}, u32[]{:S(2)}, u32[]{:S(2)}) collective-permute-start(bf16[8,16,640]{2,1,0:T(8,128)(2,1)S(1)} %collective-permute-done.15), channel_id=1, source_target_pairs={{0,992},{32,0},{64,32},{96,64},{128,96},{160,128},{192,160},{224,1... | collective-permute-start | bytes 491528 | tf_op jit(solution)/shard_map/ppermute | solution.py:34
  91.8 3.4 collective-permute-start.20
  95.7 3.2 collective-permute-done.20
  102.8 4.6 %collective-permute-start.23 = (bf16[8,16,640]{2,1,0:T(8,128)(2,1)S(1)}, bf16[8,16,640]{2,1,0:T(8,128)(2,1)}, u32[]{:S(2)}, u32[]{:S(2)}) collective-permute-start(bf16[8,16,640]{2,1,0:T(8,128)(2,1)S(1)} %collective-permute-done.19), channel_id=1, source_target_pairs={{0,992},{32,0},{64,32},{96,64},{128,96},{160,128},{192,160},{224,1... | collective-permute-start | bytes 491528 | tf_op jit(solution)/shard_map/ppermute | solution.py:34
  107.4 3.4 collective-permute-start.24
  116.3 4.6 %collective-permute-start.27 = (bf16[8,16,640]{2,1,0:T(8,128)(2,1)}, bf16[8,16,640]{2,1,0:T(8,128)(2,1)}, u32[]{:S(2)}, u32[]{:S(2)}) collective-permute-start(bf16[8,16,640]{2,1,0:T(8,128)(2,1)} %collective-permute-done.23), channel_id=1, source_target_pairs={{0,992},{32,0},{64,32},{96,64},{128,96},{160,128},{192,160},{224,1... | collective-permute-start | bytes 491528 | tf_op jit(solution)/shard_map/ppermute | solution.py:34
  122.5 3.4 collective-permute-start.28
  130.3 6.9 %all-to-all-start = ((bf16[16,2,2,8,1024]{4,1,3,2,0:T(2,128)(2,1)}), bf16[16,2,2,8,1024]{4,1,3,2,0:T(2,128)(2,1)S(1)}, u32[]{:S(2)}, u32[]{:S(2)}) async-start(bf16[16,2,2,8,1024]{4,1,3,2,0:T(2,128)(2,1)} %copy.6), calls=%async_computation | async-start | bytes 2097152 | tf_op jit(solution)/shard_map/all_to_all | solution.py:52
  144.5 4.6 %collective-permute-start.32 = (bf16[8,16,640]{2,1,0:T(8,128)(2,1)}, bf16[8,16,640]{2,1,0:T(8,128)(2,1)S(1)}, u32[]{:S(2)}, u32[]{:S(2)}) collective-permute-start(bf16[8,16,640]{2,1,0:T(8,128)(2,1)} %collective-permute-done.27), channel_id=1, source_target_pairs={{0,992},{32,0},{64,32},{96,64},{128,96},{160,128},{192,160},{224,1... | collective-permute-start | bytes 491528 | tf_op jit(solution)/shard_map/ppermute | solution.py:34
  149.0 3.4 collective-permute-start.33
  152.5 7.0 %collective-permute-start.31 = (bf16[8,32,640]{2,1,0:T(8,128)(2,1)S(1)}, bf16[8,32,640]{2,1,0:T(8,128)(2,1)S(1)}, u32[]{:S(2)}, u32[]{:S(2)}) collective-permute-start(bf16[8,32,640]{2,1,0:T(8,128)(2,1)S(1)} %constant_dynamic-update-slice_fusion.24), channel_id=1, source_target_pairs={{0,16},{16,0},{1,17},{17,1},{2,18},{18,2},{3,19},{19,3},{4,20},{20... | collective-permute-start | bytes 983048 | tf_op jit(solution)/shard_map/ppermute | solution.py:46
  164.0 4.6 %collective-permute-start.36 = (bf16[8,16,640]{2,1,0:T(8,128)(2,1)S(1)}, bf16[8,16,640]{2,1,0:T(8,128)(2,1)S(1)}, u32[]{:S(2)}, u32[]{:S(2)}) collective-permute-start(bf16[8,16,640]{2,1,0:T(8,128)(2,1)S(1)} %collective-permute-done.32), channel_id=1, source_target_pairs={{0,992},{32,0},{64,32},{96,64},{128,96},{160,128},{192,160},{224,1... | collective-permute-start | bytes 491528 | tf_op jit(solution)/shard_map/ppermute | solution.py:34
  168.6 3.4 collective-permute-start.37
  175.9 4.6 %collective-permute-start.40 = (bf16[8,16,640]{2,1,0:T(8,128)(2,1)S(1)}, bf16[8,16,640]{2,1,0:T(8,128)(2,1)S(1)}, u32[]{:S(2)}, u32[]{:S(2)}) collective-permute-start(bf16[8,16,640]{2,1,0:T(8,128)(2,1)S(1)} %collective-permute-done.36), channel_id=1, source_target_pairs={{0,992},{32,0},{64,32},{96,64},{128,96},{160,128},{192,160},{224,1... | collective-permute-start | bytes 491528 | tf_op jit(solution)/shard_map/ppermute | solution.py:34
  180.6 3.4 collective-permute-start.41
  197.8 4.6 %collective-permute-start.44 = (bf16[8,16,640]{2,1,0:T(8,128)(2,1)S(1)}, bf16[8,16,640]{2,1,0:T(8,128)(2,1)S(1)}, u32[]{:S(2)}, u32[]{:S(2)}) collective-permute-start(bf16[8,16,640]{2,1,0:T(8,128)(2,1)S(1)} %copy-done.2), channel_id=1, source_target_pairs={{0,992},{32,0},{64,32},{96,64},{128,96},{160,128},{192,160},{224,1... | collective-permute-start | bytes 491528 | tf_op jit(solution)/shard_map/ppermute | solution.py:34
  202.4 3.4 collective-permute-start.45
  211.9 4.0 collective-permute-start.47
  219.5 3.4 collective-permute-start.50
  223.5 5.6 %collective-permute-start.48 = (bf16[8,32,640]{2,1,0:T(8,128)(2,1)}, bf16[8,32,640]{2,1,0:T(8,128)(2,1)S(1)}, u32[]{:S(2)}, u32[]{:S(2)}) collective-permute-start(bf16[8,32,640]{2,1,0:T(8,128)(2,1)} %constant_dynamic-update-slice_fusion.40), channel_id=1, source_target_pairs={{0,16},{16,0},{1,17},{17,1},{2,18},{18,2},{3,19},{19,3},{4,20},{20... | collective-permute-start | bytes 983048 | tf_op jit(solution)/shard_map/ppermute | solution.py:46
  231.2 3.6 collective-permute-start.52
  237.7 3.3 collective-permute-start.54
  247.0 4.6 %collective-permute-start.55 = (bf16[8,16,640]{2,1,0:T(8,128)(2,1)}, bf16[8,16,640]{2,1,0:T(8,128)(2,1)}, u32[]{:S(2)}, u32[]{:S(2)}) collective-permute-start(bf16[8,16,640]{2,1,0:T(8,128)(2,1)} %collective-permute-done.51), channel_id=1, source_target_pairs={{0,32},{32,64},{64,96},{96,128},{128,160},{160,192},{192,224},{224... | collective-permute-start | bytes 491528 | tf_op jit(solution)/shard_map/ppermute | solution.py:31
  251.6 3.1 collective-permute-start.56
  254.7 3.4 collective-permute-start.57
  268.8 3.3 collective-permute-start.59
  273.0 6.9 %all-to-all-start.1 = ((bf16[16,2,2,8,1024]{4,1,3,2,0:T(2,128)(2,1)}), bf16[16,2,2,8,1024]{4,1,3,2,0:T(2,128)(2,1)S(1)}, u32[]{:S(2)}, u32[]{:S(2)}) async-start(bf16[16,2,2,8,1024]{4,1,3,2,0:T(2,128)(2,1)} %copy.8), calls=%async_computation.1 | async-start | bytes 2097152 | tf_op jit(solution)/shard_map/all_to_all | solution.py:52
  282.0 3.0 collective-permute-start.60
  285.6 3.5 collective-permute-start.61
  293.4 3.4 collective-permute-start.63
  298.9 6.7 %all-to-all-start.2 = ((bf16[16,2,2,8,1024]{4,1,3,2,0:T(2,128)(2,1)}), bf16[16,2,2,8,1024]{4,1,3,2,0:T(2,128)(2,1)}, u32[]{:S(2)}, u32[]{:S(2)}) async-start(bf16[16,2,2,8,1024]{4,1,3,2,0:T(2,128)(2,1)} %copy.10), calls=%async_computation.2 | async-start | bytes 2097152 | tf_op jit(solution)/shard_map/all_to_all | solution.py:52
  308.5 6.4 %collective-permute-start.65 = (bf16[8,32,640]{2,1,0:T(8,128)(2,1)}, bf16[8,32,640]{2,1,0:T(8,128)(2,1)S(1)}, u32[]{:S(2)}, u32[]{:S(2)}) collective-permute-start(bf16[8,32,640]{2,1,0:T(8,128)(2,1)} %constant_dynamic-update-slice_fusion.56), channel_id=1, source_target_pairs={{0,16},{16,0},{1,17},{17,1},{2,18},{18,2},{3,19},{19,3},{4,20},{20... | collective-permute-start | bytes 983048 | tf_op jit(solution)/shard_map/ppermute | solution.py:46
  316.8 3.0 fusion.3
  322.0 3.3 copy.12
  325.4 7.1 %all-to-all-start.3 = ((bf16[16,2,2,8,1024]{4,1,3,2,0:T(2,128)(2,1)}), bf16[16,2,2,8,1024]{4,1,3,2,0:T(2,128)(2,1)}, u32[]{:S(2)}, u32[]{:S(2)}) async-start(bf16[16,2,2,8,1024]{4,1,3,2,0:T(2,128)(2,1)} %copy.12), calls=%async_computation.3 | async-start | bytes 2097152 | tf_op jit(solution)/shard_map/all_to_all | solution.py:52
  337.0 12.8 %all-to-all-done.3 = bf16[16,2,2,8,1024]{4,1,3,2,0:T(2,128)(2,1)} async-done(((bf16[16,2,2,8,1024]{4,1,3,2,0:T(2,128)(2,1)}), bf16[16,2,2,8,1024]{4,1,3,2,0:T(2,128)(2,1)}, u32[]{:S(2)}, u32[]{:S(2)}) %all-to-all-start.3) | async-done | bytes 1048608 | tf_op jit(solution)/shard_map/all_to_all | solution.py:52
  356.7 56.3 %all_to_all.25 = bf16[2,64,1024]{2,0,1:T(2,128)(2,1)S(1)} all-to-all(bf16[2,64,1024]{2,0,1:T(2,128)(2,1)S(1)} %bitcast.564), channel_id=1, replica_groups=mesh['z'=32,'core'=2,'narrow'=16] {'z','core'}, dimensions={1} | all-to-all | bytes 524288 | tf_op jit(solution)/shard_map/all_to_all | solution.py:59
  (275 shorter events, 128.9 us)
Async XLA Ops:
  1.1 32.9 %collective-permute-start = (bf16[8,16,640]{2,1,0:T(8,128)(2,1)S(1)}, bf16[8,16,640]{2,1,0:T(8,128)(2,1)S(1)}, u32[]{:S(2)}, u32[]{:S(2)}) collective-permute-start(bf16[8,16,640]{2,1,0:T(8,128)(2,1)S(1)} %get-tuple-element.17), channel_id=1, source_target_pairs={{0,32},{32,64},{64,96},{96,128},{128,160},{160,192},{192,224},{224... | collective-permute-start | bytes 491528 | tf_op jit(solution)/shard_map/ppermute | solution.py:31
  5.5 28.6 %collective-permute-start.2 = (bf16[8,16,640]{2,1,0:T(8,128)(2,1)S(1)}, bf16[8,16,640]{2,1,0:T(8,128)(2,1)S(1)}, u32[]{:S(2)}, u32[]{:S(2)}) collective-permute-start(bf16[8,16,640]{2,1,0:T(8,128)(2,1)S(1)} %get-tuple-element.17), channel_id=1, source_target_pairs={{0,992},{32,0},{64,32},{96,64},{128,96},{160,128},{192,160},{224,1... | collective-permute-start | bytes 491528 | tf_op jit(solution)/shard_map/ppermute | solution.py:34
  22.3 11.8 %collective-permute-start.1 = (bf16[8,16,640]{2,1,0:T(8,128)(2,1)S(1)}, bf16[8,16,640]{2,1,0:T(8,128)(2,1)S(1)}, u32[]{:S(2)}, u32[]{:S(2)}) collective-permute-start(bf16[8,16,640]{2,1,0:T(8,128)(2,1)S(1)} %get-tuple-element.18), channel_id=1, source_target_pairs={{0,32},{32,64},{64,96},{96,128},{128,160},{160,192},{192,224},{224... | collective-permute-start | bytes 491528 | tf_op jit(solution)/shard_map/ppermute | solution.py:31
  34.2 11.8 %collective-permute-start.4 = (bf16[8,16,640]{2,1,0:T(8,128)(2,1)S(1)}, bf16[8,16,640]{2,1,0:T(8,128)(2,1)S(1)}, u32[]{:S(2)}, u32[]{:S(2)}) collective-permute-start(bf16[8,16,640]{2,1,0:T(8,128)(2,1)S(1)} %collective-permute-done), channel_id=1, source_target_pairs={{0,32},{32,64},{64,96},{96,128},{128,160},{160,192},{192,224},{224... | collective-permute-start | bytes 491528 | tf_op jit(solution)/shard_map/ppermute | solution.py:31
  49.0 12.3 %collective-permute-start.8 = (bf16[8,16,640]{2,1,0:T(8,128)(2,1)S(1)}, bf16[8,16,640]{2,1,0:T(8,128)(2,1)S(1)}, u32[]{:S(2)}, u32[]{:S(2)}) collective-permute-start(bf16[8,16,640]{2,1,0:T(8,128)(2,1)S(1)} %collective-permute-done.4), channel_id=1, source_target_pairs={{0,32},{32,64},{64,96},{96,128},{128,160},{160,192},{192,224},{224... | collective-permute-start | bytes 491528 | tf_op jit(solution)/shard_map/ppermute | solution.py:31
  65.3 12.5 %collective-permute-start.12 = (bf16[8,16,640]{2,1,0:T(8,128)(2,1)S(1)}, bf16[8,16,640]{2,1,0:T(8,128)(2,1)S(1)}, u32[]{:S(2)}, u32[]{:S(2)}) collective-permute-start(bf16[8,16,640]{2,1,0:T(8,128)(2,1)S(1)} %collective-permute-done.8), channel_id=1, source_target_pairs={{0,32},{32,64},{64,96},{96,128},{128,160},{160,192},{192,224},{224... | collective-permute-start | bytes 491528 | tf_op jit(solution)/shard_map/ppermute | solution.py:31
  69.2 16.0 %collective-permute-start.15 = (bf16[8,16,640]{2,1,0:T(8,128)(2,1)S(1)}, bf16[8,16,640]{2,1,0:T(8,128)(2,1)S(1)}, u32[]{:S(2)}, u32[]{:S(2)}) collective-permute-start(bf16[8,16,640]{2,1,0:T(8,128)(2,1)S(1)} %collective-permute-done.10), channel_id=1, source_target_pairs={{0,992},{32,0},{64,32},{96,64},{128,96},{160,128},{192,160},{224,1... | collective-permute-start | bytes 491528 | tf_op jit(solution)/shard_map/ppermute | solution.py:34
  74.4 10.8 %collective-permute-start.16 = (bf16[8,16,640]{2,1,0:T(8,128)(2,1)S(1)}, bf16[8,16,640]{2,1,0:T(8,128)(2,1)S(1)}, u32[]{:S(2)}, u32[]{:S(2)}) collective-permute-start(bf16[8,16,640]{2,1,0:T(8,128)(2,1)S(1)} %collective-permute-done.11), channel_id=1, source_target_pairs={{0,992},{32,0},{64,32},{96,64},{128,96},{160,128},{192,160},{224,1... | collective-permute-start | bytes 491528 | tf_op jit(solution)/shard_map/ppermute | solution.py:34
  77.9 48.1 %collective-permute-start.14 = (bf16[8,32,640]{2,1,0:T(8,128)(2,1)S(1)}, bf16[8,32,640]{2,1,0:T(8,128)(2,1)S(1)}, u32[]{:S(2)}, u32[]{:S(2)}) collective-permute-start(bf16[8,32,640]{2,1,0:T(8,128)(2,1)S(1)} %constant_dynamic-update-slice_fusion.8), channel_id=1, source_target_pairs={{0,16},{16,0},{1,17},{17,1},{2,18},{18,2},{3,19},{19,3},{4,20},{20... | collective-permute-start | bytes 983048 | tf_op jit(solution)/shard_map/ppermute | solution.py:46
  83.2 11.9 %collective-permute-start.17 = (bf16[8,16,640]{2,1,0:T(8,128)(2,1)S(1)}, bf16[8,16,640]{2,1,0:T(8,128)(2,1)S(1)}, u32[]{:S(2)}, u32[]{:S(2)}) collective-permute-start(bf16[8,16,640]{2,1,0:T(8,128)(2,1)S(1)} %collective-permute-done.12), channel_id=1, source_target_pairs={{0,32},{32,64},{64,96},{96,128},{128,160},{160,192},{192,224},{224... | collective-permute-start | bytes 491528 | tf_op jit(solution)/shard_map/ppermute | solution.py:31
  98.9 11.8 %collective-permute-start.21 = (bf16[8,16,640]{2,1,0:T(8,128)(2,1)S(1)}, bf16[8,16,640]{2,1,0:T(8,128)(2,1)}, u32[]{:S(2)}, u32[]{:S(2)}) collective-permute-start(bf16[8,16,640]{2,1,0:T(8,128)(2,1)S(1)} %collective-permute-done.17), channel_id=1, source_target_pairs={{0,32},{32,64},{64,96},{96,128},{128,160},{160,192},{192,224},{224... | collective-permute-start | bytes 491528 | tf_op jit(solution)/shard_map/ppermute | solution.py:31
  100.8 10.7 %collective-permute-start.22 = (bf16[8,16,640]{2,1,0:T(8,128)(2,1)S(1)}, bf16[8,16,640]{2,1,0:T(8,128)(2,1)}, u32[]{:S(2)}, u32[]{:S(2)}) collective-permute-start(bf16[8,16,640]{2,1,0:T(8,128)(2,1)S(1)} %collective-permute-done.18), channel_id=1, source_target_pairs={{0,32},{32,64},{64,96},{96,128},{128,160},{160,192},{192,224},{224... | collective-permute-start | bytes 491528 | tf_op jit(solution)/shard_map/ppermute | solution.py:31
  102.8 13.5 %collective-permute-start.23 = (bf16[8,16,640]{2,1,0:T(8,128)(2,1)S(1)}, bf16[8,16,640]{2,1,0:T(8,128)(2,1)}, u32[]{:S(2)}, u32[]{:S(2)}) collective-permute-start(bf16[8,16,640]{2,1,0:T(8,128)(2,1)S(1)} %collective-permute-done.19), channel_id=1, source_target_pairs={{0,992},{32,0},{64,32},{96,64},{128,96},{160,128},{192,160},{224,1... | collective-permute-start | bytes 491528 | tf_op jit(solution)/shard_map/ppermute | solution.py:34
  107.4 14.3 %collective-permute-start.24 = (bf16[8,16,640]{2,1,0:T(8,128)(2,1)S(1)}, bf16[8,16,640]{2,1,0:T(8,128)(2,1)}, u32[]{:S(2)}, u32[]{:S(2)}) collective-permute-start(bf16[8,16,640]{2,1,0:T(8,128)(2,1)S(1)} %collective-permute-done.20), channel_id=1, source_target_pairs={{0,992},{32,0},{64,32},{96,64},{128,96},{160,128},{192,160},{224,1... | collective-permute-start | bytes 491528 | tf_op jit(solution)/shard_map/ppermute | solution.py:34
  112.4 24.8 %collective-permute-start.25 = (bf16[8,16,640]{2,1,0:T(8,128)(2,1)}, bf16[8,16,640]{2,1,0:T(8,128)(2,1)}, u32[]{:S(2)}, u32[]{:S(2)}) collective-permute-start(bf16[8,16,640]{2,1,0:T(8,128)(2,1)} %collective-permute-done.21), channel_id=1, source_target_pairs={{0,32},{32,64},{64,96},{96,128},{128,160},{160,192},{192,224},{224... | collective-permute-start | bytes 491528 | tf_op jit(solution)/shard_map/ppermute | solution.py:31
  114.3 23.7 %collective-permute-start.26 = (bf16[8,16,640]{2,1,0:T(8,128)(2,1)}, bf16[8,16,640]{2,1,0:T(8,128)(2,1)}, u32[]{:S(2)}, u32[]{:S(2)}) collective-permute-start(bf16[8,16,640]{2,1,0:T(8,128)(2,1)} %collective-permute-done.22), channel_id=1, source_target_pairs={{0,32},{32,64},{64,96},{96,128},{128,160},{160,192},{192,224},{224... | collective-permute-start | bytes 491528 | tf_op jit(solution)/shard_map/ppermute | solution.py:31
  116.3 22.6 %collective-permute-start.27 = (bf16[8,16,640]{2,1,0:T(8,128)(2,1)}, bf16[8,16,640]{2,1,0:T(8,128)(2,1)}, u32[]{:S(2)}, u32[]{:S(2)}) collective-permute-start(bf16[8,16,640]{2,1,0:T(8,128)(2,1)} %collective-permute-done.23), channel_id=1, source_target_pairs={{0,992},{32,0},{64,32},{96,64},{128,96},{160,128},{192,160},{224,1... | collective-permute-start | bytes 491528 | tf_op jit(solution)/shard_map/ppermute | solution.py:34
  122.5 17.2 %collective-permute-start.28 = (bf16[8,16,640]{2,1,0:T(8,128)(2,1)}, bf16[8,16,640]{2,1,0:T(8,128)(2,1)}, u32[]{:S(2)}, u32[]{:S(2)}) collective-permute-start(bf16[8,16,640]{2,1,0:T(8,128)(2,1)} %collective-permute-done.24), channel_id=1, source_target_pairs={{0,992},{32,0},{64,32},{96,64},{128,96},{160,128},{192,160},{224,1... | collective-permute-start | bytes 491528 | tf_op jit(solution)/shard_map/ppermute | solution.py:34
  130.3 142.7 %all-to-all-start = ((bf16[16,2,2,8,1024]{4,1,3,2,0:T(2,128)(2,1)}), bf16[16,2,2,8,1024]{4,1,3,2,0:T(2,128)(2,1)S(1)}, u32[]{:S(2)}, u32[]{:S(2)}) async-start(bf16[16,2,2,8,1024]{4,1,3,2,0:T(2,128)(2,1)} %copy.6), calls=%async_computation | async-start | bytes 2097152 | tf_op jit(solution)/shard_map/all_to_all | solution.py:52
  140.6 11.8 %collective-permute-start.29 = (bf16[8,16,640]{2,1,0:T(8,128)(2,1)}, bf16[8,16,640]{2,1,0:T(8,128)(2,1)S(1)}, u32[]{:S(2)}, u32[]{:S(2)}) collective-permute-start(bf16[8,16,640]{2,1,0:T(8,128)(2,1)} %collective-permute-done.25), channel_id=1, source_target_pairs={{0,32},{32,64},{64,96},{96,128},{128,160},{160,192},{192,224},{224... | collective-permute-start | bytes 491528 | tf_op jit(solution)/shard_map/ppermute | solution.py:31
  144.5 17.0 %collective-permute-start.32 = (bf16[8,16,640]{2,1,0:T(8,128)(2,1)}, bf16[8,16,640]{2,1,0:T(8,128)(2,1)S(1)}, u32[]{:S(2)}, u32[]{:S(2)}) collective-permute-start(bf16[8,16,640]{2,1,0:T(8,128)(2,1)} %collective-permute-done.27), channel_id=1, source_target_pairs={{0,992},{32,0},{64,32},{96,64},{128,96},{160,128},{192,160},{224,1... | collective-permute-start | bytes 491528 | tf_op jit(solution)/shard_map/ppermute | solution.py:34
  149.0 12.4 %collective-permute-start.33 = (bf16[8,16,640]{2,1,0:T(8,128)(2,1)}, bf16[8,16,640]{2,1,0:T(8,128)(2,1)S(1)}, u32[]{:S(2)}, u32[]{:S(2)}) collective-permute-start(bf16[8,16,640]{2,1,0:T(8,128)(2,1)} %collective-permute-done.28), channel_id=1, source_target_pairs={{0,992},{32,0},{64,32},{96,64},{128,96},{160,128},{192,160},{224,1... | collective-permute-start | bytes 491528 | tf_op jit(solution)/shard_map/ppermute | solution.py:34
  152.5 32.7 %collective-permute-start.31 = (bf16[8,32,640]{2,1,0:T(8,128)(2,1)S(1)}, bf16[8,32,640]{2,1,0:T(8,128)(2,1)S(1)}, u32[]{:S(2)}, u32[]{:S(2)}) collective-permute-start(bf16[8,32,640]{2,1,0:T(8,128)(2,1)S(1)} %constant_dynamic-update-slice_fusion.24), channel_id=1, source_target_pairs={{0,16},{16,0},{1,17},{17,1},{2,18},{18,2},{3,19},{19,3},{4,20},{20... | collective-permute-start | bytes 983048 | tf_op jit(solution)/shard_map/ppermute | solution.py:46
  159.5 12.5 %collective-permute-start.34 = (bf16[8,16,640]{2,1,0:T(8,128)(2,1)S(1)}, bf16[8,16,640]{2,1,0:T(8,128)(2,1)S(1)}, u32[]{:S(2)}, u32[]{:S(2)}) collective-permute-start(bf16[8,16,640]{2,1,0:T(8,128)(2,1)S(1)} %collective-permute-done.29), channel_id=1, source_target_pairs={{0,32},{32,64},{64,96},{96,128},{128,160},{160,192},{192,224},{224... | collective-permute-start | bytes 491528 | tf_op jit(solution)/shard_map/ppermute | solution.py:31
  164.0 11.9 %collective-permute-start.36 = (bf16[8,16,640]{2,1,0:T(8,128)(2,1)S(1)}, bf16[8,16,640]{2,1,0:T(8,128)(2,1)S(1)}, u32[]{:S(2)}, u32[]{:S(2)}) collective-permute-start(bf16[8,16,640]{2,1,0:T(8,128)(2,1)S(1)} %collective-permute-done.32), channel_id=1, source_target_pairs={{0,992},{32,0},{64,32},{96,64},{128,96},{160,128},{192,160},{224,1... | collective-permute-start | bytes 491528 | tf_op jit(solution)/shard_map/ppermute | solution.py:34
  168.6 11.9 %collective-permute-start.37 = (bf16[8,16,640]{2,1,0:T(8,128)(2,1)S(1)}, bf16[8,16,640]{2,1,0:T(8,128)(2,1)S(1)}, u32[]{:S(2)}, u32[]{:S(2)}) collective-permute-start(bf16[8,16,640]{2,1,0:T(8,128)(2,1)S(1)} %collective-permute-done.33), channel_id=1, source_target_pairs={{0,992},{32,0},{64,32},{96,64},{128,96},{160,128},{192,160},{224,1... | collective-permute-start | bytes 491528 | tf_op jit(solution)/shard_map/ppermute | solution.py:34
  172.1 15.2 %collective-permute-start.39 = (bf16[8,16,640]{2,1,0:T(8,128)(2,1)S(1)}, bf16[8,16,640]{2,1,0:T(8,128)(2,1)}, u32[]{:S(2)}, u32[]{:S(2)}) collective-permute-start(bf16[8,16,640]{2,1,0:T(8,128)(2,1)S(1)} %collective-permute-done.35), channel_id=1, source_target_pairs={{0,32},{32,64},{64,96},{96,128},{128,160},{160,192},{192,224},{224... | collective-permute-start | bytes 491528 | tf_op jit(solution)/shard_map/ppermute | solution.py:31
  174.0 14.1 %collective-permute-start.38 = (bf16[8,16,640]{2,1,0:T(8,128)(2,1)S(1)}, bf16[8,16,640]{2,1,0:T(8,128)(2,1)}, u32[]{:S(2)}, u32[]{:S(2)}) collective-permute-start(bf16[8,16,640]{2,1,0:T(8,128)(2,1)S(1)} %collective-permute-done.34), channel_id=1, source_target_pairs={{0,32},{32,64},{64,96},{96,128},{128,160},{160,192},{192,224},{224... | collective-permute-start | bytes 491528 | tf_op jit(solution)/shard_map/ppermute | solution.py:31
  175.9 13.0 %collective-permute-start.40 = (bf16[8,16,640]{2,1,0:T(8,128)(2,1)S(1)}, bf16[8,16,640]{2,1,0:T(8,128)(2,1)S(1)}, u32[]{:S(2)}, u32[]{:S(2)}) collective-permute-start(bf16[8,16,640]{2,1,0:T(8,128)(2,1)S(1)} %collective-permute-done.36), channel_id=1, source_target_pairs={{0,992},{32,0},{64,32},{96,64},{128,96},{160,128},{192,160},{224,1... | collective-permute-start | bytes 491528 | tf_op jit(solution)/shard_map/ppermute | solution.py:34
  189.0 16.7 %collective-permute-start.42 = (bf16[8,16,640]{2,1,0:T(8,128)(2,1)}, bf16[8,16,640]{2,1,0:T(8,128)(2,1)}, u32[]{:S(2)}, u32[]{:S(2)}) collective-permute-start(bf16[8,16,640]{2,1,0:T(8,128)(2,1)} %collective-permute-done.38), channel_id=1, source_target_pairs={{0,32},{32,64},{64,96},{96,128},{128,160},{160,192},{192,224},{224... | collective-permute-start | bytes 491528 | tf_op jit(solution)/shard_map/ppermute | solution.py:31
  191.6 15.0 %collective-permute-start.43 = (bf16[8,16,640]{2,1,0:T(8,128)(2,1)}, bf16[8,16,640]{2,1,0:T(8,128)(2,1)}, u32[]{:S(2)}, u32[]{:S(2)}) collective-permute-start(bf16[8,16,640]{2,1,0:T(8,128)(2,1)} %collective-permute-done.39), channel_id=1, source_target_pairs={{0,32},{32,64},{64,96},{96,128},{128,160},{160,192},{192,224},{224... | collective-permute-start | bytes 491528 | tf_op jit(solution)/shard_map/ppermute | solution.py:31
  209.4 13.5 %collective-permute-start.46 = (bf16[8,16,640]{2,1,0:T(8,128)(2,1)}, bf16[8,16,640]{2,1,0:T(8,128)(2,1)S(1)}, u32[]{:S(2)}, u32[]{:S(2)}) collective-permute-start(bf16[8,16,640]{2,1,0:T(8,128)(2,1)} %collective-permute-done.42), channel_id=1, source_target_pairs={{0,32},{32,64},{64,96},{96,128},{128,160},{160,192},{192,224},{224... | collective-permute-start | bytes 491528 | tf_op jit(solution)/shard_map/ppermute | solution.py:31
  211.9 11.0 %collective-permute-start.47 = (bf16[8,16,640]{2,1,0:T(8,128)(2,1)}, bf16[8,16,640]{2,1,0:T(8,128)(2,1)S(1)}, u32[]{:S(2)}, u32[]{:S(2)}) collective-permute-start(bf16[8,16,640]{2,1,0:T(8,128)(2,1)} %collective-permute-done.43), channel_id=1, source_target_pairs={{0,32},{32,64},{64,96},{96,128},{128,160},{160,192},{192,224},{224... | collective-permute-start | bytes 491528 | tf_op jit(solution)/shard_map/ppermute | solution.py:31
  216.5 14.6 %collective-permute-start.49 = (bf16[8,16,640]{2,1,0:T(8,128)(2,1)S(1)}, bf16[8,16,640]{2,1,0:T(8,128)(2,1)S(1)}, u32[]{:S(2)}, u32[]{:S(2)}) collective-permute-start(bf16[8,16,640]{2,1,0:T(8,128)(2,1)S(1)} %collective-permute-done.44), channel_id=1, source_target_pairs={{0,992},{32,0},{64,32},{96,64},{128,96},{160,128},{192,160},{224,1... | collective-permute-start | bytes 491528 | tf_op jit(solution)/shard_map/ppermute | solution.py:34
  219.5 11.7 %collective-permute-start.50 = (bf16[8,16,640]{2,1,0:T(8,128)(2,1)S(1)}, bf16[8,16,640]{2,1,0:T(8,128)(2,1)S(1)}, u32[]{:S(2)}, u32[]{:S(2)}) collective-permute-start(bf16[8,16,640]{2,1,0:T(8,128)(2,1)S(1)} %collective-permute-done.45), channel_id=1, source_target_pairs={{0,992},{32,0},{64,32},{96,64},{128,96},{160,128},{192,160},{224,1... | collective-permute-start | bytes 491528 | tf_op jit(solution)/shard_map/ppermute | solution.py:34
  223.5 37.4 %collective-permute-start.48 = (bf16[8,32,640]{2,1,0:T(8,128)(2,1)}, bf16[8,32,640]{2,1,0:T(8,128)(2,1)S(1)}, u32[]{:S(2)}, u32[]{:S(2)}) collective-permute-start(bf16[8,32,640]{2,1,0:T(8,128)(2,1)} %constant_dynamic-update-slice_fusion.40), channel_id=1, source_target_pairs={{0,16},{16,0},{1,17},{17,1},{2,18},{18,2},{3,19},{19,3},{4,20},{20... | collective-permute-start | bytes 983048 | tf_op jit(solution)/shard_map/ppermute | solution.py:46
  229.1 11.9 %collective-permute-start.51 = (bf16[8,16,640]{2,1,0:T(8,128)(2,1)S(1)}, bf16[8,16,640]{2,1,0:T(8,128)(2,1)}, u32[]{:S(2)}, u32[]{:S(2)}) collective-permute-start(bf16[8,16,640]{2,1,0:T(8,128)(2,1)S(1)} %collective-permute-done.46), channel_id=1, source_target_pairs={{0,32},{32,64},{64,96},{96,128},{128,160},{160,192},{192,224},{224... | collective-permute-start | bytes 491528 | tf_op jit(solution)/shard_map/ppermute | solution.py:31
  231.2 10.7 %collective-permute-start.52 = (bf16[8,16,640]{2,1,0:T(8,128)(2,1)S(1)}, bf16[8,16,640]{2,1,0:T(8,128)(2,1)}, u32[]{:S(2)}, u32[]{:S(2)}) collective-permute-start(bf16[8,16,640]{2,1,0:T(8,128)(2,1)S(1)} %collective-permute-done.47), channel_id=1, source_target_pairs={{0,32},{32,64},{64,96},{96,128},{128,160},{160,192},{192,224},{224... | collective-permute-start | bytes 491528 | tf_op jit(solution)/shard_map/ppermute | solution.py:31
  247.0 19.6 %collective-permute-start.55 = (bf16[8,16,640]{2,1,0:T(8,128)(2,1)}, bf16[8,16,640]{2,1,0:T(8,128)(2,1)}, u32[]{:S(2)}, u32[]{:S(2)}) collective-permute-start(bf16[8,16,640]{2,1,0:T(8,128)(2,1)} %collective-permute-done.51), channel_id=1, source_target_pairs={{0,32},{32,64},{64,96},{96,128},{128,160},{160,192},{192,224},{224... | collective-permute-start | bytes 491528 | tf_op jit(solution)/shard_map/ppermute | solution.py:31
  251.6 15.8 %collective-permute-start.56 = (bf16[8,16,640]{2,1,0:T(8,128)(2,1)}, bf16[8,16,640]{2,1,0:T(8,128)(2,1)}, u32[]{:S(2)}, u32[]{:S(2)}) collective-permute-start(bf16[8,16,640]{2,1,0:T(8,128)(2,1)} %collective-permute-done.52), channel_id=1, source_target_pairs={{0,32},{32,64},{64,96},{96,128},{128,160},{160,192},{192,224},{224... | collective-permute-start | bytes 491528 | tf_op jit(solution)/shard_map/ppermute | solution.py:31
  254.7 17.5 %collective-permute-start.57 = (bf16[8,16,640]{2,1,0:T(8,128)(2,1)}, bf16[8,16,640]{2,1,0:T(8,128)(2,1)}, u32[]{:S(2)}, u32[]{:S(2)}) collective-permute-start(bf16[8,16,640]{2,1,0:T(8,128)(2,1)} %collective-permute-done.53), channel_id=1, source_target_pairs={{0,992},{32,0},{64,32},{96,64},{128,96},{160,128},{192,160},{224,1... | collective-permute-start | bytes 491528 | tf_op jit(solution)/shard_map/ppermute | solution.py:34
  258.1 21.9 %collective-permute-start.58 = (bf16[8,16,640]{2,1,0:T(8,128)(2,1)}, bf16[8,16,640]{2,1,0:T(8,128)(2,1)}, u32[]{:S(2)}, u32[]{:S(2)}) collective-permute-start(bf16[8,16,640]{2,1,0:T(8,128)(2,1)} %collective-permute-done.54), channel_id=1, source_target_pairs={{0,992},{32,0},{64,32},{96,64},{128,96},{160,128},{192,160},{224,1... | collective-permute-start | bytes 491528 | tf_op jit(solution)/shard_map/ppermute | solution.py:34
  268.8 22.3 %collective-permute-start.59 = (bf16[8,16,640]{2,1,0:T(8,128)(2,1)}, bf16[8,16,640]{2,1,0:T(8,128)(2,1)}, u32[]{:S(2)}, u32[]{:S(2)}) collective-permute-start(bf16[8,16,640]{2,1,0:T(8,128)(2,1)} %collective-permute-done.55), channel_id=1, source_target_pairs={{0,32},{32,64},{64,96},{96,128},{128,160},{160,192},{192,224},{224... | collective-permute-start | bytes 491528 | tf_op jit(solution)/shard_map/ppermute | solution.py:31
  273.0 25.9 %all-to-all-start.1 = ((bf16[16,2,2,8,1024]{4,1,3,2,0:T(2,128)(2,1)}), bf16[16,2,2,8,1024]{4,1,3,2,0:T(2,128)(2,1)S(1)}, u32[]{:S(2)}, u32[]{:S(2)}) async-start(bf16[16,2,2,8,1024]{4,1,3,2,0:T(2,128)(2,1)} %copy.8), calls=%async_computation.1 | async-start | bytes 2097152 | tf_op jit(solution)/shard_map/all_to_all | solution.py:52
  285.6 13.2 %collective-permute-start.61 = (bf16[8,16,640]{2,1,0:T(8,128)(2,1)}, bf16[8,16,640]{2,1,0:T(8,128)(2,1)S(1)}, u32[]{:S(2)}, u32[]{:S(2)}) collective-permute-start(bf16[8,16,640]{2,1,0:T(8,128)(2,1)} %collective-permute-done.57), channel_id=1, source_target_pairs={{0,992},{32,0},{64,32},{96,64},{128,96},{160,128},{192,160},{224,1... | collective-permute-start | bytes 491528 | tf_op jit(solution)/shard_map/ppermute | solution.py:34
  293.4 12.9 %collective-permute-start.63 = (bf16[8,16,640]{2,1,0:T(8,128)(2,1)}, bf16[8,16,640]{2,1,0:T(8,128)(2,1)}, u32[]{:S(2)}, u32[]{:S(2)}) collective-permute-start(bf16[8,16,640]{2,1,0:T(8,128)(2,1)} %collective-permute-done.59), channel_id=1, source_target_pairs={{0,32},{32,64},{64,96},{96,128},{128,160},{160,192},{192,224},{224... | collective-permute-start | bytes 491528 | tf_op jit(solution)/shard_map/ppermute | solution.py:31
  298.9 26.5 %all-to-all-start.2 = ((bf16[16,2,2,8,1024]{4,1,3,2,0:T(2,128)(2,1)}), bf16[16,2,2,8,1024]{4,1,3,2,0:T(2,128)(2,1)}, u32[]{:S(2)}, u32[]{:S(2)}) async-start(bf16[16,2,2,8,1024]{4,1,3,2,0:T(2,128)(2,1)} %copy.10), calls=%async_computation.2 | async-start | bytes 2097152 | tf_op jit(solution)/shard_map/all_to_all | solution.py:52
  325.4 24.5 %all-to-all-start.3 = ((bf16[16,2,2,8,1024]{4,1,3,2,0:T(2,128)(2,1)}), bf16[16,2,2,8,1024]{4,1,3,2,0:T(2,128)(2,1)}, u32[]{:S(2)}, u32[]{:S(2)}) async-start(bf16[16,2,2,8,1024]{4,1,3,2,0:T(2,128)(2,1)} %copy.12), calls=%async_computation.3 | async-start | bytes 2097152 | tf_op jit(solution)/shard_map/all_to_all | solution.py:52
  (36 other events, 401.2 us)

commit v10 on v6

--- a/solution.py
+++ b/solution.py
@@ -3,9 +3,6 @@
 from jax import lax
 from jax.sharding import Mesh
 from jax.sharding import PartitionSpec as P
-
-GROUPS = 4
-
 
 def body(trial_slab, ladder, range_irreps):
     chips = lax.axis_size("z")
@@ -33,10 +30,10 @@
             going_down = lax.ppermute(going_down, "z", down)
             arrivals.append((distance, going_down))
 
-    size = -(-len(arrivals) // GROUPS)
+    bounds = [0, 10, 20, 28, len(arrivals)]
     order, sums = [], []
-    for start in range(0, len(arrivals), size):
-        group = arrivals[start:start + size]
+    for start, end in zip(bounds[:-1], bounds[1:]):
+        group = arrivals[start:end]
         order += [r for r, _ in group]
         mine = jnp.stack([jnp.take(b, mine_irrep, axis=0) for _, b in group])
         theirs = jnp.stack([jnp.take(b, partner_irrep, axis=0) for _, b in group])

time: 336 us -> 334 us (level)
  other arithmetic: 37.8 us -> 29.9 us
  local copies, waits for them, and re-layouts: 22.4 us -> 26.2 us
    unnamed x28 -> x25, other arithmetic: 24.9 us -> 17.6 us
    all_to_all x4, waiting for transfers between devices: 11.8 us -> 7.59 us  [body(): lax.all_to_all(partial, 'narrow', split_axis=0, concat_axis=0, tiled=True)]
    reshape x8, local copies, waits for them, and re-layouts: 17.2 us -> 21.2 us  [body(): products.astype(jnp.bfloat16)]
    ppermute x15, waiting for transfers between devices: 0.04 us -> 3.67 us  [body(): going_down = lax.ppermute(going_down, 'z', down)]
  transfers between devices with their start and end apart: 39 -> 39, of which waited for: 11 -> 16; matrix products, arithmetic and copies ran while one was open for 19% -> 18% of each run, Pallas kernels for 0% -> 0%
where the time goes in v10:
time: 334 us; the launch traced here: 331 us
  starting transfers between devices  163 us (49%)
  blocking collectives  58.1 us (17%)
  waiting for transfers between devices  39.6 us (12%)
  other arithmetic  29.9 us (9%)
  local copies, waits for them, and re-layouts  26.2 us (8%)
  matrix products  9.99 us (3%)
  between operations  4.56 us (1%)
    ppermute x15, starting transfers between devices, body(): going_down = lax.ppermute(going_down, 'z', down)  82.9 us
    all_to_all x1, blocking collectives, body(): lax.all_to_all(by_device, ('z', 'core'), split_axis=1, concat_axis=1, til...  58.1 us
    ppermute x16, starting transfers between devices, body(): going_up = lax.ppermute(going_up, 'z', up)  33.2 us
    ppermute x16, waiting for transfers between devices, body(): going_up = lax.ppermute(going_up, 'z', up)  27.3 us
    all_to_all x4, starting transfers between devices, body(): lax.all_to_all(partial, 'narrow', split_axis=0, concat_axis=0, tiled=True)  24.5 us
    ppermute x4, starting transfers between devices, body(): received = lax.ppermute(theirs, 'core', [(0, 1), (1, 0)])  22.4 us
    reshape x8, local copies, waits for them, and re-layouts, body(): products.astype(jnp.bfloat16)  21.2 us
    unnamed x25, other arithmetic  17.6 us
  transfers between devices with their start and end apart: 39, of which 16 were waited for; matrix products, arithmetic and copies ran while one was open for 18% of the time, Pallas kernels for 0%

profile of v10, /device:TPU:1, one launch (start us, length us, event | category | flops | bytes accessed | tf_op | source)
XLA Modules:
  0.0 331.3 jit_solution(14492732285797509310)
XLA Ops:
  0.0 4.5 %collective-permute-start = (bf16[8,32,640]{2,1,0:T(8,128)(2,1)}, bf16[8,32,640]{2,1,0:T(8,128)(2,1)S(1)}, u32[]{:S(2)}, u32[]{:S(2)}) collective-permute-start(bf16[8,32,640]{2,1,0:T(8,128)(2,1)} %param.6), channel_id=1, source_target_pairs={{0,32},{32,64},{64,96},{96,128},{128,160},{160,192},{192,224},{224... | collective-permute-start | bytes 983048 | tf_op jit(solution)/shard_map/ppermute | solution.py:27
  4.5 16.8 %collective-permute-start.1 = (bf16[8,32,640]{2,1,0:T(8,128)(2,1)}, bf16[8,32,640]{2,1,0:T(8,128)(2,1)S(1)}, u32[]{:S(2)}, u32[]{:S(2)}) collective-permute-start(bf16[8,32,640]{2,1,0:T(8,128)(2,1)} %param.6), channel_id=1, source_target_pairs={{0,992},{32,0},{64,32},{96,64},{128,96},{160,128},{192,160},{224,1... | collective-permute-start | bytes 983048 | tf_op jit(solution)/shard_map/ppermute | solution.py:30
  21.3 5.7 %collective-permute-done = bf16[8,32,640]{2,1,0:T(8,128)(2,1)S(1)} collective-permute-done((bf16[8,32,640]{2,1,0:T(8,128)(2,1)}, bf16[8,32,640]{2,1,0:T(8,128)(2,1)S(1)}, u32[]{:S(2)}, u32[]{:S(2)}) %collective-permute-start) | collective-permute-done | bytes 327712 | tf_op jit(solution)/shard_map/ppermute | solution.py:27
  28.9 4.6 %collective-permute-start.3 = (bf16[8,32,640]{2,1,0:T(8,128)(2,1)S(1)}, bf16[8,32,640]{2,1,0:T(8,128)(2,1)S(1)}, u32[]{:S(2)}, u32[]{:S(2)}) collective-permute-start(bf16[8,32,640]{2,1,0:T(8,128)(2,1)S(1)} %collective-permute-done.1), channel_id=1, source_target_pairs={{0,992},{32,0},{64,32},{96,64},{128,96},{160,128},{192,160},{224,1... | collective-permute-start | bytes 983048 | tf_op jit(solution)/shard_map/ppermute | solution.py:30
  33.5 4.6 %collective-permute-done.2 = bf16[8,32,640]{2,1,0:T(8,128)(2,1)S(1)} collective-permute-done((bf16[8,32,640]{2,1,0:T(8,128)(2,1)S(1)}, bf16[8,32,640]{2,1,0:T(8,128)(2,1)S(1)}, u32[]{:S(2)}, u32[]{:S(2)}) %collective-permute-start.2) | collective-permute-done | bytes 327712 | tf_op jit(solution)/shard_map/ppermute | solution.py:27
  40.0 4.6 %collective-permute-start.5 = (bf16[8,32,640]{2,1,0:T(8,128)(2,1)S(1)}, bf16[8,32,640]{2,1,0:T(8,128)(2,1)S(1)}, u32[]{:S(2)}, u32[]{:S(2)}) collective-permute-start(bf16[8,32,640]{2,1,0:T(8,128)(2,1)S(1)} %collective-permute-done.3), channel_id=1, source_target_pairs={{0,992},{32,0},{64,32},{96,64},{128,96},{160,128},{192,160},{224,1... | collective-permute-start | bytes 983048 | tf_op jit(solution)/shard_map/ppermute | solution.py:30
  44.6 3.7 %collective-permute-done.4 = bf16[8,32,640]{2,1,0:T(8,128)(2,1)S(1)} collective-permute-done((bf16[8,32,640]{2,1,0:T(8,128)(2,1)S(1)}, bf16[8,32,640]{2,1,0:T(8,128)(2,1)S(1)}, u32[]{:S(2)}, u32[]{:S(2)}) %collective-permute-start.4) | collective-permute-done | bytes 327712 | tf_op jit(solution)/shard_map/ppermute | solution.py:27
  55.5 4.6 %collective-permute-start.7 = (bf16[8,32,640]{2,1,0:T(8,128)(2,1)S(1)}, bf16[8,32,640]{2,1,0:T(8,128)(2,1)S(1)}, u32[]{:S(2)}, u32[]{:S(2)}) collective-permute-start(bf16[8,32,640]{2,1,0:T(8,128)(2,1)S(1)} %collective-permute-done.5), channel_id=1, source_target_pairs={{0,992},{32,0},{64,32},{96,64},{128,96},{160,128},{192,160},{224,1... | collective-permute-start | bytes 983048 | tf_op jit(solution)/shard_map/ppermute | solution.py:30
  60.9 1.9 collective-permute-start.8
  64.0 5.0 %collective-permute-start.10 = (bf16[8,32,640]{2,1,0:T(8,128)(2,1)S(1)}, bf16[8,32,640]{2,1,0:T(8,128)(2,1)S(1)}, u32[]{:S(2)}, u32[]{:S(2)}) collective-permute-start(bf16[8,32,640]{2,1,0:T(8,128)(2,1)S(1)} %collective-permute-done.7), channel_id=1, source_target_pairs={{0,992},{32,0},{64,32},{96,64},{128,96},{160,128},{192,160},{224,1... | collective-permute-start | bytes 983048 | tf_op jit(solution)/shard_map/ppermute | solution.py:30
  73.1 5.0 %collective-permute-start.12 = (bf16[8,32,640]{2,1,0:T(8,128)(2,1)S(1)}, bf16[8,32,640]{2,1,0:T(8,128)(2,1)S(1)}, u32[]{:S(2)}, u32[]{:S(2)}) collective-permute-start(bf16[8,32,640]{2,1,0:T(8,128)(2,1)S(1)} %collective-permute-done.10), channel_id=1, source_target_pairs={{0,992},{32,0},{64,32},{96,64},{128,96},{160,128},{192,160},{224,1... | collective-permute-start | bytes 983048 | tf_op jit(solution)/shard_map/ppermute | solution.py:30
  82.1 5.0 %collective-permute-start.14 = (bf16[8,32,640]{2,1,0:T(8,128)(2,1)S(1)}, bf16[8,32,640]{2,1,0:T(8,128)(2,1)S(1)}, u32[]{:S(2)}, u32[]{:S(2)}) collective-permute-start(bf16[8,32,640]{2,1,0:T(8,128)(2,1)S(1)} %collective-permute-done.12), channel_id=1, source_target_pairs={{0,992},{32,0},{64,32},{96,64},{128,96},{160,128},{192,160},{224,1... | collective-permute-start | bytes 983048 | tf_op jit(solution)/shard_map/ppermute | solution.py:30
  87.1 9.4 %collective-permute-start.9 = (bf16[10,32,640]{2,1,0:T(8,128)(2,1)S(1)}, bf16[10,32,640]{2,1,0:T(8,128)(2,1)S(1)}, u32[]{:S(2)}, u32[]{:S(2)}) collective-permute-start(bf16[10,32,640]{2,1,0:T(8,128)(2,1)S(1)} %get-tuple-element.18), channel_id=1, source_target_pairs={{0,16},{16,0},{1,17},{17,1},{2,18},{18,2},{3,19},{19,3},{4,20},{20... | collective-permute-start | bytes 1228808 | tf_op jit(solution)/shard_map/ppermute | solution.py:40
  96.5 1.9 collective-permute-start.15
  99.8 4.6 %collective-permute-start.16 = (bf16[8,32,640]{2,1,0:T(8,128)(2,1)S(1)}, bf16[8,32,640]{2,1,0:T(8,128)(2,1)}, u32[]{:S(2)}, u32[]{:S(2)}) collective-permute-start(bf16[8,32,640]{2,1,0:T(8,128)(2,1)S(1)} %collective-permute-done.14), channel_id=1, source_target_pairs={{0,992},{32,0},{64,32},{96,64},{128,96},{160,128},{192,160},{224,1... | collective-permute-start | bytes 983048 | tf_op jit(solution)/shard_map/ppermute | solution.py:30
  105.0 4.0 %collective-permute-done.15 = bf16[8,32,640]{2,1,0:T(8,128)(2,1)} collective-permute-done((bf16[8,32,640]{2,1,0:T(8,128)(2,1)S(1)}, bf16[8,32,640]{2,1,0:T(8,128)(2,1)}, u32[]{:S(2)}, u32[]{:S(2)}) %collective-permute-start.15) | collective-permute-done | bytes 327712 | tf_op jit(solution)/shard_map/ppermute | solution.py:27
  110.9 2.3 fusion
  113.3 3.1 reshape.24
  116.3 2.4 copy.6
  118.7 6.8 %all-to-all-start = ((bf16[16,2,2,10,1024]{4,1,3,2,0:T(2,128)(2,1)}), bf16[16,2,2,10,1024]{4,1,3,2,0:T(2,128)(2,1)S(1)}, u32[]{:S(2)}, u32[]{:S(2)}) async-start(bf16[16,2,2,10,1024]{4,1,3,2,0:T(2,128)(2,1)} %copy.6), calls=%async_computation | async-start | bytes 2621440 | tf_op jit(solution)/shard_map/all_to_all | solution.py:46
  125.5 4.6 %collective-permute-start.18 = (bf16[8,32,640]{2,1,0:T(8,128)(2,1)}, bf16[8,32,640]{2,1,0:T(8,128)(2,1)S(1)}, u32[]{:S(2)}, u32[]{:S(2)}) collective-permute-start(bf16[8,32,640]{2,1,0:T(8,128)(2,1)} %collective-permute-done.16), channel_id=1, source_target_pairs={{0,992},{32,0},{64,32},{96,64},{128,96},{160,128},{192,160},{224,1... | collective-permute-start | bytes 983048 | tf_op jit(solution)/shard_map/ppermute | solution.py:30
  136.0 5.2 %collective-permute-start.21 = (bf16[8,32,640]{2,1,0:T(8,128)(2,1)S(1)}, bf16[8,32,640]{2,1,0:T(8,128)(2,1)S(1)}, u32[]{:S(2)}, u32[]{:S(2)}) collective-permute-start(bf16[8,32,640]{2,1,0:T(8,128)(2,1)S(1)} %collective-permute-done.18), channel_id=1, source_target_pairs={{0,992},{32,0},{64,32},{96,64},{128,96},{160,128},{192,160},{224,1... | collective-permute-start | bytes 983048 | tf_op jit(solution)/shard_map/ppermute | solution.py:30
  146.8 4.6 %collective-permute-start.23 = (bf16[8,32,640]{2,1,0:T(8,128)(2,1)S(1)}, bf16[8,32,640]{2,1,0:T(8,128)(2,1)S(1)}, u32[]{:S(2)}, u32[]{:S(2)}) collective-permute-start(bf16[8,32,640]{2,1,0:T(8,128)(2,1)S(1)} %collective-permute-done.21), channel_id=1, source_target_pairs={{0,992},{32,0},{64,32},{96,64},{128,96},{160,128},{192,160},{224,1... | collective-permute-start | bytes 983048 | tf_op jit(solution)/shard_map/ppermute | solution.py:30
  152.0 5.3 %collective-permute-start.20 = (bf16[10,32,640]{2,1,0:T(8,128)(2,1)}, bf16[10,32,640]{2,1,0:T(8,128)(2,1)S(1)}, u32[]{:S(2)}, u32[]{:S(2)}) collective-permute-start(bf16[10,32,640]{2,1,0:T(8,128)(2,1)} %get-tuple-element.38), channel_id=1, source_target_pairs={{0,16},{16,0},{1,17},{17,1},{2,18},{18,2},{3,19},{19,3},{4,20},{20... | collective-permute-start | bytes 1228808 | tf_op jit(solution)/shard_map/ppermute | solution.py:40
  157.3 1.9 collective-permute-start.24
  159.9 4.6 %collective-permute-start.25 = (bf16[8,32,640]{2,1,0:T(8,128)(2,1)S(1)}, bf16[8,32,640]{2,1,0:T(8,128)(2,1)}, u32[]{:S(2)}, u32[]{:S(2)}) collective-permute-start(bf16[8,32,640]{2,1,0:T(8,128)(2,1)S(1)} %collective-permute-done.23), channel_id=1, source_target_pairs={{0,992},{32,0},{64,32},{96,64},{128,96},{160,128},{192,160},{224,1... | collective-permute-start | bytes 983048 | tf_op jit(solution)/shard_map/ppermute | solution.py:30
  165.1 4.6 %collective-permute-done.24 = bf16[8,32,640]{2,1,0:T(8,128)(2,1)} collective-permute-done((bf16[8,32,640]{2,1,0:T(8,128)(2,1)S(1)}, bf16[8,32,640]{2,1,0:T(8,128)(2,1)}, u32[]{:S(2)}, u32[]{:S(2)}) %collective-permute-start.24) | collective-permute-done | bytes 327712 | tf_op jit(solution)/shard_map/ppermute | solution.py:27
  171.7 3.3 fusion.1
  175.0 4.0 %reshape.25 = bf16[16,2,2,10,1024]{4,1,0,3,2:T(2,128)(2,1)} reshape(bf16[32,2,10,1024]{3,0,2,1:T(8,128)(2,1)} %fusion.1) | data formatting | bytes 2621440 | tf_op jit(solution)/shard_map/reshape | solution.py:43
  178.9 3.6 %copy.8 = bf16[16,2,2,10,1024]{4,1,3,2,0:T(2,128)(2,1)} copy(bf16[16,2,2,10,1024]{4,1,0,3,2:T(2,128)(2,1)} %reshape.25) | data formatting | bytes 2621440 | tf_op jit(solution)/shard_map/reshape | solution.py:43
  182.5 4.6 %collective-permute-start.27 = (bf16[8,32,640]{2,1,0:T(8,128)(2,1)}, bf16[8,32,640]{2,1,0:T(8,128)(2,1)}, u32[]{:S(2)}, u32[]{:S(2)}) collective-permute-start(bf16[8,32,640]{2,1,0:T(8,128)(2,1)} %collective-permute-done.25), channel_id=1, source_target_pairs={{0,992},{32,0},{64,32},{96,64},{128,96},{160,128},{192,160},{224,1... | collective-permute-start | bytes 983048 | tf_op jit(solution)/shard_map/ppermute | solution.py:30
  187.1 6.5 %all-to-all-start.1 = ((bf16[16,2,2,10,1024]{4,1,3,2,0:T(2,128)(2,1)}), bf16[16,2,2,10,1024]{4,1,3,2,0:T(2,128)(2,1)}, u32[]{:S(2)}, u32[]{:S(2)}) async-start(bf16[16,2,2,10,1024]{4,1,3,2,0:T(2,128)(2,1)} %copy.8), calls=%async_computation.1 | async-start | bytes 2621440 | tf_op jit(solution)/shard_map/all_to_all | solution.py:46
  199.2 4.6 %collective-permute-start.30 = (bf16[8,32,640]{2,1,0:T(8,128)(2,1)}, bf16[8,32,640]{2,1,0:T(8,128)(2,1)S(1)}, u32[]{:S(2)}, u32[]{:S(2)}) collective-permute-start(bf16[8,32,640]{2,1,0:T(8,128)(2,1)} %collective-permute-done.27), channel_id=1, source_target_pairs={{0,992},{32,0},{64,32},{96,64},{128,96},{160,128},{192,160},{224,1... | collective-permute-start | bytes 983048 | tf_op jit(solution)/shard_map/ppermute | solution.py:30
  208.0 4.5 %collective-permute-start.29 = (bf16[8,32,640]{2,1,0:T(8,128)(2,1)}, bf16[8,32,640]{2,1,0:T(8,128)(2,1)S(1)}, u32[]{:S(2)}, u32[]{:S(2)}) collective-permute-start(bf16[8,32,640]{2,1,0:T(8,128)(2,1)} %get-tuple-element.58), channel_id=1, source_target_pairs={{0,16},{16,0},{1,17},{17,1},{2,18},{18,2},{3,19},{19,3},{4,20},{20... | collective-permute-start | bytes 983048 | tf_op jit(solution)/shard_map/ppermute | solution.py:40
  212.5 1.9 collective-permute-start.31
  214.4 4.8 %collective-permute-start.32 = (bf16[8,32,640]{2,1,0:T(8,128)(2,1)S(1)}, bf16[8,32,640]{2,1,0:T(8,128)(2,1)}, u32[]{:S(2)}, u32[]{:S(2)}) collective-permute-start(bf16[8,32,640]{2,1,0:T(8,128)(2,1)S(1)} %collective-permute-done.30), channel_id=1, source_target_pairs={{0,992},{32,0},{64,32},{96,64},{128,96},{160,128},{192,160},{224,1... | collective-permute-start | bytes 983048 | tf_op jit(solution)/shard_map/ppermute | solution.py:30
  219.2 3.0 fusion.2
  222.2 2.3 reshape.26
  224.4 3.3 copy.10
  229.7 6.7 %all-to-all-start.2 = ((bf16[16,2,2,8,1024]{4,1,3,2,0:T(2,128)(2,1)}), bf16[16,2,2,8,1024]{4,1,3,2,0:T(2,128)(2,1)}, u32[]{:S(2)}, u32[]{:S(2)}) async-start(bf16[16,2,2,8,1024]{4,1,3,2,0:T(2,128)(2,1)} %copy.10), calls=%async_computation.2 | async-start | bytes 2097152 | tf_op jit(solution)/shard_map/all_to_all | solution.py:46
  237.3 2.3 collective-permute-done.33
  240.5 3.3 %collective-permute-start.34 = (bf16[4,32,640]{2,1,0:T(8,128)(2,1)S(1)}, bf16[4,32,640]{2,1,0:T(8,128)(2,1)S(1)}, u32[]{:S(2)}, u32[]{:S(2)}) collective-permute-start(bf16[4,32,640]{2,1,0:T(8,128)(2,1)S(1)} %pad_maximum_fusion.1), channel_id=1, source_target_pairs={{0,16},{16,0},{1,17},{17,1},{2,18},{18,2},{3,19},{19,3},{4,20},{20... | collective-permute-start | bytes 491528 | tf_op jit(solution)/shard_map/ppermute | solution.py:40
  249.0 3.6 %all-to-all-done.2 = bf16[16,2,2,8,1024]{4,1,3,2,0:T(2,128)(2,1)} async-done(((bf16[16,2,2,8,1024]{4,1,3,2,0:T(2,128)(2,1)}), bf16[16,2,2,8,1024]{4,1,3,2,0:T(2,128)(2,1)}, u32[]{:S(2)}, u32[]{:S(2)}) %all-to-all-start.2) | async-done | bytes 1048608 | tf_op jit(solution)/shard_map/all_to_all | solution.py:46
  252.5 4.6 %all-to-all-start.3 = ((bf16[16,2,2,4,1024]{4,1,3,2,0:T(2,128)(2,1)}), bf16[16,2,2,4,1024]{4,1,3,2,0:T(2,128)(2,1)S(1)}, u32[]{:S(2)}, u32[]{:S(2)}) async-start(bf16[16,2,2,4,1024]{4,1,3,2,0:T(2,128)(2,1)} %copy.12), calls=%async_computation.3 | async-start | bytes 1048576 | tf_op jit(solution)/shard_map/all_to_all | solution.py:46
  258.5 2.5 reduce_sum.49
  261.0 2.2 reduce_sum.50
  263.3 4.0 %all-to-all-done.3 = bf16[16,2,2,4,1024]{4,1,3,2,0:T(2,128)(2,1)S(1)} async-done(((bf16[16,2,2,4,1024]{4,1,3,2,0:T(2,128)(2,1)}), bf16[16,2,2,4,1024]{4,1,3,2,0:T(2,128)(2,1)S(1)}, u32[]{:S(2)}, u32[]{:S(2)}) %all-to-all-start.3) | async-done | bytes 524320 | tf_op jit(solution)/shard_map/all_to_all | solution.py:46
  272.4 58.1 %all_to_all.25 = bf16[2,64,1024]{2,0,1:T(2,128)(2,1)S(1)} all-to-all(bf16[2,64,1024]{2,0,1:T(2,128)(2,1)S(1)} %bitcast.121), channel_id=1, replica_groups=mesh['z'=32,'core'=2,'narrow'=16] {'z','core'}, dimensions={1} | all-to-all | bytes 524288 | tf_op jit(solution)/shard_map/all_to_all | solution.py:53
  (100 shorter events, 62.2 us)
Async XLA Ops:
  0.0 110.9 %copy-start = (bf16[1024,640]{1,0:T(8,128)(2,1)S(1)}, bf16[1024,640]{1,0:T(8,128)(2,1)}, u32[]{:S(2)}) copy-start(bf16[1024,640]{1,0:T(8,128)(2,1)} %param.7) | copy-start | bytes 3932164
  0.0 27.0 %collective-permute-start = (bf16[8,32,640]{2,1,0:T(8,128)(2,1)}, bf16[8,32,640]{2,1,0:T(8,128)(2,1)S(1)}, u32[]{:S(2)}, u32[]{:S(2)}) collective-permute-start(bf16[8,32,640]{2,1,0:T(8,128)(2,1)} %param.6), channel_id=1, source_target_pairs={{0,32},{32,64},{64,96},{96,128},{128,160},{160,192},{192,224},{224... | collective-permute-start | bytes 983048 | tf_op jit(solution)/shard_map/ppermute | solution.py:27
  4.5 24.4 %collective-permute-start.1 = (bf16[8,32,640]{2,1,0:T(8,128)(2,1)}, bf16[8,32,640]{2,1,0:T(8,128)(2,1)S(1)}, u32[]{:S(2)}, u32[]{:S(2)}) collective-permute-start(bf16[8,32,640]{2,1,0:T(8,128)(2,1)} %param.6), channel_id=1, source_target_pairs={{0,992},{32,0},{64,32},{96,64},{128,96},{160,128},{192,160},{224,1... | collective-permute-start | bytes 983048 | tf_op jit(solution)/shard_map/ppermute | solution.py:30
  27.0 6.5 %copy-start.1 = (bf16[8,32,640]{2,1,0:T(8,128)(2,1)}, bf16[8,32,640]{2,1,0:T(8,128)(2,1)S(1)}, u32[]{:S(2)}) copy-start(bf16[8,32,640]{2,1,0:T(8,128)(2,1)S(1)} %collective-permute-done) | copy-start | bytes 983044
  27.0 11.1 %collective-permute-start.2 = (bf16[8,32,640]{2,1,0:T(8,128)(2,1)S(1)}, bf16[8,32,640]{2,1,0:T(8,128)(2,1)S(1)}, u32[]{:S(2)}, u32[]{:S(2)}) collective-permute-start(bf16[8,32,640]{2,1,0:T(8,128)(2,1)S(1)} %collective-permute-done), channel_id=1, source_target_pairs={{0,32},{32,64},{64,96},{96,128},{128,160},{160,192},{192,224},{224... | collective-permute-start | bytes 983048 | tf_op jit(solution)/shard_map/ppermute | solution.py:27
  28.9 11.1 %collective-permute-start.3 = (bf16[8,32,640]{2,1,0:T(8,128)(2,1)S(1)}, bf16[8,32,640]{2,1,0:T(8,128)(2,1)S(1)}, u32[]{:S(2)}, u32[]{:S(2)}) collective-permute-start(bf16[8,32,640]{2,1,0:T(8,128)(2,1)S(1)} %collective-permute-done.1), channel_id=1, source_target_pairs={{0,992},{32,0},{64,32},{96,64},{128,96},{160,128},{192,160},{224,1... | collective-permute-start | bytes 983048 | tf_op jit(solution)/shard_map/ppermute | solution.py:30
  38.1 10.3 %collective-permute-start.4 = (bf16[8,32,640]{2,1,0:T(8,128)(2,1)S(1)}, bf16[8,32,640]{2,1,0:T(8,128)(2,1)S(1)}, u32[]{:S(2)}, u32[]{:S(2)}) collective-permute-start(bf16[8,32,640]{2,1,0:T(8,128)(2,1)S(1)} %collective-permute-done.2), channel_id=1, source_target_pairs={{0,32},{32,64},{64,96},{96,128},{128,160},{160,192},{192,224},{224... | collective-permute-start | bytes 983048 | tf_op jit(solution)/shard_map/ppermute | solution.py:27
  40.0 15.5 %collective-permute-start.5 = (bf16[8,32,640]{2,1,0:T(8,128)(2,1)S(1)}, bf16[8,32,640]{2,1,0:T(8,128)(2,1)S(1)}, u32[]{:S(2)}, u32[]{:S(2)}) collective-permute-start(bf16[8,32,640]{2,1,0:T(8,128)(2,1)S(1)} %collective-permute-done.3), channel_id=1, source_target_pairs={{0,992},{32,0},{64,32},{96,64},{128,96},{160,128},{192,160},{224,1... | collective-permute-start | bytes 983048 | tf_op jit(solution)/shard_map/ppermute | solution.py:30
  48.3 12.6 %collective-permute-start.6 = (bf16[8,32,640]{2,1,0:T(8,128)(2,1)S(1)}, bf16[8,32,640]{2,1,0:T(8,128)(2,1)S(1)}, u32[]{:S(2)}, u32[]{:S(2)}) collective-permute-start(bf16[8,32,640]{2,1,0:T(8,128)(2,1)S(1)} %collective-permute-done.4), channel_id=1, source_target_pairs={{0,32},{32,64},{64,96},{96,128},{128,160},{160,192},{192,224},{224... | collective-permute-start | bytes 983048 | tf_op jit(solution)/shard_map/ppermute | solution.py:27
  55.5 8.6 %collective-permute-start.7 = (bf16[8,32,640]{2,1,0:T(8,128)(2,1)S(1)}, bf16[8,32,640]{2,1,0:T(8,128)(2,1)S(1)}, u32[]{:S(2)}, u32[]{:S(2)}) collective-permute-start(bf16[8,32,640]{2,1,0:T(8,128)(2,1)S(1)} %collective-permute-done.5), channel_id=1, source_target_pairs={{0,992},{32,0},{64,32},{96,64},{128,96},{160,128},{192,160},{224,1... | collective-permute-start | bytes 983048 | tf_op jit(solution)/shard_map/ppermute | solution.py:30
  60.9 9.0 %collective-permute-start.8 = (bf16[8,32,640]{2,1,0:T(8,128)(2,1)S(1)}, bf16[8,32,640]{2,1,0:T(8,128)(2,1)S(1)}, u32[]{:S(2)}, u32[]{:S(2)}) collective-permute-start(bf16[8,32,640]{2,1,0:T(8,128)(2,1)S(1)} %collective-permute-done.6), channel_id=1, source_target_pairs={{0,32},{32,64},{64,96},{96,128},{128,160},{160,192},{192,224},{224... | collective-permute-start | bytes 983048 | tf_op jit(solution)/shard_map/ppermute | solution.py:27
  64.0 9.0 %collective-permute-start.10 = (bf16[8,32,640]{2,1,0:T(8,128)(2,1)S(1)}, bf16[8,32,640]{2,1,0:T(8,128)(2,1)S(1)}, u32[]{:S(2)}, u32[]{:S(2)}) collective-permute-start(bf16[8,32,640]{2,1,0:T(8,128)(2,1)S(1)} %collective-permute-done.7), channel_id=1, source_target_pairs={{0,992},{32,0},{64,32},{96,64},{128,96},{160,128},{192,160},{224,1... | collective-permute-start | bytes 983048 | tf_op jit(solution)/shard_map/ppermute | solution.py:30
  70.0 9.0 %collective-permute-start.11 = (bf16[8,32,640]{2,1,0:T(8,128)(2,1)S(1)}, bf16[8,32,640]{2,1,0:T(8,128)(2,1)S(1)}, u32[]{:S(2)}, u32[]{:S(2)}) collective-permute-start(bf16[8,32,640]{2,1,0:T(8,128)(2,1)S(1)} %collective-permute-done.8), channel_id=1, source_target_pairs={{0,32},{32,64},{64,96},{96,128},{128,160},{160,192},{192,224},{224... | collective-permute-start | bytes 983048 | tf_op jit(solution)/shard_map/ppermute | solution.py:27
  73.1 9.0 %collective-permute-start.12 = (bf16[8,32,640]{2,1,0:T(8,128)(2,1)S(1)}, bf16[8,32,640]{2,1,0:T(8,128)(2,1)S(1)}, u32[]{:S(2)}, u32[]{:S(2)}) collective-permute-start(bf16[8,32,640]{2,1,0:T(8,128)(2,1)S(1)} %collective-permute-done.10), channel_id=1, source_target_pairs={{0,992},{32,0},{64,32},{96,64},{128,96},{160,128},{192,160},{224,1... | collective-permute-start | bytes 983048 | tf_op jit(solution)/shard_map/ppermute | solution.py:30
  79.0 17.5 %collective-permute-start.13 = (bf16[8,32,640]{2,1,0:T(8,128)(2,1)S(1)}, bf16[8,32,640]{2,1,0:T(8,128)(2,1)S(1)}, u32[]{:S(2)}, u32[]{:S(2)}) collective-permute-start(bf16[8,32,640]{2,1,0:T(8,128)(2,1)S(1)} %collective-permute-done.11), channel_id=1, source_target_pairs={{0,32},{32,64},{64,96},{96,128},{128,160},{160,192},{192,224},{224... | collective-permute-start | bytes 983048 | tf_op jit(solution)/shard_map/ppermute | solution.py:27
  82.1 17.7 %collective-permute-start.14 = (bf16[8,32,640]{2,1,0:T(8,128)(2,1)S(1)}, bf16[8,32,640]{2,1,0:T(8,128)(2,1)S(1)}, u32[]{:S(2)}, u32[]{:S(2)}) collective-permute-start(bf16[8,32,640]{2,1,0:T(8,128)(2,1)S(1)} %collective-permute-done.12), channel_id=1, source_target_pairs={{0,992},{32,0},{64,32},{96,64},{128,96},{160,128},{192,160},{224,1... | collective-permute-start | bytes 983048 | tf_op jit(solution)/shard_map/ppermute | solution.py:30
  87.1 23.8 %collective-permute-start.9 = (bf16[10,32,640]{2,1,0:T(8,128)(2,1)S(1)}, bf16[10,32,640]{2,1,0:T(8,128)(2,1)S(1)}, u32[]{:S(2)}, u32[]{:S(2)}) collective-permute-start(bf16[10,32,640]{2,1,0:T(8,128)(2,1)S(1)} %get-tuple-element.18), channel_id=1, source_target_pairs={{0,16},{16,0},{1,17},{17,1},{2,18},{18,2},{3,19},{19,3},{4,20},{20... | collective-permute-start | bytes 1228808 | tf_op jit(solution)/shard_map/ppermute | solution.py:40
  96.5 12.5 %collective-permute-start.15 = (bf16[8,32,640]{2,1,0:T(8,128)(2,1)S(1)}, bf16[8,32,640]{2,1,0:T(8,128)(2,1)}, u32[]{:S(2)}, u32[]{:S(2)}) collective-permute-start(bf16[8,32,640]{2,1,0:T(8,128)(2,1)S(1)} %collective-permute-done.13), channel_id=1, source_target_pairs={{0,32},{32,64},{64,96},{96,128},{128,160},{160,192},{192,224},{224... | collective-permute-start | bytes 983048 | tf_op jit(solution)/shard_map/ppermute | solution.py:27
  99.8 25.7 %collective-permute-start.16 = (bf16[8,32,640]{2,1,0:T(8,128)(2,1)S(1)}, bf16[8,32,640]{2,1,0:T(8,128)(2,1)}, u32[]{:S(2)}, u32[]{:S(2)}) collective-permute-start(bf16[8,32,640]{2,1,0:T(8,128)(2,1)S(1)} %collective-permute-done.14), channel_id=1, source_target_pairs={{0,992},{32,0},{64,32},{96,64},{128,96},{160,128},{192,160},{224,1... | collective-permute-start | bytes 983048 | tf_op jit(solution)/shard_map/ppermute | solution.py:30
  109.0 21.7 %collective-permute-start.17 = (bf16[8,32,640]{2,1,0:T(8,128)(2,1)}, bf16[8,32,640]{2,1,0:T(8,128)(2,1)}, u32[]{:S(2)}, u32[]{:S(2)}) collective-permute-start(bf16[8,32,640]{2,1,0:T(8,128)(2,1)} %collective-permute-done.15), channel_id=1, source_target_pairs={{0,32},{32,64},{64,96},{96,128},{128,160},{160,192},{192,224},{224... | collective-permute-start | bytes 983048 | tf_op jit(solution)/shard_map/ppermute | solution.py:27
  118.7 68.4 %all-to-all-start = ((bf16[16,2,2,10,1024]{4,1,3,2,0:T(2,128)(2,1)}), bf16[16,2,2,10,1024]{4,1,3,2,0:T(2,128)(2,1)S(1)}, u32[]{:S(2)}, u32[]{:S(2)}) async-start(bf16[16,2,2,10,1024]{4,1,3,2,0:T(2,128)(2,1)} %copy.6), calls=%async_computation | async-start | bytes 2621440 | tf_op jit(solution)/shard_map/all_to_all | solution.py:46
  125.5 10.5 %collective-permute-start.18 = (bf16[8,32,640]{2,1,0:T(8,128)(2,1)}, bf16[8,32,640]{2,1,0:T(8,128)(2,1)S(1)}, u32[]{:S(2)}, u32[]{:S(2)}) collective-permute-start(bf16[8,32,640]{2,1,0:T(8,128)(2,1)} %collective-permute-done.16), channel_id=1, source_target_pairs={{0,992},{32,0},{64,32},{96,64},{128,96},{160,128},{192,160},{224,1... | collective-permute-start | bytes 983048 | tf_op jit(solution)/shard_map/ppermute | solution.py:30
  130.7 12.0 %collective-permute-start.19 = (bf16[8,32,640]{2,1,0:T(8,128)(2,1)}, bf16[8,32,640]{2,1,0:T(8,128)(2,1)S(1)}, u32[]{:S(2)}, u32[]{:S(2)}) collective-permute-start(bf16[8,32,640]{2,1,0:T(8,128)(2,1)} %collective-permute-done.17), channel_id=1, source_target_pairs={{0,32},{32,64},{64,96},{96,128},{128,160},{160,192},{192,224},{224... | collective-permute-start | bytes 983048 | tf_op jit(solution)/shard_map/ppermute | solution.py:27
  136.0 10.8 %collective-permute-start.21 = (bf16[8,32,640]{2,1,0:T(8,128)(2,1)S(1)}, bf16[8,32,640]{2,1,0:T(8,128)(2,1)S(1)}, u32[]{:S(2)}, u32[]{:S(2)}) collective-permute-start(bf16[8,32,640]{2,1,0:T(8,128)(2,1)S(1)} %collective-permute-done.18), channel_id=1, source_target_pairs={{0,992},{32,0},{64,32},{96,64},{128,96},{160,128},{192,160},{224,1... | collective-permute-start | bytes 983048 | tf_op jit(solution)/shard_map/ppermute | solution.py:30
  142.7 14.6 %collective-permute-start.22 = (bf16[8,32,640]{2,1,0:T(8,128)(2,1)S(1)}, bf16[8,32,640]{2,1,0:T(8,128)(2,1)S(1)}, u32[]{:S(2)}, u32[]{:S(2)}) collective-permute-start(bf16[8,32,640]{2,1,0:T(8,128)(2,1)S(1)} %collective-permute-done.19), channel_id=1, source_target_pairs={{0,32},{32,64},{64,96},{96,128},{128,160},{160,192},{192,224},{224... | collective-permute-start | bytes 983048 | tf_op jit(solution)/shard_map/ppermute | solution.py:27
  146.8 13.1 %collective-permute-start.23 = (bf16[8,32,640]{2,1,0:T(8,128)(2,1)S(1)}, bf16[8,32,640]{2,1,0:T(8,128)(2,1)S(1)}, u32[]{:S(2)}, u32[]{:S(2)}) collective-permute-start(bf16[8,32,640]{2,1,0:T(8,128)(2,1)S(1)} %collective-permute-done.21), channel_id=1, source_target_pairs={{0,992},{32,0},{64,32},{96,64},{128,96},{160,128},{192,160},{224,1... | collective-permute-start | bytes 983048 | tf_op jit(solution)/shard_map/ppermute | solution.py:30
  152.0 19.7 %collective-permute-start.20 = (bf16[10,32,640]{2,1,0:T(8,128)(2,1)}, bf16[10,32,640]{2,1,0:T(8,128)(2,1)S(1)}, u32[]{:S(2)}, u32[]{:S(2)}) collective-permute-start(bf16[10,32,640]{2,1,0:T(8,128)(2,1)} %get-tuple-element.38), channel_id=1, source_target_pairs={{0,16},{16,0},{1,17},{17,1},{2,18},{18,2},{3,19},{19,3},{4,20},{20... | collective-permute-start | bytes 1228808 | tf_op jit(solution)/shard_map/ppermute | solution.py:40
  157.3 12.5 %collective-permute-start.24 = (bf16[8,32,640]{2,1,0:T(8,128)(2,1)S(1)}, bf16[8,32,640]{2,1,0:T(8,128)(2,1)}, u32[]{:S(2)}, u32[]{:S(2)}) collective-permute-start(bf16[8,32,640]{2,1,0:T(8,128)(2,1)S(1)} %collective-permute-done.22), channel_id=1, source_target_pairs={{0,32},{32,64},{64,96},{96,128},{128,160},{160,192},{192,224},{224... | collective-permute-start | bytes 983048 | tf_op jit(solution)/shard_map/ppermute | solution.py:27
  159.9 22.7 %collective-permute-start.25 = (bf16[8,32,640]{2,1,0:T(8,128)(2,1)S(1)}, bf16[8,32,640]{2,1,0:T(8,128)(2,1)}, u32[]{:S(2)}, u32[]{:S(2)}) collective-permute-start(bf16[8,32,640]{2,1,0:T(8,128)(2,1)S(1)} %collective-permute-done.23), channel_id=1, source_target_pairs={{0,992},{32,0},{64,32},{96,64},{128,96},{160,128},{192,160},{224,1... | collective-permute-start | bytes 983048 | tf_op jit(solution)/shard_map/ppermute | solution.py:30
  169.7 26.0 %collective-permute-start.26 = (bf16[8,32,640]{2,1,0:T(8,128)(2,1)}, bf16[8,32,640]{2,1,0:T(8,128)(2,1)S(1)}, u32[]{:S(2)}, u32[]{:S(2)}) collective-permute-start(bf16[8,32,640]{2,1,0:T(8,128)(2,1)} %collective-permute-done.24), channel_id=1, source_target_pairs={{0,32},{32,64},{64,96},{96,128},{128,160},{160,192},{192,224},{224... | collective-permute-start | bytes 983048 | tf_op jit(solution)/shard_map/ppermute | solution.py:27
  182.5 16.7 %collective-permute-start.27 = (bf16[8,32,640]{2,1,0:T(8,128)(2,1)}, bf16[8,32,640]{2,1,0:T(8,128)(2,1)}, u32[]{:S(2)}, u32[]{:S(2)}) collective-permute-start(bf16[8,32,640]{2,1,0:T(8,128)(2,1)} %collective-permute-done.25), channel_id=1, source_target_pairs={{0,992},{32,0},{64,32},{96,64},{128,96},{160,128},{192,160},{224,1... | collective-permute-start | bytes 983048 | tf_op jit(solution)/shard_map/ppermute | solution.py:30
  187.1 42.5 %all-to-all-start.1 = ((bf16[16,2,2,10,1024]{4,1,3,2,0:T(2,128)(2,1)}), bf16[16,2,2,10,1024]{4,1,3,2,0:T(2,128)(2,1)}, u32[]{:S(2)}, u32[]{:S(2)}) async-start(bf16[16,2,2,10,1024]{4,1,3,2,0:T(2,128)(2,1)} %copy.8), calls=%async_computation.1 | async-start | bytes 2621440 | tf_op jit(solution)/shard_map/all_to_all | solution.py:46
  195.8 10.8 %collective-permute-start.28 = (bf16[8,32,640]{2,1,0:T(8,128)(2,1)S(1)}, bf16[8,32,640]{2,1,0:T(8,128)(2,1)}, u32[]{:S(2)}, u32[]{:S(2)}) collective-permute-start(bf16[8,32,640]{2,1,0:T(8,128)(2,1)S(1)} %collective-permute-done.26), channel_id=1, source_target_pairs={{0,32},{32,64},{64,96},{96,128},{128,160},{160,192},{192,224},{224... | collective-permute-start | bytes 983048 | tf_op jit(solution)/shard_map/ppermute | solution.py:27
  199.2 15.2 %collective-permute-start.30 = (bf16[8,32,640]{2,1,0:T(8,128)(2,1)}, bf16[8,32,640]{2,1,0:T(8,128)(2,1)S(1)}, u32[]{:S(2)}, u32[]{:S(2)}) collective-permute-start(bf16[8,32,640]{2,1,0:T(8,128)(2,1)} %collective-permute-done.27), channel_id=1, source_target_pairs={{0,992},{32,0},{64,32},{96,64},{128,96},{160,128},{192,160},{224,1... | collective-permute-start | bytes 983048 | tf_op jit(solution)/shard_map/ppermute | solution.py:30
  208.0 11.2 %collective-permute-start.29 = (bf16[8,32,640]{2,1,0:T(8,128)(2,1)}, bf16[8,32,640]{2,1,0:T(8,128)(2,1)S(1)}, u32[]{:S(2)}, u32[]{:S(2)}) collective-permute-start(bf16[8,32,640]{2,1,0:T(8,128)(2,1)} %get-tuple-element.58), channel_id=1, source_target_pairs={{0,16},{16,0},{1,17},{17,1},{2,18},{18,2},{3,19},{19,3},{4,20},{20... | collective-permute-start | bytes 983048 | tf_op jit(solution)/shard_map/ppermute | solution.py:40
  212.5 15.2 %collective-permute-start.31 = (bf16[8,32,640]{2,1,0:T(8,128)(2,1)}, bf16[8,32,640]{2,1,0:T(8,128)(2,1)S(1)}, u32[]{:S(2)}, u32[]{:S(2)}) collective-permute-start(bf16[8,32,640]{2,1,0:T(8,128)(2,1)} %collective-permute-done.28), channel_id=1, source_target_pairs={{0,32},{32,64},{64,96},{96,128},{128,160},{160,192},{192,224},{224... | collective-permute-start | bytes 983048 | tf_op jit(solution)/shard_map/ppermute | solution.py:27
  214.4 22.0 %collective-permute-start.32 = (bf16[8,32,640]{2,1,0:T(8,128)(2,1)S(1)}, bf16[8,32,640]{2,1,0:T(8,128)(2,1)}, u32[]{:S(2)}, u32[]{:S(2)}) collective-permute-start(bf16[8,32,640]{2,1,0:T(8,128)(2,1)S(1)} %collective-permute-done.30), channel_id=1, source_target_pairs={{0,992},{32,0},{64,32},{96,64},{128,96},{160,128},{192,160},{224,1... | collective-permute-start | bytes 983048 | tf_op jit(solution)/shard_map/ppermute | solution.py:30
  227.7 11.9 %collective-permute-start.33 = (bf16[8,32,640]{2,1,0:T(8,128)(2,1)S(1)}, bf16[8,32,640]{2,1,0:T(8,128)(2,1)}, u32[]{:S(2)}, u32[]{:S(2)}) collective-permute-start(bf16[8,32,640]{2,1,0:T(8,128)(2,1)S(1)} %collective-permute-done.31), channel_id=1, source_target_pairs={{0,32},{32,64},{64,96},{96,128},{128,160},{160,192},{192,224},{224... | collective-permute-start | bytes 983048 | tf_op jit(solution)/shard_map/ppermute | solution.py:27
  229.7 22.9 %all-to-all-start.2 = ((bf16[16,2,2,8,1024]{4,1,3,2,0:T(2,128)(2,1)}), bf16[16,2,2,8,1024]{4,1,3,2,0:T(2,128)(2,1)}, u32[]{:S(2)}, u32[]{:S(2)}) async-start(bf16[16,2,2,8,1024]{4,1,3,2,0:T(2,128)(2,1)} %copy.10), calls=%async_computation.2 | async-start | bytes 2097152 | tf_op jit(solution)/shard_map/all_to_all | solution.py:46
  240.5 4.4 %collective-permute-start.34 = (bf16[4,32,640]{2,1,0:T(8,128)(2,1)S(1)}, bf16[4,32,640]{2,1,0:T(8,128)(2,1)S(1)}, u32[]{:S(2)}, u32[]{:S(2)}) collective-permute-start(bf16[4,32,640]{2,1,0:T(8,128)(2,1)S(1)} %pad_maximum_fusion.1), channel_id=1, source_target_pairs={{0,16},{16,0},{1,17},{17,1},{2,18},{18,2},{3,19},{19,3},{4,20},{20... | collective-permute-start | bytes 491528 | tf_op jit(solution)/shard_map/ppermute | solution.py:40
  247.6 9.6 %copy-start.2 = (s32[32]{0:T(128)S(1)}, s32[32]{0:T(128)}, u32[]{:S(2)}) copy-start(s32[32]{0:T(128)} %constant.229) | copy-start | bytes 388
  252.5 14.8 %all-to-all-start.3 = ((bf16[16,2,2,4,1024]{4,1,3,2,0:T(2,128)(2,1)}), bf16[16,2,2,4,1024]{4,1,3,2,0:T(2,128)(2,1)S(1)}, u32[]{:S(2)}, u32[]{:S(2)}) async-start(bf16[16,2,2,4,1024]{4,1,3,2,0:T(2,128)(2,1)} %copy.12), calls=%async_computation.3 | async-start | bytes 1048576 | tf_op jit(solution)/shard_map/all_to_all | solution.py:46
